TPU v7x, 256 devices: a whole 4x4x8 slice. The times are simulated.
256 devices in a mesh: tm: 16 (over y, z_hi, core), space: 16 (over x, z_lo).
Axes of the slice: x: 4, y: 4, z: 8 (z_hi: 2, z_lo: 4; z = z_hi * 4 + z_lo), core: 2. Of those that a mesh axis runs over, the one named last changes fastest.
Arguments:
- guess: float32 [16, 4, 64, 64, 128], P('tm', None, 'space'), may hold values from 0 to 1
- fibre: int32 [64, 64, 128], P('space'), may hold values from 0 to 2
- labels: int32 [64, 64, 128], P('space'), may hold values from 0 to 3
Outputs:
- end_state: float32 [16, 4, 64, 64, 128], P('tm', None, 'space')
All inputs are finite; a program needn't handle non-finite values.
Results may differ from a plain program's by a relative error of at most 0.0003.
Values sent between devices are 32-bit elements; how exact they have to be, the bound alone decides.
No kernel may reach another device: no remote copies, remote signals or barrier semaphores. Data moves between devices by JAX's collectives and lax.ppermute only.
A program may use at most 64 MiB of HBM per device.

v0:
```python
import jax
import jax.numpy as jnp
from jax import lax
from jax.sharding import PartitionSpec as P

ITERS = 3


radau_nodes = [0.05710419611451768, 0.2768430136381238, 0.5835904323689168, 0.8602401356562195, 1.0]
slice_len = 0.6


def padded_2(block, sides, width):
    for axis, dim in sides:
        count = lax.axis_size(axis)
        forward = [(i, i + 1) for i in range(count - 1)]
        backward = [(target, source) for source, target in forward]
        low = lax.ppermute(
            lax.slice_in_dim(block, block.shape[dim] - width, None, axis=dim), axis, forward
        )
        high = lax.ppermute(lax.slice_in_dim(block, 0, width, axis=dim), axis, backward)
        block = jnp.concatenate([low, block, high], axis=dim)
    return block


def passed_along(block, axis, distance):
    devices = range(lax.axis_size(axis))
    route = [(i - distance, i) for i in devices if i - distance in devices]
    return lax.ppermute(block, axis, route)


def radau_table():
    table = []
    for m in range(5):
        row_values = []
        for j in range(5):
            polynom = [1.0]
            for i in range(5):
                if i != j:
                    factor = radau_nodes[j] - radau_nodes[i]
                    shifted = [0.0] + [value / factor for value in polynom]
                    scaled = [-radau_nodes[i] * value / factor for value in polynom] + [0.0]
                    polynom = [shifted[p] + scaled[p] for p in range(len(polynom) + 1)]
            integral = 0.0
            for p in range(len(polynom)):
                integral = integral + polynom[p] * radau_nodes[m] ** (p + 1) / (p + 1)
            row_values.append(integral)
        table.append(row_values)
    return table


def lookup(labels, values):
    total = jnp.zeros(labels.shape, jnp.float32)
    for level in range(len(values)):
        total = total + jnp.where(labels == level, values[level], 0.0).astype(jnp.float32)
    return total


def edge_pad(field, axis):
    size = field.shape[axis]
    low = lax.slice_in_dim(field, 0, 1, axis=axis)
    high = lax.slice_in_dim(field, size - 1, size, axis=axis)
    return jnp.concatenate([low, field, high], axis=axis)


def second(padded, axis):
    size = padded.shape[axis]
    upper = lax.slice_in_dim(padded, 2, size, axis=axis)
    lower = lax.slice_in_dim(padded, 0, size - 2, axis=axis)
    middle = lax.slice_in_dim(padded, 1, size - 1, axis=axis)
    return upper + lower - 2.0 * middle


def close_ends(padded, volts):
    place = lax.axis_index("space")
    count = lax.axis_size("space")
    rows = padded.shape[1]
    low = jnp.where(place == 0, volts[:, :1], padded[:, :1])
    high = jnp.where(place == count - 1, volts[:, -1:], padded[:, rows - 1 :])
    return jnp.concatenate([low, padded[:, 1 : rows - 1], high], axis=1)


def rates(states, lap, fast_g, slow_g, slow_tau):
    volt = states[:, 0]
    act = states[:, 1]
    inact = states[:, 2]
    slow = states[:, 3]
    current = (
        fast_g * act * act * act * inact * (volt - 1.0)
        + slow_g * slow * (volt + 0.2)
        + 0.3 * (volt + 0.1)
    )
    dvolt = lap - current
    dact = (jax.nn.sigmoid(8.0 * (volt - 0.2)) - act) / 0.5
    dinact = (jax.nn.sigmoid(-8.0 * (volt - 0.3)) - inact) / (
        1.0 + 3.0 * jax.nn.sigmoid(6.0 * (volt - 0.3))
    )
    dslow = (jax.nn.sigmoid(5.0 * (volt - 0.5)) - slow) / slow_tau
    return jnp.stack([dvolt, dact, dinact, dslow], axis=1)


def quadrature(start, derivs, row):
    total = row[0] * derivs[0]
    for j in range(1, 5):
        total = total + row[j] * derivs[j]
    return start + slice_len * total


def shards(guess, fibre, labels):
    table = radau_table()
    fast_g = lookup(labels, [4.0, 3.0, 3.5, 1.0])
    slow_g = lookup(labels, [0.6, 0.9, 0.75, 0.3])
    slow_tau = 4.0 * lookup(labels, [1.0, 1.5, 1.2, 3.0])
    conduct = [0.2 + 0.6 * (fibre == d).astype(jnp.float32) for d in range(3)]
    first_slice = lax.axis_index("tm") == 0
    start0 = guess[0]
    start = start0
    nodes = jnp.stack([start0] * 5)
    for k in range(ITERS):
        volts = nodes[:, 0]
        padded = padded_2(volts, (("space", 1),), 1)
        padded = close_ends(padded, volts)
        lap = conduct[0] * second(padded, 1)
        lap = lap + conduct[1] * second(edge_pad(volts, 2), 2)
        lap = lap + conduct[2] * second(edge_pad(volts, 3), 3)
        derivs = rates(nodes, lap, fast_g, slow_g, slow_tau)
        nodes = jnp.stack([quadrature(start, derivs, table[m]) for m in range(5)])
        if k < ITERS - 1:
            arrived = passed_along(nodes[4], "tm", 1)
            start = jnp.where(first_slice, start0, arrived)
    return nodes[4][None]


def solution(mesh):
    placed = (P("tm", None, "space", None, None), P("space", None, None), P("space", None, None))
    return jax.shard_map(
        shards,
        mesh=mesh,
        in_specs=placed,
        out_specs=P("tm", None, "space", None, None),
        check_vma=False,
    )
```

profile of v0, /device:TPU:27, one launch (start us, length us, event | category | flops | bytes accessed | tf_op | source)
XLA Modules:
  0.0 77.6 jit_solution(6792343845805429690)
XLA Ops:
  0.0 0.8 %slice_bitcast_fusion.3 = (f32[64,128]{1,0:T(8,128)S(1)}, f32[64,128]{1,0:T(8,128)S(1)}) fusion(f32[1,4,4,64,128]{4,3,2,1,0:T(8,128)} %param.3), kind=kLoop, calls=%fused_computation.185 | loop fusion | bytes 131072 | tf_op jit(solution)/shard_map/slice | solution.py:78
  0.8 3.5 %collective-permute-start.1 = (f32[5,1,64,128]{3,2,1,0:T(8,128)S(1)}, f32[5,1,64,128]{3,2,1,0:T(8,128)S(1)}, u32[]{:S(2)}, u32[]{:S(2)}) collective-permute-start(f32[5,1,64,128]{3,2,1,0:T(8,128)S(1)} %stack.89), channel_id=1, source_target_pairs={{0,1},{1,2},{2,3},{3,4},{4,5},{5,6},{6,7},{7,8},{8,9},{9,10},{10,1... | collective-permute-start | bytes 491528 | tf_op jit(solution)/shard_map/ppermute | solution.py:18
  4.4 4.6 %collective-permute-start = (f32[5,1,64,128]{3,2,1,0:T(8,128)S(1)}, f32[5,1,64,128]{3,2,1,0:T(8,128)S(1)}, u32[]{:S(2)}, u32[]{:S(2)}) collective-permute-start(f32[5,1,64,128]{3,2,1,0:T(8,128)S(1)} %stack.90), channel_id=1, source_target_pairs={{1,0},{2,1},{3,2},{4,3},{5,4},{6,5},{7,6},{8,7},{9,8},{10,9},{11,1... | collective-permute-start | bytes 491528 | tf_op jit(solution)/shard_map/ppermute | solution.py:21
  9.0 0.9 %slice_bitcast_fusion.2 = f32[4,64,128]{2,1,0:T(8,128)S(1)} fusion(f32[1,4,4,64,128]{4,3,2,1,0:T(8,128)} %param.3), kind=kLoop, calls=%fused_computation.172 | loop fusion | bytes 262144 | tf_op jit(solution)/shard_map/stack | solution.py:118
  9.9 1.0 %select_add_fusion.1 = (f32[4,64,128]{2,1,0:T(8,128)S(1)}, pred[4,64,128]{2,1,0:T(8,128)(4,1)S(1)}, pred[4,64,128]{2,1,0:T(8,128)(4,1)S(1)}, pred[4,64,128]{2,1,0:T(8,128)(4,1)S(1)}, pred[4,64,128]{2,1,0:T(8,128)(4,1)S(1)}) fusion(s32[4,64,128]{2,1,0:T(8,128)} %param.5), kind=kLoop, calls=%fused_computation.169 | loop fusion | flops 360448 | bytes 393216 | tf_op jit(solution)/shard_map/add | solution.py:55
  10.9 1.5 %fusion.92 = (f32[4,64,128]{2,1,0:T(8,128)S(1)}, f32[4,64,128]{2,1,0:T(8,128)S(1)}, f32[4,64,128]{2,1,0:T(8,128)S(1)}, f32[4,64,128]{2,1,0:T(8,128)S(1)}, f32[4,...) fusion(f32[1,4,4,64,128]{4,3,2,1,0:T(8,128)} %param.3, ...), kind=kLoop, calls=%fused_computation.156 | loop fusion | flops 2359296 | bytes 2097152 | tf_op jit(solution)/shard_map/add | solution.py:89
  12.5 0.2 slice_reduce_fusion.1
  12.7 0.0 collective-permute-done.1
  12.8 2.5 %collective-permute-done = f32[5,1,64,128]{3,2,1,0:T(8,128)S(1)} collective-permute-done((f32[5,1,64,128]{3,2,1,0:T(8,128)S(1)}, f32[5,1,64,128]{3,2,1,0:T(8,128)S(1)}, u32[]{:S(2)}, u32[]{:S(2)}) %collective-permute-start) | collective-permute-done | bytes 163872 | tf_op jit(solution)/shard_map/ppermute | solution.py:21
  15.3 0.1 stack.88
  15.3 0.1 stack.94
  15.5 0.1 stack.95
  15.6 0.6 fusion.37
  16.2 0.1 div.119
  16.3 0.1 stack.102
  16.4 0.1 stack.101
  16.4 0.0 copy-start
  16.5 0.3 pad_maximum_fusion
  16.7 0.7 copy-done
  17.5 0.3 add_dynamic-update-slice_fusion.4
  17.8 0.3 add_dynamic-update-slice_fusion.3
  18.2 0.3 add_dynamic-update-slice_fusion.2
  18.5 0.3 add_dynamic-update-slice_fusion.1
  18.9 0.3 add_dynamic-update-slice_fusion
  19.2 0.2 slice_bitcast_fusion.1
  19.5 0.2 fusion.102
  19.7 0.6 fusion.65
  20.3 0.1 bitcast_add_fusion.11
  20.4 9.0 %collective-permute-start.2 = (f32[4,4,64,128]{3,2,1,0:T(8,128)S(1)}, f32[4,4,64,128]{3,2,1,0:T(8,128)S(1)}, u32[]{:S(2)}, u32[]{:S(2)}) collective-permute-start(f32[4,4,64,128]{3,2,1,0:T(8,128)S(1)} %bitcast_add_fusion.11), channel_id=1, source_target_pairs={{0,16},{16,32},{32,48},{48,64},{64,80},{80,96},{96,112},{112,128},... | collective-permute-start | bytes 1572872 | tf_op jit(solution)/shard_map/ppermute | solution.py:29
  29.4 4.5 %collective-permute-start.3 = (f32[5,1,64,128]{3,2,1,0:T(8,128)S(1)}, f32[5,1,64,128]{3,2,1,0:T(8,128)S(1)}, u32[]{:S(2)}, u32[]{:S(2)}) collective-permute-start(f32[5,1,64,128]{3,2,1,0:T(8,128)S(1)} %get-tuple-element.36), channel_id=1, source_target_pairs={{1,0},{2,1},{3,2},{4,3},{5,4},{6,5},{7,6},{8,7},{9,8},{10,9},{11,1... | collective-permute-start | bytes 491528 | tf_op jit(solution)/shard_map/ppermute | solution.py:21
  33.9 1.9 %collective-permute-start.4 = (f32[5,1,64,128]{3,2,1,0:T(8,128)S(1)}, f32[5,1,64,128]{3,2,1,0:T(8,128)S(1)}, u32[]{:S(2)}, u32[]{:S(2)}) collective-permute-start(f32[5,1,64,128]{3,2,1,0:T(8,128)S(1)} %get-tuple-element.37), channel_id=1, source_target_pairs={{0,1},{1,2},{2,3},{3,4},{4,5},{5,6},{6,7},{7,8},{8,9},{9,10},{10,1... | collective-permute-start | bytes 491528 | tf_op jit(solution)/shard_map/ppermute | solution.py:18
  35.9 11.3 %collective-permute-done.3 = f32[5,1,64,128]{3,2,1,0:T(8,128)S(1)} collective-permute-done((f32[5,1,64,128]{3,2,1,0:T(8,128)S(1)}, f32[5,1,64,128]{3,2,1,0:T(8,128)S(1)}, u32[]{:S(2)}, u32[]{:S(2)}) %collective-permute-start.3) | collective-permute-done | bytes 163872 | tf_op jit(solution)/shard_map/ppermute | solution.py:21
  47.2 0.0 collective-permute-done.4
  47.2 0.9 %fusion.5 = f32[5,1,4,64,128]{4,3,2,1,0:T(8,128)S(1)} fusion(f32[5,4,64,128]{3,2,1,0:T(8,128)S(1)} %get-tuple-element.22, f32[5,4,64,1]{3,2,1,0:T(8,128)S(1)} %get-tuple-element.41, f32[5,4,64,1]{3,2,1,0:T(8,128)S(1)} %get-tuple-element.40, f32[5,4,1,128]{3,2,1,0:T(1,128)S(1)} %get-tuple-element.39, f32[5,4,1,128]{3,2,1,0:T(1,128)S(1)} %get-tuple-element.38, ...), kind=kLoop, calls=%fused_computation.10 | loop fusion | flops 5242880 | bytes 4290560 | tf_op jit(solution)/shard_map/stack | solution.py:99
  48.1 0.2 pad_maximum_fusion.1
  48.2 0.0 collective-permute-done.2
  48.3 0.4 bitcast_dynamic-update-slice_fusion.4
  48.7 0.3 bitcast_dynamic-update-slice_fusion.3
  49.0 0.3 bitcast_dynamic-update-slice_fusion.2
  49.4 0.3 bitcast_dynamic-update-slice_fusion.1
  49.7 0.3 bitcast_dynamic-update-slice_fusion
  50.1 0.2 slice_bitcast_fusion
  50.3 0.2 fusion.99
  50.6 0.6 fusion.48
  51.2 1.9 %collective-permute-start.5 = (f32[4,4,64,128]{3,2,1,0:T(8,128)S(1)}, f32[4,4,64,128]{3,2,1,0:T(8,128)S(1)}, u32[]{:S(2)}, u32[]{:S(2)}) collective-permute-start(f32[4,4,64,128]{3,2,1,0:T(8,128)S(1)} %get-tuple-element.8), channel_id=1, source_target_pairs={{0,16},{16,32},{32,48},{48,64},{64,80},{80,96},{96,112},{112,128},... | collective-permute-start | bytes 1572872 | tf_op jit(solution)/shard_map/ppermute | solution.py:29
  53.1 1.9 %collective-permute-start.6 = (f32[5,1,64,128]{3,2,1,0:T(8,128)S(1)}, f32[5,1,64,128]{3,2,1,0:T(8,128)S(1)}, u32[]{:S(2)}, u32[]{:S(2)}) collective-permute-start(f32[5,1,64,128]{3,2,1,0:T(8,128)S(1)} %get-tuple-element.28), channel_id=1, source_target_pairs={{1,0},{2,1},{3,2},{4,3},{5,4},{6,5},{7,6},{8,7},{9,8},{10,9},{11,1... | collective-permute-start | bytes 491528 | tf_op jit(solution)/shard_map/ppermute | solution.py:21
  55.1 5.0 %collective-permute-start.7 = (f32[5,1,64,128]{3,2,1,0:T(8,128)S(1)}, f32[5,1,64,128]{3,2,1,0:T(8,128)S(1)}, u32[]{:S(2)}, u32[]{:S(2)}) collective-permute-start(f32[5,1,64,128]{3,2,1,0:T(8,128)S(1)} %get-tuple-element.29), channel_id=1, source_target_pairs={{0,1},{1,2},{2,3},{3,4},{4,5},{5,6},{6,7},{7,8},{8,9},{9,10},{10,1... | collective-permute-start | bytes 491528 | tf_op jit(solution)/shard_map/ppermute | solution.py:18
  60.1 15.2 %collective-permute-done.6 = f32[5,1,64,128]{3,2,1,0:T(8,128)S(1)} collective-permute-done((f32[5,1,64,128]{3,2,1,0:T(8,128)S(1)}, f32[5,1,64,128]{3,2,1,0:T(8,128)S(1)}, u32[]{:S(2)}, u32[]{:S(2)}) %collective-permute-start.6) | collective-permute-done | bytes 163872 | tf_op jit(solution)/shard_map/ppermute | solution.py:21
  75.3 0.0 collective-permute-done.7
  75.3 0.9 %fusion.11 = f32[5,1,4,64,128]{4,3,2,1,0:T(8,128)S(1)} fusion(f32[5,4,64,128]{3,2,1,0:T(8,128)S(1)} %get-tuple-element.18, f32[5,4,64,1]{3,2,1,0:T(8,128)S(1)} %get-tuple-element.33, f32[5,4,64,1]{3,2,1,0:T(8,128)S(1)} %get-tuple-element.32, f32[5,4,1,128]{3,2,1,0:T(1,128)S(1)} %get-tuple-element.31, f32[5,4,1,128]{3,2,1,0:T(1,128)S(1)} %get-tuple-element.30, ...), kind=kLoop, calls=%fused_computation.16 | loop fusion | flops 5242880 | bytes 4290560 | tf_op jit(solution)/shard_map/stack | solution.py:99
  76.2 0.2 pad_maximum_fusion.2
  76.4 0.0 collective-permute-done.5
  76.4 1.2 %fusion.85 = f32[1,4,4,64,128]{4,3,2,1,0:T(8,128)} fusion(f32[5,4,4,64,128]{4,3,2,1,0:T(8,128)S(1)} %pad_maximum_fusion.2, f32[4,4,64,128]{3,2,1,0:T(8,128)S(1)} %collective-permute-done.5, f32[1,4,4,64,128]{4,3,2,1,0:T(8,128)S(1)} %copy-done, pred[]{:T(512)S(6)} %eq.20), kind=kLoop, calls=%fused_computation.125 | loop fusion | flops 1572864 | bytes 4194305 | tf_op jit(solution)/shard_map/stack | solution.py:127
  (13 shorter events, 0.2 us)
Async XLA Ops:
  0.8 11.9 %collective-permute-start.1 = (f32[5,1,64,128]{3,2,1,0:T(8,128)S(1)}, f32[5,1,64,128]{3,2,1,0:T(8,128)S(1)}, u32[]{:S(2)}, u32[]{:S(2)}) collective-permute-start(f32[5,1,64,128]{3,2,1,0:T(8,128)S(1)} %stack.89), channel_id=1, source_target_pairs={{0,1},{1,2},{2,3},{3,4},{4,5},{5,6},{6,7},{7,8},{8,9},{9,10},{10,1... | collective-permute-start | bytes 491528 | tf_op jit(solution)/shard_map/ppermute | solution.py:18
  4.4 10.8 %collective-permute-start = (f32[5,1,64,128]{3,2,1,0:T(8,128)S(1)}, f32[5,1,64,128]{3,2,1,0:T(8,128)S(1)}, u32[]{:S(2)}, u32[]{:S(2)}) collective-permute-start(f32[5,1,64,128]{3,2,1,0:T(8,128)S(1)} %stack.90), channel_id=1, source_target_pairs={{1,0},{2,1},{3,2},{4,3},{5,4},{6,5},{7,6},{8,7},{9,8},{10,9},{11,1... | collective-permute-start | bytes 491528 | tf_op jit(solution)/shard_map/ppermute | solution.py:21
  16.4 1.0 %copy-start = (f32[1,4,4,64,128]{4,3,2,1,0:T(8,128)S(1)}, f32[1,4,4,64,128]{4,3,2,1,0:T(8,128)}, u32[]{:S(2)}) copy-start(f32[1,4,4,64,128]{4,3,2,1,0:T(8,128)} %param.3) | copy-start | bytes 1572868
  20.4 27.8 %collective-permute-start.2 = (f32[4,4,64,128]{3,2,1,0:T(8,128)S(1)}, f32[4,4,64,128]{3,2,1,0:T(8,128)S(1)}, u32[]{:S(2)}, u32[]{:S(2)}) collective-permute-start(f32[4,4,64,128]{3,2,1,0:T(8,128)S(1)} %bitcast_add_fusion.11), channel_id=1, source_target_pairs={{0,16},{16,32},{32,48},{48,64},{64,80},{80,96},{96,112},{112,128},... | collective-permute-start | bytes 1572872 | tf_op jit(solution)/shard_map/ppermute | solution.py:29
  29.4 17.8 %collective-permute-start.3 = (f32[5,1,64,128]{3,2,1,0:T(8,128)S(1)}, f32[5,1,64,128]{3,2,1,0:T(8,128)S(1)}, u32[]{:S(2)}, u32[]{:S(2)}) collective-permute-start(f32[5,1,64,128]{3,2,1,0:T(8,128)S(1)} %get-tuple-element.36), channel_id=1, source_target_pairs={{1,0},{2,1},{3,2},{4,3},{5,4},{6,5},{7,6},{8,7},{9,8},{10,9},{11,1... | collective-permute-start | bytes 491528 | tf_op jit(solution)/shard_map/ppermute | solution.py:21
  33.9 13.2 %collective-permute-start.4 = (f32[5,1,64,128]{3,2,1,0:T(8,128)S(1)}, f32[5,1,64,128]{3,2,1,0:T(8,128)S(1)}, u32[]{:S(2)}, u32[]{:S(2)}) collective-permute-start(f32[5,1,64,128]{3,2,1,0:T(8,128)S(1)} %get-tuple-element.37), channel_id=1, source_target_pairs={{0,1},{1,2},{2,3},{3,4},{4,5},{5,6},{6,7},{7,8},{8,9},{9,10},{10,1... | collective-permute-start | bytes 491528 | tf_op jit(solution)/shard_map/ppermute | solution.py:18
  51.2 25.2 %collective-permute-start.5 = (f32[4,4,64,128]{3,2,1,0:T(8,128)S(1)}, f32[4,4,64,128]{3,2,1,0:T(8,128)S(1)}, u32[]{:S(2)}, u32[]{:S(2)}) collective-permute-start(f32[4,4,64,128]{3,2,1,0:T(8,128)S(1)} %get-tuple-element.8), channel_id=1, source_target_pairs={{0,16},{16,32},{32,48},{48,64},{64,80},{80,96},{96,112},{112,128},... | collective-permute-start | bytes 1572872 | tf_op jit(solution)/shard_map/ppermute | solution.py:29
  53.1 22.2 %collective-permute-start.6 = (f32[5,1,64,128]{3,2,1,0:T(8,128)S(1)}, f32[5,1,64,128]{3,2,1,0:T(8,128)S(1)}, u32[]{:S(2)}, u32[]{:S(2)}) collective-permute-start(f32[5,1,64,128]{3,2,1,0:T(8,128)S(1)} %get-tuple-element.28), channel_id=1, source_target_pairs={{1,0},{2,1},{3,2},{4,3},{5,4},{6,5},{7,6},{8,7},{9,8},{10,9},{11,1... | collective-permute-start | bytes 491528 | tf_op jit(solution)/shard_map/ppermute | solution.py:21
  55.1 20.2 %collective-permute-start.7 = (f32[5,1,64,128]{3,2,1,0:T(8,128)S(1)}, f32[5,1,64,128]{3,2,1,0:T(8,128)S(1)}, u32[]{:S(2)}, u32[]{:S(2)}) collective-permute-start(f32[5,1,64,128]{3,2,1,0:T(8,128)S(1)} %get-tuple-element.29), channel_id=1, source_target_pairs={{0,1},{1,2},{2,3},{3,4},{4,5},{5,6},{6,7},{7,8},{8,9},{9,10},{10,1... | collective-permute-start | bytes 491528 | tf_op jit(solution)/shard_map/ppermute | solution.py:18
where the time goes:
time: 78 us; the launch traced here: 77.6 us
  starting transfers between devices  32.4 us (42%)
  waiting for transfers between devices  29 us (37%)
  other arithmetic  12.1 us (16%)
  local copies, waits for them, and re-layouts  3.8 us (5%)
    ppermute x3, waiting for transfers between devices, padded_2(): lax.ppermute(lax.slice_in_dim(block, 0, width, axis=dim), axis, backward)  28.9 us
    ppermute x3, starting transfers between devices, padded_2(): lax.ppermute(lax.slice_in_dim(block, 0, width, axis=dim), axis, backward)  11 us
    ppermute x2, starting transfers between devices, passed_along(): return lax.ppermute(block, axis, route)  10.9 us
    ppermute x3, starting transfers between devices, padded_2(): lax.ppermute(lax.slice_in_dim(block, block.shape[dim] - width, None, axis...  10.5 us
    another operation x6, other arithmetic, rates(): return jnp.stack([dvolt, dact, dinact, dslow], axis=1)  2.99 us
    unnamed x8, other arithmetic  2.81 us
    another operation x3, other arithmetic, shards(): nodes = jnp.stack([quadrature(start, derivs, table[m]) for m in range(5)])  1.88 us
  transfers between devices with their start and end apart: 8, of which 3 were waited for; matrix products, arithmetic and copies ran while one was open for 8% of the time, Pallas kernels for 0%

commit v1 on v0

v1 whole, which is shorter than its diff:
```python
import jax
import jax.numpy as jnp
from jax import lax
from jax.sharding import PartitionSpec as P

ITERS = 3


radau_nodes = [0.05710419611451768, 0.2768430136381238, 0.5835904323689168, 0.8602401356562195, 1.0]
slice_len = 0.6


def radau_table():
    table = []
    for m in range(5):
        row_values = []
        for j in range(5):
            polynom = [1.0]
            for i in range(5):
                if i != j:
                    factor = radau_nodes[j] - radau_nodes[i]
                    shifted = [0.0] + [value / factor for value in polynom]
                    scaled = [-radau_nodes[i] * value / factor for value in polynom] + [0.0]
                    polynom = [shifted[p] + scaled[p] for p in range(len(polynom) + 1)]
            integral = 0.0
            for p in range(len(polynom)):
                integral = integral + polynom[p] * radau_nodes[m] ** (p + 1) / (p + 1)
            row_values.append(integral)
        table.append(row_values)
    return table


def lookup(labels, values):
    total = jnp.zeros(labels.shape, jnp.float32)
    for level in range(len(values)):
        total = total + jnp.where(labels == level, values[level], 0.0).astype(jnp.float32)
    return total


def edge_pad(field, axis):
    size = field.shape[axis]
    low = lax.slice_in_dim(field, 0, 1, axis=axis)
    high = lax.slice_in_dim(field, size - 1, size, axis=axis)
    return jnp.concatenate([low, field, high], axis=axis)


def second(padded, axis):
    size = padded.shape[axis]
    upper = lax.slice_in_dim(padded, 2, size, axis=axis)
    lower = lax.slice_in_dim(padded, 0, size - 2, axis=axis)
    middle = lax.slice_in_dim(padded, 1, size - 1, axis=axis)
    return upper + lower - 2.0 * middle


def shift_space(block, forward):
    count = lax.axis_size("space")
    pairs = [(i, i + 1) for i in range(count - 1)]
    if not forward:
        pairs = [(t, s) for s, t in pairs]
    return lax.ppermute(block, "space", pairs)


def halos(volts):
    planes = volts.shape[-3]
    low = shift_space(volts[..., planes - 1 : planes, :, :], True)
    high = shift_space(volts[..., 0:1, :, :], False)
    return low, high


def laplacian(volts, low, high, conduct):
    padded = jnp.concatenate([low, volts, high], axis=-3)
    lap = conduct[0] * second(padded, volts.ndim - 3)
    lap = lap + conduct[1] * second(edge_pad(volts, volts.ndim - 2), volts.ndim - 2)
    lap = lap + conduct[2] * second(edge_pad(volts, volts.ndim - 1), volts.ndim - 1)
    return lap


def rates(states, lap, fast_g, slow_g, slow_tau):
    volt = states[..., 0, :, :, :]
    act = states[..., 1, :, :, :]
    inact = states[..., 2, :, :, :]
    slow = states[..., 3, :, :, :]
    current = (
        fast_g * act * act * act * inact * (volt - 1.0)
        + slow_g * slow * (volt + 0.2)
        + 0.3 * (volt + 0.1)
    )
    dvolt = lap - current
    dact = (jax.nn.sigmoid(8.0 * (volt - 0.2)) - act) / 0.5
    dinact = (jax.nn.sigmoid(-8.0 * (volt - 0.3)) - inact) / (
        1.0 + 3.0 * jax.nn.sigmoid(6.0 * (volt - 0.3))
    )
    dslow = (jax.nn.sigmoid(5.0 * (volt - 0.5)) - slow) / slow_tau
    return jnp.stack([dvolt, dact, dinact, dslow], axis=-4)


def quadrature(start, derivs, row):
    total = row[0] * derivs[0]
    for j in range(1, 5):
        total = total + row[j] * derivs[j]
    return start + slice_len * total


def shards(guess, fibre, labels):
    table = radau_table()
    sums = [sum(row) for row in table]
    fast_g = lookup(labels, [4.0, 3.0, 3.5, 1.0])
    slow_g = lookup(labels, [0.6, 0.9, 0.75, 0.3])
    slow_tau = 4.0 * lookup(labels, [1.0, 1.5, 1.2, 3.0])
    conduct = [0.2 + 0.6 * (fibre == d).astype(jnp.float32) for d in range(3)]
    place = lax.axis_index("space")
    at_low = place == 0
    at_high = place == lax.axis_size("space") - 1
    first_slice = lax.axis_index("tm") == 0
    count = lax.axis_size("tm")
    tm_pairs = [(i, i + 1) for i in range(count - 1)]

    start0 = guess[0]
    volts0 = start0[0]
    planes = volts0.shape[0]

    low0, high0 = halos(volts0)
    low0 = jnp.where(at_low, volts0[:1], low0)
    high0 = jnp.where(at_high, volts0[planes - 1 :], high0)
    derivs0 = rates(start0, laplacian(volts0, low0, high0, conduct), fast_g, slow_g, slow_tau)
    ends0 = start0 + slice_len * (sums[4] * derivs0)
    arrived1 = lax.ppermute(ends0, "tm", tm_pairs)

    dv = derivs0[0]
    dlow, dhigh = halos(dv)
    nodes0 = jnp.stack([start0 + slice_len * (sums[m] * derivs0) for m in range(5)])
    volts1 = nodes0[:, 0]
    low1 = jnp.stack([low0 + slice_len * (sums[m] * dlow) for m in range(5)])
    high1 = jnp.stack([high0 + slice_len * (sums[m] * dhigh) for m in range(5)])
    low1 = jnp.where(at_low, volts1[:, :1], low1)
    high1 = jnp.where(at_high, volts1[:, planes - 1 :], high1)
    derivs1 = rates(nodes0, laplacian(volts1, low1, high1, conduct), fast_g, slow_g, slow_tau)
    start1 = jnp.where(first_slice, start0, arrived1)
    ends1 = quadrature(start1, derivs1, table[4])
    arrived2 = lax.ppermute(ends1, "tm", tm_pairs)
    nodes1 = jnp.stack([quadrature(start1, derivs1, table[m]) for m in range(4)] + [ends1])

    volts2 = nodes1[:, 0]
    low2, high2 = halos(volts2)
    low2 = jnp.where(at_low, volts2[:, :1], low2)
    high2 = jnp.where(at_high, volts2[:, planes - 1 :], high2)
    derivs2 = rates(nodes1, laplacian(volts2, low2, high2, conduct), fast_g, slow_g, slow_tau)
    start2 = jnp.where(first_slice, start0, arrived2)
    ends2 = quadrature(start2, derivs2, table[4])
    return ends2[None]


def solution(mesh):
    placed = (P("tm", None, "space", None, None), P("space", None, None), P("space", None, None))
    return jax.shard_map(
        shards,
        mesh=mesh,
        in_specs=placed,
        out_specs=P("tm", None, "space", None, None),
        check_vma=False,
    )
```

time: 78 us -> 72.3 us (0.927)
  waiting for transfers between devices: 29 us -> 19.6 us
  starting transfers between devices: 32.4 us -> 39.6 us
  local copies, waits for them, and re-layouts: 3.8 us -> 1.51 us
  other arithmetic: 12.1 us -> 10.9 us
    ppermute x8, waiting for transfers between devices: 29 us -> 19.6 us  [the longest x6 16.2 us: shift_space(): return lax.ppermute(block, 'space', pairs)]
    ppermute x8, starting transfers between devices: 32.4 us -> 39.6 us  [the longest x6 23.2 us: shift_space(): return lax.ppermute(block, 'space', pairs)]
    another operation x9 -> x8, other arithmetic: 4.87 us -> 2.52 us  [the longest x4 2.09 us: rates(): return jnp.stack([dvolt, dact, dinact, dslow], axis=-4)]
    another operation x10 -> x0, local copies, waits for them, and re-layouts: 1.4 us -> none  [shards(): nodes = jnp.stack([start0] * 5)]
    broadcast_in_dim x0 -> x1, other arithmetic: none -> 1.2 us  [shards(): return ends2[None]]
    unnamed x8 -> x15, other arithmetic: 2.81 us -> 1.78 us
  transfers between devices with their start and end apart: 8 -> 8, of which waited for: 3 -> 3; matrix products, arithmetic and copies ran while one was open for 8% -> 10% of each run, Pallas kernels for 0% -> 0%
where the time goes in v1:
time: 72.3 us; the launch traced here: 71.9 us
  starting transfers between devices  39.6 us (55%)
  waiting for transfers between devices  19.6 us (27%)
  other arithmetic  10.9 us (15%)
  local copies, waits for them, and re-layouts  1.51 us (2%)
    ppermute x6, starting transfers between devices, shift_space(): return lax.ppermute(block, 'space', pairs)  23.2 us
    ppermute x6, waiting for transfers between devices, shift_space(): return lax.ppermute(block, 'space', pairs)  16.2 us
    ppermute x1, starting transfers between devices, shards(): arrived2 = lax.ppermute(ends1, 'tm', tm_pairs)  8.4 us
    ppermute x1, starting transfers between devices, shards(): arrived1 = lax.ppermute(ends0, 'tm', tm_pairs)  7.93 us
    ppermute x1, waiting for transfers between devices, shards(): arrived1 = lax.ppermute(ends0, 'tm', tm_pairs)  3.36 us
    another operation x4, other arithmetic, rates(): return jnp.stack([dvolt, dact, dinact, dslow], axis=-4)  2.09 us
    div x2, other arithmetic, rates(): dact = (jax.nn.sigmoid(8.0 * (volt - 0.2)) - act) / 0.5  1.78 us
    unnamed x15, other arithmetic  1.78 us
  transfers between devices with their start and end apart: 8, of which 3 were waited for; matrix products, arithmetic and copies ran while one was open for 10% of the time, Pallas kernels for 0%

profile of v1, /device:TPU:27, one launch (start us, length us, event | category | flops | bytes accessed | tf_op | source)
XLA Modules:
  0.0 71.9 jit_solution(17840074493558761834)
XLA Ops:
  0.0 0.0 copy-start
  0.0 0.0 copy-start.1
  0.0 0.8 %slice_bitcast_fusion.3 = (f32[1,64,128]{2,1,0:T(8,128)S(1)}, f32[1,64,128]{2,1,0:T(8,128)S(1)}) fusion(f32[1,4,4,64,128]{4,3,2,1,0:T(8,128)} %param.3), kind=kLoop, calls=%fused_computation.175 | loop fusion | bytes 131072 | tf_op jit(solution)/shard_map/slice | solution.py:123
  0.9 6.2 %collective-permute-start = (f32[1,64,128]{2,1,0:T(8,128)S(1)}, f32[1,64,128]{2,1,0:T(8,128)S(1)}, u32[]{:S(2)}, u32[]{:S(2)}) collective-permute-start(f32[1,64,128]{2,1,0:T(8,128)S(1)} %get-tuple-element.41), channel_id=1, source_target_pairs={{1,0},{2,1},{3,2},{4,3},{5,4},{6,5},{7,6},{8,7},{9,8},{10,9},{11,1... | collective-permute-start | bytes 98312 | tf_op jit(solution)/shard_map/ppermute | solution.py:60
  7.1 1.9 %collective-permute-start.1 = (f32[1,64,128]{2,1,0:T(8,128)S(1)}, f32[1,64,128]{2,1,0:T(8,128)S(1)}, u32[]{:S(2)}, u32[]{:S(2)}) collective-permute-start(f32[1,64,128]{2,1,0:T(8,128)S(1)} %get-tuple-element.42), channel_id=1, source_target_pairs={{0,1},{1,2},{2,3},{3,4},{4,5},{5,6},{6,7},{7,8},{8,9},{9,10},{10,1... | collective-permute-start | bytes 98312 | tf_op jit(solution)/shard_map/ppermute | solution.py:60
  9.0 1.2 %fusion.85 = (f32[1,4,64,128]{3,2,1,0:T(8,128)S(1)}, f32[1,1,4,64,128]{4,3,2,0,1:T(8,128)S(1)}, f32[1,1,4,64,128]{4,3,2,1,0:T(8,128)S(1)}, f32[4,64,128]{2,1,0:T(8,128)S(1)}) fusion(f32[1,4,4,64,128]{4,3,2,1,0:T(8,128)} %param.3), kind=kLoop, calls=%fused_computation.180 | loop fusion | flops 655360 | bytes 917504 | tf_op jit(solution)/shard_map/div | solution.py:89
  10.2 1.0 %select_add_fusion.1 = (f32[4,64,128]{2,1,0:T(8,128)S(1)}, pred[4,64,128]{2,1,0:T(8,128)(4,1)S(1)}, pred[4,64,128]{2,1,0:T(8,128)(4,1)S(1)}, pred[4,64,128]{2,1,0:T(8,128)(4,1)S(1)}, pred[4,64,128]{2,1,0:T(8,128)(4,1)S(1)}) fusion(s32[4,64,128]{2,1,0:T(8,128)} %param.5), kind=kLoop, calls=%fused_computation.154 | loop fusion | flops 360448 | bytes 393216 | tf_op jit(solution)/shard_map/add | solution.py:36
  11.2 1.0 %select_add_fusion.4 = (f32[4,64,128]{2,1,0:T(8,128)S(1)}, f32[4,64,128]{2,1,0:T(8,128)S(1)}, f32[4,64,128]{2,1,0:T(8,128)S(1)}) fusion(s32[4,64,128]{2,1,0:T(8,128)} %param.4), kind=kLoop, calls=%fused_computation.157 | loop fusion | flops 294912 | bytes 524288 | tf_op jit(solution)/shard_map/add | solution.py:110
  12.2 0.1 fusion.93
  12.2 0.0 copy-done
  12.3 0.2 select_add_fusion
  12.4 0.0 collective-permute-done
  12.5 2.0 %collective-permute-done.1 = f32[1,64,128]{2,1,0:T(8,128)S(1)} collective-permute-done((f32[1,64,128]{2,1,0:T(8,128)S(1)}, f32[1,64,128]{2,1,0:T(8,128)S(1)}, u32[]{:S(2)}, u32[]{:S(2)}) %collective-permute-start.1) | collective-permute-done | bytes 32800 | tf_op jit(solution)/shard_map/ppermute | solution.py:60
  14.4 0.0 copy-done.1
  14.5 0.3 fusion.71
  14.8 4.1 %collective-permute-start.3 = (f32[1,64,128]{2,1,0:T(8,128)S(1)}, f32[1,64,128]{2,1,0:T(8,128)S(1)}, u32[]{:S(2)}, u32[]{:S(2)}) collective-permute-start(f32[1,64,128]{2,1,0:T(8,128)S(1)} %get-tuple-element.49), channel_id=1, source_target_pairs={{1,0},{2,1},{3,2},{4,3},{5,4},{6,5},{7,6},{8,7},{9,8},{10,9},{11,1... | collective-permute-start | bytes 98312 | tf_op jit(solution)/shard_map/ppermute | solution.py:60
  18.9 1.9 %collective-permute-start.4 = (f32[1,64,128]{2,1,0:T(8,128)S(1)}, f32[1,64,128]{2,1,0:T(8,128)S(1)}, u32[]{:S(2)}, u32[]{:S(2)}) collective-permute-start(f32[1,64,128]{2,1,0:T(8,128)S(1)} %get-tuple-element.50), channel_id=1, source_target_pairs={{0,1},{1,2},{2,3},{3,4},{4,5},{5,6},{6,7},{7,8},{8,9},{9,10},{10,1... | collective-permute-start | bytes 98312 | tf_op jit(solution)/shard_map/ppermute | solution.py:60
  20.8 0.1 fusion.60
  20.9 7.9 %collective-permute-start.2 = (f32[4,4,64,128]{3,2,1,0:T(8,128)S(1)}, f32[4,4,64,128]{3,2,1,0:T(8,128)S(1)}, u32[]{:S(2)}, u32[]{:S(2)}) collective-permute-start(f32[4,4,64,128]{3,2,1,0:T(8,128)S(1)} %fusion.60), channel_id=1, source_target_pairs={{0,16},{16,32},{32,48},{48,64},{64,80},{80,96},{96,112},{112,128},... | collective-permute-start | bytes 1572872 | tf_op jit(solution)/shard_map/ppermute | solution.py:127
  28.8 0.1 fusion.63
  28.9 0.1 fusion.64
  29.0 0.1 fusion.65
  29.1 0.1 fusion.66
  29.1 0.1 fusion.62
  29.2 0.6 slice_bitcast_fusion.1
  29.8 0.2 fusion.50
  30.0 0.2 fusion.90
  30.3 0.0 collective-permute-done.3
  30.3 0.0 collective-permute-done.4
  30.5 0.9 %fusion.5 = f32[5,1,4,64,128]{4,3,2,1,0:T(8,128)S(1)} fusion(f32[5,4,64,128]{3,2,1,0:T(8,128)S(1)} %get-tuple-element.18, f32[5,4,64,1]{3,2,1,0:T(8,128)S(1)} %get-tuple-element.34, f32[5,4,64,1]{3,2,1,0:T(8,128)S(1)} %get-tuple-element.33, f32[5,4,1,128]{3,2,1,0:T(1,128)S(1)} %get-tuple-element.32, f32[5,4,1,128]{3,2,1,0:T(1,128)S(1)} %get-tuple-element.31, ...), kind=kLoop, calls=%fused_computation.9 | loop fusion | flops 5242880 | bytes 4290560 | tf_op jit(solution)/shard_map/stack | solution.py:94
  31.4 0.2 pad_maximum_fusion
  31.6 3.4 %collective-permute-done.2 = f32[4,4,64,128]{3,2,1,0:T(8,128)S(1)} collective-permute-done((f32[4,4,64,128]{3,2,1,0:T(8,128)S(1)}, f32[4,4,64,128]{3,2,1,0:T(8,128)S(1)}, u32[]{:S(2)}, u32[]{:S(2)}) %collective-permute-start.2) | collective-permute-done | bytes 524320 | tf_op jit(solution)/shard_map/ppermute | solution.py:127
  34.9 0.4 bitcast_dynamic-update-slice_fusion.4
  35.4 0.3 bitcast_dynamic-update-slice_fusion.3
  35.7 0.3 bitcast_dynamic-update-slice_fusion.2
  36.0 0.3 bitcast_dynamic-update-slice_fusion.1
  36.4 0.3 bitcast_dynamic-update-slice_fusion
  36.7 0.2 slice_bitcast_fusion
  37.0 0.2 fusion.88
  37.3 0.6 fusion.35
  37.9 8.4 %collective-permute-start.5 = (f32[4,4,64,128]{3,2,1,0:T(8,128)S(1)}, f32[4,4,64,128]{3,2,1,0:T(8,128)S(1)}, u32[]{:S(2)}, u32[]{:S(2)}) collective-permute-start(f32[4,4,64,128]{3,2,1,0:T(8,128)S(1)} %get-tuple-element.6), channel_id=1, source_target_pairs={{0,16},{16,32},{32,48},{48,64},{64,80},{80,96},{96,112},{112,128},... | collective-permute-start | bytes 1572872 | tf_op jit(solution)/shard_map/ppermute | solution.py:140
  46.3 5.8 %collective-permute-start.6 = (f32[5,1,64,128]{3,2,1,0:T(8,128)S(1)}, f32[5,1,64,128]{3,2,1,0:T(8,128)S(1)}, u32[]{:S(2)}, u32[]{:S(2)}) collective-permute-start(f32[5,1,64,128]{3,2,1,0:T(8,128)S(1)} %get-tuple-element.23), channel_id=1, source_target_pairs={{1,0},{2,1},{3,2},{4,3},{5,4},{6,5},{7,6},{8,7},{9,8},{10,9},{11,1... | collective-permute-start | bytes 491528 | tf_op jit(solution)/shard_map/ppermute | solution.py:60
  52.1 3.2 %collective-permute-start.7 = (f32[5,1,64,128]{3,2,1,0:T(8,128)S(1)}, f32[5,1,64,128]{3,2,1,0:T(8,128)S(1)}, u32[]{:S(2)}, u32[]{:S(2)}) collective-permute-start(f32[5,1,64,128]{3,2,1,0:T(8,128)S(1)} %get-tuple-element.24), channel_id=1, source_target_pairs={{0,1},{1,2},{2,3},{3,4},{4,5},{5,6},{6,7},{7,8},{8,9},{9,10},{10,1... | collective-permute-start | bytes 491528 | tf_op jit(solution)/shard_map/ppermute | solution.py:60
  55.4 14.2 %collective-permute-done.6 = f32[5,1,64,128]{3,2,1,0:T(8,128)S(1)} collective-permute-done((f32[5,1,64,128]{3,2,1,0:T(8,128)S(1)}, f32[5,1,64,128]{3,2,1,0:T(8,128)S(1)}, u32[]{:S(2)}, u32[]{:S(2)}) %collective-permute-start.6) | collective-permute-done | bytes 163872 | tf_op jit(solution)/shard_map/ppermute | solution.py:60
  69.6 0.0 collective-permute-done.7
  69.7 0.9 %fusion.11 = f32[5,1,4,64,128]{4,3,2,1,0:T(8,128)S(1)} fusion(f32[5,4,64,128]{3,2,1,0:T(8,128)S(1)} %get-tuple-element.14, f32[5,4,64,1]{3,2,1,0:T(8,128)S(1)} %get-tuple-element.28, f32[5,4,64,1]{3,2,1,0:T(8,128)S(1)} %get-tuple-element.27, f32[5,4,1,128]{3,2,1,0:T(1,128)S(1)} %get-tuple-element.26, f32[5,4,1,128]{3,2,1,0:T(1,128)S(1)} %get-tuple-element.25, ...), kind=kLoop, calls=%fused_computation.15 | loop fusion | flops 5242880 | bytes 4290560 | tf_op jit(solution)/shard_map/stack | solution.py:94
  70.5 0.2 pad_maximum_fusion.1
  70.7 0.0 collective-permute-done.5
  70.7 1.2 %fusion.56 = f32[1,4,4,64,128]{4,3,2,1,0:T(8,128)} fusion(f32[5,4,4,64,128]{4,3,2,1,0:T(8,128)S(1)} %pad_maximum_fusion.1, f32[4,4,64,128]{3,2,1,0:T(8,128)S(1)} %collective-permute-done.5, f32[1,4,4,64,128]{4,3,2,1,0:T(8,128)S(1)} %copy-done, pred[]{:T(512)S(6)} %eq.38), kind=kLoop, calls=%fused_computation.87 | loop fusion | flops 1572864 | bytes 4194305 | tf_op jit(solution)/shard_map/broadcast_in_dim | solution.py:150
  (17 shorter events, 0.2 us)
Async XLA Ops:
  0.0 12.3 %copy-start = (f32[1,4,4,64,128]{4,3,2,1,0:T(8,128)S(1)}, f32[1,4,4,64,128]{4,3,2,1,0:T(8,128)}, u32[]{:S(2)}) copy-start(f32[1,4,4,64,128]{4,3,2,1,0:T(8,128)} %param.3) | copy-start | bytes 1572868
  0.0 14.4 %copy-start.1 = (s32[4,64,128]{2,1,0:T(8,128)S(1)}, s32[4,64,128]{2,1,0:T(8,128)}, u32[]{:S(2)}) copy-start(s32[4,64,128]{2,1,0:T(8,128)} %param.4) | copy-start | bytes 393220
  0.9 11.6 %collective-permute-start = (f32[1,64,128]{2,1,0:T(8,128)S(1)}, f32[1,64,128]{2,1,0:T(8,128)S(1)}, u32[]{:S(2)}, u32[]{:S(2)}) collective-permute-start(f32[1,64,128]{2,1,0:T(8,128)S(1)} %get-tuple-element.41), channel_id=1, source_target_pairs={{1,0},{2,1},{3,2},{4,3},{5,4},{6,5},{7,6},{8,7},{9,8},{10,9},{11,1... | collective-permute-start | bytes 98312 | tf_op jit(solution)/shard_map/ppermute | solution.py:60
  7.1 7.4 %collective-permute-start.1 = (f32[1,64,128]{2,1,0:T(8,128)S(1)}, f32[1,64,128]{2,1,0:T(8,128)S(1)}, u32[]{:S(2)}, u32[]{:S(2)}) collective-permute-start(f32[1,64,128]{2,1,0:T(8,128)S(1)} %get-tuple-element.42), channel_id=1, source_target_pairs={{0,1},{1,2},{2,3},{3,4},{4,5},{5,6},{6,7},{7,8},{8,9},{9,10},{10,1... | collective-permute-start | bytes 98312 | tf_op jit(solution)/shard_map/ppermute | solution.py:60
  14.8 15.5 %collective-permute-start.3 = (f32[1,64,128]{2,1,0:T(8,128)S(1)}, f32[1,64,128]{2,1,0:T(8,128)S(1)}, u32[]{:S(2)}, u32[]{:S(2)}) collective-permute-start(f32[1,64,128]{2,1,0:T(8,128)S(1)} %get-tuple-element.49), channel_id=1, source_target_pairs={{1,0},{2,1},{3,2},{4,3},{5,4},{6,5},{7,6},{8,7},{9,8},{10,9},{11,1... | collective-permute-start | bytes 98312 | tf_op jit(solution)/shard_map/ppermute | solution.py:60
  18.9 11.4 %collective-permute-start.4 = (f32[1,64,128]{2,1,0:T(8,128)S(1)}, f32[1,64,128]{2,1,0:T(8,128)S(1)}, u32[]{:S(2)}, u32[]{:S(2)}) collective-permute-start(f32[1,64,128]{2,1,0:T(8,128)S(1)} %get-tuple-element.50), channel_id=1, source_target_pairs={{0,1},{1,2},{2,3},{3,4},{4,5},{5,6},{6,7},{7,8},{8,9},{9,10},{10,1... | collective-permute-start | bytes 98312 | tf_op jit(solution)/shard_map/ppermute | solution.py:60
  20.9 14.0 %collective-permute-start.2 = (f32[4,4,64,128]{3,2,1,0:T(8,128)S(1)}, f32[4,4,64,128]{3,2,1,0:T(8,128)S(1)}, u32[]{:S(2)}, u32[]{:S(2)}) collective-permute-start(f32[4,4,64,128]{3,2,1,0:T(8,128)S(1)} %fusion.60), channel_id=1, source_target_pairs={{0,16},{16,32},{32,48},{48,64},{64,80},{80,96},{96,112},{112,128},... | collective-permute-start | bytes 1572872 | tf_op jit(solution)/shard_map/ppermute | solution.py:127
  37.9 32.8 %collective-permute-start.5 = (f32[4,4,64,128]{3,2,1,0:T(8,128)S(1)}, f32[4,4,64,128]{3,2,1,0:T(8,128)S(1)}, u32[]{:S(2)}, u32[]{:S(2)}) collective-permute-start(f32[4,4,64,128]{3,2,1,0:T(8,128)S(1)} %get-tuple-element.6), channel_id=1, source_target_pairs={{0,16},{16,32},{32,48},{48,64},{64,80},{80,96},{96,112},{112,128},... | collective-permute-start | bytes 1572872 | tf_op jit(solution)/shard_map/ppermute | solution.py:140
  46.3 23.3 %collective-permute-start.6 = (f32[5,1,64,128]{3,2,1,0:T(8,128)S(1)}, f32[5,1,64,128]{3,2,1,0:T(8,128)S(1)}, u32[]{:S(2)}, u32[]{:S(2)}) collective-permute-start(f32[5,1,64,128]{3,2,1,0:T(8,128)S(1)} %get-tuple-element.23), channel_id=1, source_target_pairs={{1,0},{2,1},{3,2},{4,3},{5,4},{6,5},{7,6},{8,7},{9,8},{10,9},{11,1... | collective-permute-start | bytes 491528 | tf_op jit(solution)/shard_map/ppermute | solution.py:60
  52.1 17.5 %collective-permute-start.7 = (f32[5,1,64,128]{3,2,1,0:T(8,128)S(1)}, f32[5,1,64,128]{3,2,1,0:T(8,128)S(1)}, u32[]{:S(2)}, u32[]{:S(2)}) collective-permute-start(f32[5,1,64,128]{3,2,1,0:T(8,128)S(1)} %get-tuple-element.24), channel_id=1, source_target_pairs={{0,1},{1,2},{2,3},{3,4},{4,5},{5,6},{6,7},{7,8},{8,9},{9,10},{10,1... | collective-permute-start | bytes 491528 | tf_op jit(solution)/shard_map/ppermute | solution.py:60

commit v2 on v1

--- a/solution.py
+++ b/solution.py
@@ -2,8 +2,6 @@
 import jax.numpy as jnp
 from jax import lax
 from jax.sharding import PartitionSpec as P
-
-ITERS = 3
 
 
 radau_nodes = [0.05710419611451768, 0.2768430136381238, 0.5835904323689168, 0.8602401356562195, 1.0]
@@ -101,7 +99,7 @@
     return start + slice_len * total
 
 
-def shards(guess, fibre, labels):
+def steps(guess, fibre, labels):
     table = radau_table()
     sums = [sum(row) for row in table]
     fast_g = lookup(labels, [4.0, 3.0, 3.5, 1.0])
@@ -119,12 +117,17 @@
     volts0 = start0[0]
     planes = volts0.shape[0]
 
-    low0, high0 = halos(volts0)
+    rough = rates(start0, laplacian(volts0, volts0[:1], volts0[planes - 1 :], conduct), fast_g, slow_g, slow_tau)
+    rough_ends, edge_volts = lax.optimization_barrier((start0 + slice_len * (sums[4] * rough), volts0))
+    arrived_rough = lax.ppermute(rough_ends, "tm", tm_pairs)
+    low0, high0 = halos(edge_volts)
     low0 = jnp.where(at_low, volts0[:1], low0)
     high0 = jnp.where(at_high, volts0[planes - 1 :], high0)
     derivs0 = rates(start0, laplacian(volts0, low0, high0, conduct), fast_g, slow_g, slow_tau)
     ends0 = start0 + slice_len * (sums[4] * derivs0)
-    arrived1 = lax.ppermute(ends0, "tm", tm_pairs)
+    edges = jnp.concatenate([ends0[0, :1], ends0[0, planes - 1 :]])
+    arrived_edges = lax.ppermute(edges, "tm", tm_pairs)
+    arrived1 = arrived_rough.at[0, 0].set(arrived_edges[0]).at[0, planes - 1].set(arrived_edges[1])
 
     dv = derivs0[0]
     dlow, dhigh = halos(dv)
@@ -153,7 +156,7 @@
 def solution(mesh):
     placed = (P("tm", None, "space", None, None), P("space", None, None), P("space", None, None))
     return jax.shard_map(
-        shards,
+        steps,
         mesh=mesh,
         in_specs=placed,
         out_specs=P("tm", None, "space", None, None),

time: 72.3 us -> 73.4 us (1.015)
  the two profiles are of different devices: /device:TPU:27 before, /device:TPU:7 now
where the time goes in v2:
time: 73.4 us; the launch traced here: 73 us
  starting transfers between devices  40.3 us (55%)
  waiting for transfers between devices  16.3 us (22%)
  other arithmetic  13.8 us (19%)
  local copies, waits for them, and re-layouts  2.12 us (3%)
    ppermute x6, starting transfers between devices, shift_space(): return lax.ppermute(block, 'space', pairs)  25.5 us
    ppermute x6, waiting for transfers between devices, shift_space(): return lax.ppermute(block, 'space', pairs)  16.3 us
    ppermute x1, starting transfers between devices, steps(): arrived_rough = lax.ppermute(rough_ends, 'tm', tm_pairs)  6.96 us
    ppermute x1, starting transfers between devices, steps(): arrived_edges = lax.ppermute(edges, 'tm', tm_pairs)  4.74 us
    ppermute x1, starting transfers between devices, steps(): arrived2 = lax.ppermute(ends1, 'tm', tm_pairs)  3.09 us
    another operation x5, other arithmetic, rates(): return jnp.stack([dvolt, dact, dinact, dslow], axis=-4)  2.38 us
    add x2, other arithmetic, lookup(): total + jnp.where(labels == level, values[level], 0.0).astype(jnp.float32)  2.13 us
    scatter x1, other arithmetic, steps(): arrived_rough.at[0, 0].set(arrived_edges[0]).at[0, planes - 1]  1.89 us
  transfers between devices with their start and end apart: 9, of which 3 were waited for; matrix products, arithmetic and copies ran while one was open for 7% of the time, Pallas kernels for 0%

profile of v2, /device:TPU:7, one launch (start us, length us, event | category | flops | bytes accessed | tf_op | source)
XLA Modules:
  0.0 73.0 jit_solution(17911499352670564244)
XLA Ops:
  0.0 0.0 copy-start
  0.0 0.0 copy-start.1
  0.0 0.8 %slice_bitcast_fusion.8 = (f32[1,64,128]{2,1,0:T(8,128)S(1)}, f32[1,64,128]{2,1,0:T(8,128)S(1)}) fusion(f32[1,4,4,64,128]{4,3,2,1,0:T(8,128)} %param.7), kind=kLoop, calls=%fused_computation.201 | loop fusion | bytes 131072 | tf_op jit(solution)/shard_map/slice | solution.py:120
  0.9 1.2 %fusion.99 = (f32[1,4,64,128]{3,2,1,0:T(8,128)S(1)}, f32[1,1,4,64,128]{4,3,2,0,1:T(8,128)S(1)}, f32[1,1,4,64,128]{4,3,2,1,0:T(8,128)S(1)}, f32[4,64,128]{2,1,0:T(8,128)S(1)}) fusion(f32[1,4,4,64,128]{4,3,2,1,0:T(8,128)} %param.7), kind=kLoop, calls=%fused_computation.207 | loop fusion | flops 655360 | bytes 917504 | tf_op jit(solution)/shard_map/div | solution.py:87
  2.0 0.0 copy-start.2
  2.0 0.1 fusion.108
  2.1 1.0 %select_add_fusion.1 = (f32[4,64,128]{2,1,0:T(8,128)S(1)}, pred[4,64,128]{2,1,0:T(8,128)(4,1)S(1)}, pred[4,64,128]{2,1,0:T(8,128)(4,1)S(1)}, pred[4,64,128]{2,1,0:T(8,128)(4,1)S(1)}, pred[4,64,128]{2,1,0:T(8,128)(4,1)S(1)}) fusion(s32[4,64,128]{2,1,0:T(8,128)} %param.9), kind=kLoop, calls=%fused_computation.171 | loop fusion | flops 360448 | bytes 393216 | tf_op jit(solution)/shard_map/add | solution.py:34
  3.2 1.1 %select_add_fusion = (f32[4,64,128]{2,1,0:T(8,128)S(1)}, f32[4,64,128]{2,1,0:T(8,128)S(1)}, f32[4,64,128]{2,1,0:T(8,128)S(1)}) fusion(pred[4,64,128]{2,1,0:T(8,128)(4,1)S(1)} %get-tuple-element.41, pred[4,64,128]{2,1,0:T(8,128)(4,1)S(1)} %get-tuple-element.40, pred[4,64,128]{2,1,0:T(8,128)(4,1)S(1)} %get-tuple-element.39, ...), kind=kLoop, calls=%fused_computation.170 | loop fusion | flops 720896 | bytes 786432 | tf_op jit(solution)/shard_map/add | solution.py:34
  4.3 0.0 copy-done
  4.3 0.0 copy-done.1
  4.3 0.3 fusion.92
  4.6 0.1 fusion.53
  4.7 6.5 %collective-permute-start.1 = (f32[1,64,128]{2,1,0:T(8,128)S(1)}, f32[1,64,128]{2,1,0:T(8,128)S(1)}, u32[]{:S(2)}, u32[]{:S(2)}) collective-permute-start(f32[1,64,128]{2,1,0:T(8,128)S(1)} %get-tuple-element.84), channel_id=1, source_target_pairs={{1,0},{2,1},{3,2},{4,3},{5,4},{6,5},{7,6},{8,7},{9,8},{10,9},{11,1... | collective-permute-start | bytes 98312 | tf_op jit(solution)/shard_map/ppermute | solution.py:58
  11.2 1.9 %collective-permute-start.2 = (f32[1,64,128]{2,1,0:T(8,128)S(1)}, f32[1,64,128]{2,1,0:T(8,128)S(1)}, u32[]{:S(2)}, u32[]{:S(2)}) collective-permute-start(f32[1,64,128]{2,1,0:T(8,128)S(1)} %get-tuple-element.85), channel_id=1, source_target_pairs={{0,1},{1,2},{2,3},{3,4},{4,5},{5,6},{6,7},{7,8},{8,9},{9,10},{10,1... | collective-permute-start | bytes 98312 | tf_op jit(solution)/shard_map/ppermute | solution.py:58
  13.2 7.0 %collective-permute-start = (f32[4,4,64,128]{3,2,1,0:T(8,128)S(1)}, f32[4,4,64,128]{3,2,1,0:T(8,128)S(1)}, u32[]{:S(2)}, u32[]{:S(2)}) collective-permute-start(f32[4,4,64,128]{3,2,1,0:T(8,128)S(1)} %fusion.53), channel_id=1, source_target_pairs={{0,16},{16,32},{32,48},{48,64},{64,80},{80,96},{96,112},{112,128},... | collective-permute-start | bytes 1572872 | tf_op jit(solution)/shard_map/ppermute | solution.py:122
  20.1 0.0 copy-done.2
  20.2 0.8 %and_reduce_fusion = pred[]{:T(512)} fusion(s32[4]{0:T(128)S(1)} %copy-done.2, s32[1]{0:T(128)} %constant.192.clone.1, s32[2]{0:T(128)S(1)} %iota_multiply_fusion), kind=kLoop, calls=%fused_computation.204 | loop fusion | flops 23 | bytes 29 | tf_op jit(solution)/shard_map/reduce.3
  20.9 0.6 fusion.110
  21.5 0.0 collective-permute-done.1
  21.5 0.0 collective-permute-done.2
  21.5 0.2 select_add_fusion.4
  21.7 2.5 %collective-permute-start.5 = (f32[1,64,128]{2,1,0:T(8,128)S(1)}, f32[1,64,128]{2,1,0:T(8,128)S(1)}, u32[]{:S(2)}, u32[]{:S(2)}) collective-permute-start(f32[1,64,128]{2,1,0:T(8,128)S(1)} %get-tuple-element.83), channel_id=1, source_target_pairs={{0,1},{1,2},{2,3},{3,4},{4,5},{5,6},{6,7},{7,8},{8,9},{9,10},{10,1... | collective-permute-start | bytes 98312 | tf_op jit(solution)/shard_map/ppermute | solution.py:58
  24.2 0.1 fusion.55
  24.3 4.7 %collective-permute-start.3 = (f32[2,64,128]{2,1,0:T(8,128)S(1)}, f32[2,64,128]{2,1,0:T(8,128)S(1)}, u32[]{:S(2)}, u32[]{:S(2)}) collective-permute-start(f32[2,64,128]{2,1,0:T(8,128)S(1)} %pad_maximum_fusion.29), channel_id=1, source_target_pairs={{0,16},{16,32},{32,48},{48,64},{64,80},{80,96},{96,112},{112,128},... | collective-permute-start | bytes 196616 | tf_op jit(solution)/shard_map/ppermute | solution.py:129
  29.1 0.1 fusion.66
  29.2 0.1 fusion.67
  29.2 0.1 fusion.68
  29.3 0.1 fusion.69
  29.4 0.1 fusion.65
  29.5 0.6 slice_bitcast_fusion.1
  30.1 0.2 fusion.50
  30.3 0.2 fusion.105
  30.6 6.3 %collective-permute-start.4 = (f32[1,64,128]{2,1,0:T(8,128)S(1)}, f32[1,64,128]{2,1,0:T(8,128)S(1)}, u32[]{:S(2)}, u32[]{:S(2)}) collective-permute-start(f32[1,64,128]{2,1,0:T(8,128)S(1)} %get-tuple-element.82), channel_id=1, source_target_pairs={{1,0},{2,1},{3,2},{4,3},{5,4},{6,5},{7,6},{8,7},{9,8},{10,9},{11,1... | collective-permute-start | bytes 98312 | tf_op jit(solution)/shard_map/ppermute | solution.py:58
  36.9 0.0 collective-permute-done.5
  36.9 1.0 %collective-permute-done.4 = f32[1,64,128]{2,1,0:T(8,128)S(1)} collective-permute-done((f32[1,64,128]{2,1,0:T(8,128)S(1)}, f32[1,64,128]{2,1,0:T(8,128)S(1)}, u32[]{:S(2)}, u32[]{:S(2)}) %collective-permute-start.4) | collective-permute-done | bytes 32800 | tf_op jit(solution)/shard_map/ppermute | solution.py:58
  38.1 0.9 %fusion.5 = f32[5,1,4,64,128]{4,3,2,1,0:T(8,128)S(1)} fusion(f32[5,4,64,128]{3,2,1,0:T(8,128)S(1)} %get-tuple-element.48, f32[5,4,64,1]{3,2,1,0:T(8,128)S(1)} %get-tuple-element.64, f32[5,4,64,1]{3,2,1,0:T(8,128)S(1)} %get-tuple-element.63, f32[5,4,1,128]{3,2,1,0:T(1,128)S(1)} %get-tuple-element.62, f32[5,4,1,128]{3,2,1,0:T(1,128)S(1)} %get-tuple-element.61, ...), kind=kLoop, calls=%fused_computation.15 | loop fusion | flops 5242880 | bytes 4290560 | tf_op jit(solution)/shard_map/stack | solution.py:92
  38.9 0.2 pad_maximum_fusion
  39.1 0.0 collective-permute-done.3
  39.1 0.0 collective-permute-done
  39.1 1.9 %fusion.96 = f32[4,4,64,128]{3,2,1,0:T(8,128)S(1)} fusion(f32[4,4,64,128]{3,2,1,0:T(8,128)S(1)} %fusion.97, s32[]{:T(128)} %bitcast.16, s32[]{:T(128)} %bitcast.17, f32[2,64,128]{2,1,0:T(8,128)S(1)} %collective-permute-done.3, pred[]{:T(512)} %and_reduce_fusion), kind=kLoop, calls=%fused_computation.195 | loop fusion | flops 8192 | bytes 98313 | tf_op jit(solution)/shard_map/scatter | solution.py:130
  41.0 0.4 bitcast_dynamic-update-slice_fusion.4
  41.4 0.3 bitcast_dynamic-update-slice_fusion.3
  41.8 0.3 bitcast_dynamic-update-slice_fusion.2
  42.1 0.3 bitcast_dynamic-update-slice_fusion.1
  42.5 0.3 bitcast_dynamic-update-slice_fusion
  42.8 0.2 slice_bitcast_fusion
  43.1 0.2 fusion.103
  43.3 0.6 fusion.35
  44.0 3.1 %collective-permute-start.6 = (f32[4,4,64,128]{3,2,1,0:T(8,128)S(1)}, f32[4,4,64,128]{3,2,1,0:T(8,128)S(1)}, u32[]{:S(2)}, u32[]{:S(2)}) collective-permute-start(f32[4,4,64,128]{3,2,1,0:T(8,128)S(1)} %get-tuple-element.34), channel_id=1, source_target_pairs={{0,16},{16,32},{32,48},{48,64},{64,80},{80,96},{96,112},{112,128},... | collective-permute-start | bytes 1572872 | tf_op jit(solution)/shard_map/ppermute | solution.py:143
  47.1 6.3 %collective-permute-start.7 = (f32[5,1,64,128]{3,2,1,0:T(8,128)S(1)}, f32[5,1,64,128]{3,2,1,0:T(8,128)S(1)}, u32[]{:S(2)}, u32[]{:S(2)}) collective-permute-start(f32[5,1,64,128]{3,2,1,0:T(8,128)S(1)} %get-tuple-element.53), channel_id=1, source_target_pairs={{1,0},{2,1},{3,2},{4,3},{5,4},{6,5},{7,6},{8,7},{9,8},{10,9},{11,1... | collective-permute-start | bytes 491528 | tf_op jit(solution)/shard_map/ppermute | solution.py:58
  53.4 1.9 %collective-permute-start.8 = (f32[5,1,64,128]{3,2,1,0:T(8,128)S(1)}, f32[5,1,64,128]{3,2,1,0:T(8,128)S(1)}, u32[]{:S(2)}, u32[]{:S(2)}) collective-permute-start(f32[5,1,64,128]{3,2,1,0:T(8,128)S(1)} %get-tuple-element.54), channel_id=1, source_target_pairs={{0,1},{1,2},{2,3},{3,4},{4,5},{5,6},{6,7},{7,8},{8,9},{9,10},{10,1... | collective-permute-start | bytes 491528 | tf_op jit(solution)/shard_map/ppermute | solution.py:58
  55.3 8.7 %collective-permute-done.7 = f32[5,1,64,128]{3,2,1,0:T(8,128)S(1)} collective-permute-done((f32[5,1,64,128]{3,2,1,0:T(8,128)S(1)}, f32[5,1,64,128]{3,2,1,0:T(8,128)S(1)}, u32[]{:S(2)}, u32[]{:S(2)}) %collective-permute-start.7) | collective-permute-done | bytes 163872 | tf_op jit(solution)/shard_map/ppermute | solution.py:58
  64.1 6.6 %collective-permute-done.8 = f32[5,1,64,128]{3,2,1,0:T(8,128)S(1)} collective-permute-done((f32[5,1,64,128]{3,2,1,0:T(8,128)S(1)}, f32[5,1,64,128]{3,2,1,0:T(8,128)S(1)}, u32[]{:S(2)}, u32[]{:S(2)}) %collective-permute-start.8) | collective-permute-done | bytes 163872 | tf_op jit(solution)/shard_map/ppermute | solution.py:58
  70.7 0.9 %fusion.11 = f32[5,1,4,64,128]{4,3,2,1,0:T(8,128)S(1)} fusion(f32[5,4,64,128]{3,2,1,0:T(8,128)S(1)} %get-tuple-element.44, f32[5,4,64,1]{3,2,1,0:T(8,128)S(1)} %get-tuple-element.58, f32[5,4,64,1]{3,2,1,0:T(8,128)S(1)} %get-tuple-element.57, f32[5,4,1,128]{3,2,1,0:T(1,128)S(1)} %get-tuple-element.56, f32[5,4,1,128]{3,2,1,0:T(1,128)S(1)} %get-tuple-element.55, ...), kind=kLoop, calls=%fused_computation.21 | loop fusion | flops 5242880 | bytes 4290560 | tf_op jit(solution)/shard_map/stack | solution.py:92
  71.6 0.2 pad_maximum_fusion.1
  71.8 0.0 collective-permute-done.6
  71.8 1.2 %fusion.60 = f32[1,4,4,64,128]{4,3,2,1,0:T(8,128)} fusion(f32[5,4,4,64,128]{4,3,2,1,0:T(8,128)S(1)} %pad_maximum_fusion.1, f32[4,4,64,128]{3,2,1,0:T(8,128)S(1)} %collective-permute-done.6, f32[1,4,4,64,128]{4,3,2,1,0:T(8,128)S(1)} %copy-done, pred[]{:T(512)S(6)} %eq.38), kind=kLoop, calls=%fused_computation.97 | loop fusion | flops 1572864 | bytes 4194305 | tf_op jit(solution)/shard_map/broadcast_in_dim | solution.py:153
  (22 shorter events, 0.3 us)
Async XLA Ops:
  0.0 4.3 %copy-start = (f32[1,4,4,64,128]{4,3,2,1,0:T(8,128)S(1)}, f32[1,4,4,64,128]{4,3,2,1,0:T(8,128)}, u32[]{:S(2)}) copy-start(f32[1,4,4,64,128]{4,3,2,1,0:T(8,128)} %param.7) | copy-start | bytes 1572868
  0.0 4.3 %copy-start.1 = (s32[4,64,128]{2,1,0:T(8,128)S(1)}, s32[4,64,128]{2,1,0:T(8,128)}, u32[]{:S(2)}) copy-start(s32[4,64,128]{2,1,0:T(8,128)} %param.8) | copy-start | bytes 393220
  2.0 18.1 %copy-start.2 = (s32[4]{0:T(128)S(1)}, s32[4]{0:T(128)}, u32[]{:S(2)}) copy-start(s32[4]{0:T(128)} %constant.193.clone.1) | copy-start | bytes 52
  4.7 16.8 %collective-permute-start.1 = (f32[1,64,128]{2,1,0:T(8,128)S(1)}, f32[1,64,128]{2,1,0:T(8,128)S(1)}, u32[]{:S(2)}, u32[]{:S(2)}) collective-permute-start(f32[1,64,128]{2,1,0:T(8,128)S(1)} %get-tuple-element.84), channel_id=1, source_target_pairs={{1,0},{2,1},{3,2},{4,3},{5,4},{6,5},{7,6},{8,7},{9,8},{10,9},{11,1... | collective-permute-start | bytes 98312 | tf_op jit(solution)/shard_map/ppermute | solution.py:58
  11.2 10.3 %collective-permute-start.2 = (f32[1,64,128]{2,1,0:T(8,128)S(1)}, f32[1,64,128]{2,1,0:T(8,128)S(1)}, u32[]{:S(2)}, u32[]{:S(2)}) collective-permute-start(f32[1,64,128]{2,1,0:T(8,128)S(1)} %get-tuple-element.85), channel_id=1, source_target_pairs={{0,1},{1,2},{2,3},{3,4},{4,5},{5,6},{6,7},{7,8},{8,9},{9,10},{10,1... | collective-permute-start | bytes 98312 | tf_op jit(solution)/shard_map/ppermute | solution.py:58
  13.2 26.0 %collective-permute-start = (f32[4,4,64,128]{3,2,1,0:T(8,128)S(1)}, f32[4,4,64,128]{3,2,1,0:T(8,128)S(1)}, u32[]{:S(2)}, u32[]{:S(2)}) collective-permute-start(f32[4,4,64,128]{3,2,1,0:T(8,128)S(1)} %fusion.53), channel_id=1, source_target_pairs={{0,16},{16,32},{32,48},{48,64},{64,80},{80,96},{96,112},{112,128},... | collective-permute-start | bytes 1572872 | tf_op jit(solution)/shard_map/ppermute | solution.py:122
  21.7 15.2 %collective-permute-start.5 = (f32[1,64,128]{2,1,0:T(8,128)S(1)}, f32[1,64,128]{2,1,0:T(8,128)S(1)}, u32[]{:S(2)}, u32[]{:S(2)}) collective-permute-start(f32[1,64,128]{2,1,0:T(8,128)S(1)} %get-tuple-element.83), channel_id=1, source_target_pairs={{0,1},{1,2},{2,3},{3,4},{4,5},{5,6},{6,7},{7,8},{8,9},{9,10},{10,1... | collective-permute-start | bytes 98312 | tf_op jit(solution)/shard_map/ppermute | solution.py:58
  24.3 14.8 %collective-permute-start.3 = (f32[2,64,128]{2,1,0:T(8,128)S(1)}, f32[2,64,128]{2,1,0:T(8,128)S(1)}, u32[]{:S(2)}, u32[]{:S(2)}) collective-permute-start(f32[2,64,128]{2,1,0:T(8,128)S(1)} %pad_maximum_fusion.29), channel_id=1, source_target_pairs={{0,16},{16,32},{32,48},{48,64},{64,80},{80,96},{96,112},{112,128},... | collective-permute-start | bytes 196616 | tf_op jit(solution)/shard_map/ppermute | solution.py:129
  30.6 7.3 %collective-permute-start.4 = (f32[1,64,128]{2,1,0:T(8,128)S(1)}, f32[1,64,128]{2,1,0:T(8,128)S(1)}, u32[]{:S(2)}, u32[]{:S(2)}) collective-permute-start(f32[1,64,128]{2,1,0:T(8,128)S(1)} %get-tuple-element.82), channel_id=1, source_target_pairs={{1,0},{2,1},{3,2},{4,3},{5,4},{6,5},{7,6},{8,7},{9,8},{10,9},{11,1... | collective-permute-start | bytes 98312 | tf_op jit(solution)/shard_map/ppermute | solution.py:58
  44.0 27.8 %collective-permute-start.6 = (f32[4,4,64,128]{3,2,1,0:T(8,128)S(1)}, f32[4,4,64,128]{3,2,1,0:T(8,128)S(1)}, u32[]{:S(2)}, u32[]{:S(2)}) collective-permute-start(f32[4,4,64,128]{3,2,1,0:T(8,128)S(1)} %get-tuple-element.34), channel_id=1, source_target_pairs={{0,16},{16,32},{32,48},{48,64},{64,80},{80,96},{96,112},{112,128},... | collective-permute-start | bytes 1572872 | tf_op jit(solution)/shard_map/ppermute | solution.py:143
  47.1 17.0 %collective-permute-start.7 = (f32[5,1,64,128]{3,2,1,0:T(8,128)S(1)}, f32[5,1,64,128]{3,2,1,0:T(8,128)S(1)}, u32[]{:S(2)}, u32[]{:S(2)}) collective-permute-start(f32[5,1,64,128]{3,2,1,0:T(8,128)S(1)} %get-tuple-element.53), channel_id=1, source_target_pairs={{1,0},{2,1},{3,2},{4,3},{5,4},{6,5},{7,6},{8,7},{9,8},{10,9},{11,1... | collective-permute-start | bytes 491528 | tf_op jit(solution)/shard_map/ppermute | solution.py:58
  53.4 17.3 %collective-permute-start.8 = (f32[5,1,64,128]{3,2,1,0:T(8,128)S(1)}, f32[5,1,64,128]{3,2,1,0:T(8,128)S(1)}, u32[]{:S(2)}, u32[]{:S(2)}) collective-permute-start(f32[5,1,64,128]{3,2,1,0:T(8,128)S(1)} %get-tuple-element.54), channel_id=1, source_target_pairs={{0,1},{1,2},{2,3},{3,4},{4,5},{5,6},{6,7},{7,8},{8,9},{9,10},{10,1... | collective-permute-start | bytes 491528 | tf_op jit(solution)/shard_map/ppermute | solution.py:58

commit v3 on v1

--- a/solution.py
+++ b/solution.py
@@ -60,18 +60,25 @@
     return lax.ppermute(block, "space", pairs)
 
 
-def halos(volts):
-    planes = volts.shape[-3]
-    low = shift_space(volts[..., planes - 1 : planes, :, :], True)
-    high = shift_space(volts[..., 0:1, :, :], False)
-    return low, high
+def close_edges(volts, depth, at_low, at_high):
+    size = volts.shape[-3]
+    inner_low = volts[..., depth : depth + 1, :, :]
+    inner_high = volts[..., size - depth - 1 : size - depth, :, :]
+    outer_low = jnp.where(at_low, inner_low, volts[..., depth - 1 : depth, :, :])
+    outer_high = jnp.where(at_high, inner_high, volts[..., size - depth : size - depth + 1, :, :])
+    return jnp.concatenate(
+        [volts[..., : depth - 1, :, :], outer_low, volts[..., depth : size - depth, :, :], outer_high,
+         volts[..., size - depth + 1 :, :, :]],
+        axis=-3,
+    )
 
 
-def laplacian(volts, low, high, conduct):
-    padded = jnp.concatenate([low, volts, high], axis=-3)
-    lap = conduct[0] * second(padded, volts.ndim - 3)
-    lap = lap + conduct[1] * second(edge_pad(volts, volts.ndim - 2), volts.ndim - 2)
-    lap = lap + conduct[2] * second(edge_pad(volts, volts.ndim - 1), volts.ndim - 1)
+def laplacian(volts, conduct):
+    x = volts.ndim - 3
+    inner = lax.slice_in_dim(volts, 1, volts.shape[x] - 1, axis=x)
+    lap = conduct[0] * second(volts, x)
+    lap = lap + conduct[1] * second(edge_pad(inner, x + 1), x + 1)
+    lap = lap + conduct[2] * second(edge_pad(inner, x + 2), x + 2)
     return lap
 
 
@@ -101,13 +108,14 @@
     return start + slice_len * total
 
 
+def trim(block, depth):
+    size = block.shape[-3]
+    return block[..., depth : size - depth, :, :]
+
+
 def shards(guess, fibre, labels):
     table = radau_table()
     sums = [sum(row) for row in table]
-    fast_g = lookup(labels, [4.0, 3.0, 3.5, 1.0])
-    slow_g = lookup(labels, [0.6, 0.9, 0.75, 0.3])
-    slow_tau = 4.0 * lookup(labels, [1.0, 1.5, 1.2, 3.0])
-    conduct = [0.2 + 0.6 * (fibre == d).astype(jnp.float32) for d in range(3)]
     place = lax.axis_index("space")
     at_low = place == 0
     at_high = place == lax.axis_size("space") - 1
@@ -116,35 +124,60 @@
     tm_pairs = [(i, i + 1) for i in range(count - 1)]
 
     start0 = guess[0]
-    volts0 = start0[0]
-    planes = volts0.shape[0]
+    planes = start0.shape[1]
+    code = (labels + 4 * fibre).astype(jnp.float32)
 
-    low0, high0 = halos(volts0)
-    low0 = jnp.where(at_low, volts0[:1], low0)
-    high0 = jnp.where(at_high, volts0[planes - 1 :], high0)
-    derivs0 = rates(start0, laplacian(volts0, low0, high0, conduct), fast_g, slow_g, slow_tau)
-    ends0 = start0 + slice_len * (sums[4] * derivs0)
-    arrived1 = lax.ppermute(ends0, "tm", tm_pairs)
+    top = jnp.concatenate([start0[0, planes - 3 :], start0[1:, planes - 2 :].reshape(-1, *start0.shape[2:]), code[planes - 2 :]])
+    bottom = jnp.concatenate([start0[0, :3], start0[1:, :2].reshape(-1, *start0.shape[2:]), code[:2]])
+    below = shift_space(top, True)
+    above = shift_space(bottom, False)
 
-    dv = derivs0[0]
-    dlow, dhigh = halos(dv)
-    nodes0 = jnp.stack([start0 + slice_len * (sums[m] * derivs0) for m in range(5)])
-    volts1 = nodes0[:, 0]
-    low1 = jnp.stack([low0 + slice_len * (sums[m] * dlow) for m in range(5)])
-    high1 = jnp.stack([high0 + slice_len * (sums[m] * dhigh) for m in range(5)])
-    low1 = jnp.where(at_low, volts1[:, :1], low1)
-    high1 = jnp.where(at_high, volts1[:, planes - 1 :], high1)
-    derivs1 = rates(nodes0, laplacian(volts1, low1, high1, conduct), fast_g, slow_g, slow_tau)
-    start1 = jnp.where(first_slice, start0, arrived1)
-    ends1 = quadrature(start1, derivs1, table[4])
+    def unpack(part, volts_first):
+        volts = part[:3]
+        gates = part[3:9].reshape(3, 2, *part.shape[1:])
+        return volts, gates, part[9:11]
+
+    low_v, low_g, low_c = unpack(below, True)
+    high_v, high_g, high_c = unpack(above, False)
+    volts_ext = jnp.concatenate([low_v, start0[0], high_v])
+    gates_ext = jnp.concatenate([low_g, start0[1:], high_g], axis=1)
+    code_ext = jnp.concatenate([low_c, code, high_c]).astype(jnp.int32)
+    fibre_ext = code_ext // 4
+    labels_ext = code_ext % 4
+    fast_g = lookup(labels_ext, [4.0, 3.0, 3.5, 1.0])
+    slow_g = lookup(labels_ext, [0.6, 0.9, 0.75, 0.3])
+    slow_tau = 4.0 * lookup(labels_ext, [1.0, 1.5, 1.2, 3.0])
+    conduct = [0.2 + 0.6 * (fibre_ext == d).astype(jnp.float32) for d in range(3)]
+    coef = lambda depth: [trim(c, 2 - depth) for c in (fast_g, slow_g, slow_tau)]
+    cond = lambda depth: [trim(c, 2 - depth) for c in conduct]
+
+    state_ext = jnp.concatenate([trim(volts_ext, 1)[None], gates_ext])
+    lap0 = laplacian(close_edges(volts_ext, 3, at_low, at_high), cond(2))
+    derivs0 = rates(state_ext, lap0, *coef(2))
+    nodes0 = jnp.stack([state_ext + slice_len * (sums[m] * derivs0) for m in range(5)])
+    ends0 = trim(nodes0[4], 1)
+    message1 = jnp.concatenate(
+        [trim(ends0, 1).reshape(-1, *ends0.shape[2:]), ends0[0, :1], ends0[0, planes + 1 :]]
+    )
+    arrived1 = lax.ppermute(message1, "tm", tm_pairs)
+    fields = start0.shape[0]
+    start1_block = jnp.where(first_slice, start0, arrived1[: fields * planes].reshape(start0.shape))
+    start1_volts = jnp.where(
+        first_slice,
+        trim(volts_ext, 2),
+        jnp.concatenate([arrived1[fields * planes : fields * planes + 1], start1_block[0], arrived1[fields * planes + 1 :]]),
+    )
+
+    lap1 = laplacian(close_edges(nodes0[:, 0], 2, at_low, at_high), cond(1))
+    derivs1 = rates(trim(nodes0, 1), lap1, *coef(1))
+    ends1 = quadrature(start1_block, trim(derivs1, 1), table[4])
     arrived2 = lax.ppermute(ends1, "tm", tm_pairs)
-    nodes1 = jnp.stack([quadrature(start1, derivs1, table[m]) for m in range(4)] + [ends1])
+    volts1 = jnp.stack([quadrature(start1_volts, derivs1[:, 0], table[m]) for m in range(5)])
+    gates1 = jnp.stack([quadrature(start1_block[1:], trim(derivs1[:, 1:], 1), table[m]) for m in range(5)])
+    nodes1 = jnp.concatenate([trim(volts1, 1)[:, None], gates1], axis=1)
 
-    volts2 = nodes1[:, 0]
-    low2, high2 = halos(volts2)
-    low2 = jnp.where(at_low, volts2[:, :1], low2)
-    high2 = jnp.where(at_high, volts2[:, planes - 1 :], high2)
-    derivs2 = rates(nodes1, laplacian(volts2, low2, high2, conduct), fast_g, slow_g, slow_tau)
+    lap2 = laplacian(close_edges(volts1, 1, at_low, at_high), cond(0))
+    derivs2 = rates(nodes1, lap2, *coef(0))
     start2 = jnp.where(first_slice, start0, arrived2)
     ends2 = quadrature(start2, derivs2, table[4])
     return ends2[None]

time: 72.3 us -> 77.1 us (1.066)
  the two profiles are of different devices: /device:TPU:27 before, /device:TPU:1 now
where the time goes in v3:
time: 77.1 us; the launch traced here: 76.8 us
  waiting for transfers between devices  35.7 us (46%)
  starting transfers between devices  23.1 us (30%)
  other arithmetic  12.8 us (17%)
  local copies, waits for them, and re-layouts  4.63 us (6%)
    ppermute x2, waiting for transfers between devices, shift_space(): return lax.ppermute(block, 'space', pairs)  17.8 us
    ppermute x1, waiting for transfers between devices, shards(): arrived2 = lax.ppermute(ends1, 'tm', tm_pairs)  9.87 us
    ppermute x1, starting transfers between devices, shards(): arrived1 = lax.ppermute(message1, 'tm', tm_pairs)  9.01 us
    ppermute x1, starting transfers between devices, shards(): arrived2 = lax.ppermute(ends1, 'tm', tm_pairs)  8.38 us
    ppermute x1, waiting for transfers between devices, shards(): arrived1 = lax.ppermute(message1, 'tm', tm_pairs)  8.05 us
    ppermute x2, starting transfers between devices, shift_space(): return lax.ppermute(block, 'space', pairs)  5.67 us
    sub x2, other arithmetic, rates(): dvolt = lap - current  2.67 us
    another operation x4, other arithmetic, rates(): return jnp.stack([dvolt, dact, dinact, dslow], axis=-4)  2.33 us
  transfers between devices with their start and end apart: 4, of which 4 were waited for; matrix products, arithmetic and copies ran while one was open for 7% of the time, Pallas kernels for 0%

profile of v3, /device:TPU:1, one launch (start us, length us, event | category | flops | bytes accessed | tf_op | source)
XLA Modules:
  0.0 76.8 jit_solution(4807653012630879832)
XLA Ops:
  0.0 0.0 copy-start
  0.0 1.1 %fusion.73 = (f32[3,2,64,128]{3,2,1,0:T(8,128)S(1)}, f32[3,2,64,128]{3,2,1,0:T(8,128)S(1)}) fusion(f32[4,4,64,128]{3,2,1,0:T(8,128)} %bitcast.238), kind=kLoop, calls=%fused_computation.215 | loop fusion | bytes 786432 | tf_op jit(solution)/shard_map/slice | solution.py:130
  1.1 1.0 %slice_bitcast_fusion.13 = (f32[3,64,128]{2,1,0:T(8,128)S(1)}, f32[3,64,128]{2,1,0:T(8,128)S(1)}) fusion(f32[4,4,64,128]{3,2,1,0:T(8,128)} %bitcast.239), kind=kLoop, calls=%fused_computation.196 | loop fusion | bytes 393216 | tf_op jit(solution)/shard_map/squeeze | solution.py:130
  2.1 1.0 %add_convert_fusion = f32[4,64,128]{2,1,0:T(8,128)S(1)} fusion(s32[4,64,128]{2,1,0:T(8,128)} %param.5, s32[4,64,128]{2,1,0:T(8,128)} %param.4), kind=kLoop, calls=%fused_computation.194 | loop fusion | flops 98304 | bytes 393216 | tf_op jit(solution)/shard_map/convert_element_type | solution.py:128
  3.1 4.4 %collective-permute-start = (f32[11,64,128]{2,1,0:T(8,128)S(1)}, f32[11,64,128]{2,1,0:T(8,128)S(1)}, u32[]{:S(2)}, u32[]{:S(2)}) collective-permute-start(f32[11,64,128]{2,1,0:T(8,128)S(1)} %pad_maximum_fusion.33), channel_id=1, source_target_pairs={{0,1},{1,2},{2,3},{3,4},{4,5},{5,6},{6,7},{7,8},{8,9},{9,10},{10,1... | collective-permute-start | bytes 1081352 | tf_op jit(solution)/shard_map/ppermute | solution.py:60
  7.6 1.3 %collective-permute-start.1 = (f32[11,64,128]{2,1,0:T(8,128)S(1)}, f32[11,64,128]{2,1,0:T(8,128)S(1)}, u32[]{:S(2)}, u32[]{:S(2)}) collective-permute-start(f32[11,64,128]{2,1,0:T(8,128)S(1)} %pad_maximum_fusion.34), channel_id=1, source_target_pairs={{1,0},{2,1},{3,2},{4,3},{5,4},{6,5},{7,6},{8,7},{9,8},{10,9},{11,1... | collective-permute-start | bytes 1081352 | tf_op jit(solution)/shard_map/ppermute | solution.py:60
  8.9 0.0 copy-done
  8.9 5.6 %collective-permute-done = f32[11,64,128]{2,1,0:T(8,128)S(1)} collective-permute-done((f32[11,64,128]{2,1,0:T(8,128)S(1)}, f32[11,64,128]{2,1,0:T(8,128)S(1)}, u32[]{:S(2)}, u32[]{:S(2)}) %collective-permute-start) | collective-permute-done | bytes 360480 | tf_op jit(solution)/shard_map/ppermute | solution.py:60
  14.6 12.2 %collective-permute-done.1 = f32[11,64,128]{2,1,0:T(8,128)S(1)} collective-permute-done((f32[11,64,128]{2,1,0:T(8,128)S(1)}, f32[11,64,128]{2,1,0:T(8,128)S(1)}, u32[]{:S(2)}, u32[]{:S(2)}) %collective-permute-start.1) | collective-permute-done | bytes 360480 | tf_op jit(solution)/shard_map/ppermute | solution.py:60
  26.8 0.1 fusion.77
  27.0 0.5 select_add_fusion.1
  27.5 0.2 pad_maximum_fusion.16
  27.8 0.5 fusion.65
  28.3 0.6 fusion.53
  28.9 0.2 maximum_add_fusion
  29.1 0.0 copy-start.1
  29.1 0.2 add_dynamic-update-slice_fusion.4
  29.3 0.2 add_dynamic-update-slice_fusion.3
  29.6 0.5 copy-done.1
  30.1 0.2 add_dynamic-update-slice_fusion.2
  30.3 0.2 add_dynamic-update-slice_fusion.1
  30.5 0.2 add_dynamic-update-slice_fusion
  30.7 0.1 slice_bitcast_fusion
  30.9 0.1 fusion.67
  30.9 0.1 slice.609
  31.0 0.1 pad_maximum_fusion.15
  31.1 0.3 fusion.71
  31.4 0.0 slice-start
  31.5 0.1 select_add_fusion.3
  31.8 0.7 slice-done
  32.5 9.0 %collective-permute-start.2 = (f32[18,64,128]{2,1,0:T(8,128)S(1)}, f32[18,64,128]{2,1,0:T(8,128)S(1)}, u32[]{:S(2)}, u32[]{:S(2)}) collective-permute-start(f32[18,64,128]{2,1,0:T(8,128)S(1)} %pad_maximum_fusion.23), channel_id=1, source_target_pairs={{0,16},{16,32},{32,48},{48,64},{64,80},{80,96},{96,112},{112,128},... | collective-permute-start | bytes 1769480 | tf_op jit(solution)/shard_map/ppermute | solution.py:162
  41.6 1.2 %subtract_multiply_fusion = (f32[5,1,6,64,128]{4,3,2,0,1:T(8,128)S(1)}, f32[5,1,6,64,128]{4,3,2,0,1:T(8,128)S(1)}, f32[5,1,6,64,128]{4,3,2,0,1:T(8,128)S(1)}) fusion(f32[5,4,8,64,128]{4,3,2,0,1:T(8,128)S(1)} %add_dynamic-update-slice_fusion, f32[6,64,128]{2,1,0:T(8,128)S(1)} %slice.628), kind=kLoop, calls=%fused_computation.46 | loop fusion | flops 6635520 | bytes 7077888 | tf_op jit(solution)/shard_map/div | solution.py:96
  42.7 2.1 %fusion.4 = f32[5,6,64,128]{3,2,1,0:T(8,128)S(1)} fusion(f32[5,6,64,1]{3,2,1,0:T(8,128)S(1)} %get-tuple-element.52, f32[5,1,64,128]{3,2,1,0:T(8,128)S(1)} %get-tuple-element.34, f32[5,4,64,128]{3,2,1,0:T(8,128)S(1)} %slice.609, f32[5,1,64,128]{3,2,1,0:T(8,128)S(1)} %get-tuple-element.35, f32[5,6,64,1]{3,2,1,0:T(8,128)S(1)} %get-tuple-element.51, ...), kind=kLoop, calls=%fused_computation.16 | loop fusion | flops 10813440 | bytes 7255040 | tf_op jit(solution)/shard_map/sub | solution.py:95
  44.8 8.0 %collective-permute-done.2 = f32[18,64,128]{2,1,0:T(8,128)S(1)} collective-permute-done((f32[18,64,128]{2,1,0:T(8,128)S(1)}, f32[18,64,128]{2,1,0:T(8,128)S(1)}, u32[]{:S(2)}, u32[]{:S(2)}) %collective-permute-start.2) | collective-permute-done | bytes 589856 | tf_op jit(solution)/shard_map/ppermute | solution.py:162
  52.9 0.4 fusion.45
  53.4 0.3 bitcast_dynamic-update-slice_fusion.4
  53.7 0.1 bitcast_dynamic-update-slice_fusion.9
  53.8 0.1 bitcast_dynamic-update-slice_fusion.8
  53.9 0.1 bitcast_dynamic-update-slice_fusion.7
  54.0 0.1 bitcast_dynamic-update-slice_fusion.6
  54.1 0.1 bitcast_dynamic-update-slice_fusion.5
  54.2 0.2 fusion.69
  54.5 0.2 bitcast_dynamic-update-slice_fusion.3
  54.7 0.2 bitcast_dynamic-update-slice_fusion.2
  55.0 0.2 bitcast_dynamic-update-slice_fusion.1
  55.2 0.2 bitcast_dynamic-update-slice_fusion
  55.5 8.4 %collective-permute-start.3 = (f32[4,4,64,128]{3,2,1,0:T(8,128)S(1)}, f32[4,4,64,128]{3,2,1,0:T(8,128)S(1)}, u32[]{:S(2)}, u32[]{:S(2)}) collective-permute-start(f32[4,4,64,128]{3,2,1,0:T(8,128)S(1)} %get-tuple-element.5), channel_id=1, source_target_pairs={{0,16},{16,32},{32,48},{48,64},{64,80},{80,96},{96,112},{112,128},... | collective-permute-start | bytes 1572872 | tf_op jit(solution)/shard_map/ppermute | solution.py:174
  63.9 0.8 %multiply_bitcast_fusion = (f32[5,1,4,64,128]{4,3,2,0,1:T(8,128)S(1)}, f32[5,1,4,64,128]{4,3,2,0,1:T(8,128)S(1)}, f32[5,1,4,64,128]{4,3,2,0,1:T(8,128)S(1)}, f32[5,4,64,128]{3,2,1,0:T(8,128)S(1)}) fusion(f32[5,3,4,64,128]{4,3,2,1,0:T(8,128)S(1)} %bitcast_dynamic-update-slice_fusion, f32[5,6,64,128]{3,2,1,0:T(8,128)S(1)} %bitcast_dynamic-update-slice_fusion.5, ...), kind=kLoop, calls=%fused_computation.76 | loop fusion | flops 4423680 | bytes 5373952 | tf_op jit(solution)/shard_map/stack | solution.py:101
  64.7 0.9 %fusion.20 = f32[5,1,4,64,128]{4,3,2,0,1:T(8,128)S(1)} fusion(f32[5,4,64,128]{3,2,1,0:T(8,128)S(1)} %get-tuple-element.48, f32[5,4,64,1]{3,2,1,0:T(8,128)S(1)} %get-tuple-element.47, f32[5,4,64,1]{3,2,1,0:T(8,128)S(1)} %get-tuple-element.46, f32[5,4,1,128]{3,2,1,0:T(1,128)S(1)} %get-tuple-element.45, f32[5,4,1,128]{3,2,1,0:T(1,128)S(1)} %get-tuple-element.44, ...), kind=kLoop, calls=%fused_computation.53 | loop fusion | flops 5242880 | bytes 4290560 | tf_op jit(solution)/shard_map/stack | solution.py:101
  65.5 0.2 pad_maximum_fusion
  65.7 9.9 %collective-permute-done.3 = f32[4,4,64,128]{3,2,1,0:T(8,128)S(1)} collective-permute-done((f32[4,4,64,128]{3,2,1,0:T(8,128)S(1)}, f32[4,4,64,128]{3,2,1,0:T(8,128)S(1)}, u32[]{:S(2)}, u32[]{:S(2)}) %collective-permute-start.3) | collective-permute-done | bytes 524320 | tf_op jit(solution)/shard_map/ppermute | solution.py:174
  75.6 1.2 %fusion.36 = f32[1,4,4,64,128]{4,3,2,1,0:T(8,128)} fusion(f32[5,4,4,64,128]{4,3,2,0,1:T(8,128)S(1)} %pad_maximum_fusion, f32[4,4,64,128]{3,2,1,0:T(8,128)S(1)} %collective-permute-done.3, pred[]{:T(512)S(6)} %eq.40, f32[1,4,4,64,128]{4,3,2,1,0:T(8,128)S(1)} %copy-done), kind=kLoop, calls=%fused_computation.84 | loop fusion | flops 1572864 | bytes 4194305 | tf_op jit(solution)/shard_map/broadcast_in_dim | solution.py:183
  (37 shorter events, 0.6 us)
Async XLA Ops:
  0.0 8.9 %copy-start = (f32[1,4,4,64,128]{4,3,2,1,0:T(8,128)S(1)}, f32[1,4,4,64,128]{4,3,2,1,0:T(8,128)}, u32[]{:S(2)}) copy-start(f32[1,4,4,64,128]{4,3,2,1,0:T(8,128)} %param.3) | copy-start | bytes 1572868
  3.1 11.4 %collective-permute-start = (f32[11,64,128]{2,1,0:T(8,128)S(1)}, f32[11,64,128]{2,1,0:T(8,128)S(1)}, u32[]{:S(2)}, u32[]{:S(2)}) collective-permute-start(f32[11,64,128]{2,1,0:T(8,128)S(1)} %pad_maximum_fusion.33), channel_id=1, source_target_pairs={{0,1},{1,2},{2,3},{3,4},{4,5},{5,6},{6,7},{7,8},{8,9},{9,10},{10,1... | collective-permute-start | bytes 1081352 | tf_op jit(solution)/shard_map/ppermute | solution.py:60
  7.6 19.2 %collective-permute-start.1 = (f32[11,64,128]{2,1,0:T(8,128)S(1)}, f32[11,64,128]{2,1,0:T(8,128)S(1)}, u32[]{:S(2)}, u32[]{:S(2)}) collective-permute-start(f32[11,64,128]{2,1,0:T(8,128)S(1)} %pad_maximum_fusion.34), channel_id=1, source_target_pairs={{1,0},{2,1},{3,2},{4,3},{5,4},{6,5},{7,6},{8,7},{9,8},{10,9},{11,1... | collective-permute-start | bytes 1081352 | tf_op jit(solution)/shard_map/ppermute | solution.py:60
  29.1 1.0 %copy-start.1 = (f32[4,8,64,128]{3,2,1,0:T(8,128)}, f32[4,8,64,128]{3,2,1,0:T(8,128)S(1)}, u32[]{:S(2)}) copy-start(f32[4,8,64,128]{3,2,1,0:T(8,128)S(1)} %maximum_add_fusion) | copy-start | bytes 3145732
  31.4 1.0 %slice-start = ((f32[4,8,64,128]{3,2,1,0:T(8,128)}), f32[4,4,64,128]{3,2,1,0:T(8,128)S(1)}, s32[]{:S(2)}) async-start(f32[4,8,64,128]{3,2,1,0:T(8,128)} %copy-done.1), calls=%async_computation | async-start | bytes 1048576 | tf_op jit(solution)/shard_map/slice | solution.py:113
  32.5 20.3 %collective-permute-start.2 = (f32[18,64,128]{2,1,0:T(8,128)S(1)}, f32[18,64,128]{2,1,0:T(8,128)S(1)}, u32[]{:S(2)}, u32[]{:S(2)}) collective-permute-start(f32[18,64,128]{2,1,0:T(8,128)S(1)} %pad_maximum_fusion.23), channel_id=1, source_target_pairs={{0,16},{16,32},{32,48},{48,64},{64,80},{80,96},{96,112},{112,128},... | collective-permute-start | bytes 1769480 | tf_op jit(solution)/shard_map/ppermute | solution.py:162
  55.5 20.1 %collective-permute-start.3 = (f32[4,4,64,128]{3,2,1,0:T(8,128)S(1)}, f32[4,4,64,128]{3,2,1,0:T(8,128)S(1)}, u32[]{:S(2)}, u32[]{:S(2)}) collective-permute-start(f32[4,4,64,128]{3,2,1,0:T(8,128)S(1)} %get-tuple-element.5), channel_id=1, source_target_pairs={{0,16},{16,32},{32,48},{48,64},{64,80},{80,96},{96,112},{112,128},... | collective-permute-start | bytes 1572872 | tf_op jit(solution)/shard_map/ppermute | solution.py:174

commit v4 on v1

--- a/solution.py
+++ b/solution.py
@@ -2,8 +2,6 @@
 import jax.numpy as jnp
 from jax import lax
 from jax.sharding import PartitionSpec as P
-
-ITERS = 3
 
 
 radau_nodes = [0.05710419611451768, 0.2768430136381238, 0.5835904323689168, 0.8602401356562195, 1.0]
@@ -101,7 +99,7 @@
     return start + slice_len * total
 
 
-def shards(guess, fibre, labels):
+def steps(guess, fibre, labels):
     table = radau_table()
     sums = [sum(row) for row in table]
     fast_g = lookup(labels, [4.0, 3.0, 3.5, 1.0])
@@ -153,7 +151,7 @@
 def solution(mesh):
     placed = (P("tm", None, "space", None, None), P("space", None, None), P("space", None, None))
     return jax.shard_map(
-        shards,
+        steps,
         mesh=mesh,
         in_specs=placed,
         out_specs=P("tm", None, "space", None, None),

time: 72.3 us -> 72.3 us (level)
  no operation moved by 1% of the time
where the time goes in v4:
time: 72.3 us; the launch traced here: 71.9 us
  starting transfers between devices  39.6 us (55%)
  waiting for transfers between devices  19.6 us (27%)
  other arithmetic  10.9 us (15%)
  local copies, waits for them, and re-layouts  1.51 us (2%)
    ppermute x6, starting transfers between devices, shift_space(): return lax.ppermute(block, 'space', pairs)  23.2 us
    ppermute x6, waiting for transfers between devices, shift_space(): return lax.ppermute(block, 'space', pairs)  16.2 us
    ppermute x1, starting transfers between devices, steps(): arrived2 = lax.ppermute(ends1, 'tm', tm_pairs)  8.4 us
    ppermute x1, starting transfers between devices, steps(): arrived1 = lax.ppermute(ends0, 'tm', tm_pairs)  7.93 us
    ppermute x1, waiting for transfers between devices, steps(): arrived1 = lax.ppermute(ends0, 'tm', tm_pairs)  3.36 us
    another operation x4, other arithmetic, rates(): return jnp.stack([dvolt, dact, dinact, dslow], axis=-4)  2.09 us
    div x2, other arithmetic, rates(): dact = (jax.nn.sigmoid(8.0 * (volt - 0.2)) - act) / 0.5  1.78 us
    unnamed x15, other arithmetic  1.78 us
  transfers between devices with their start and end apart: 8, of which 3 were waited for; matrix products, arithmetic and copies ran while one was open for 10% of the time, Pallas kernels for 0%

profile of v4, /device:TPU:27, one launch (start us, length us, event | category | flops | bytes accessed | tf_op | source)
XLA Modules:
  0.0 71.9 jit_solution(17840074493558761834)
XLA Ops:
  0.0 0.0 copy-start
  0.0 0.0 copy-start.1
  0.0 0.8 %slice_bitcast_fusion.3 = (f32[1,64,128]{2,1,0:T(8,128)S(1)}, f32[1,64,128]{2,1,0:T(8,128)S(1)}) fusion(f32[1,4,4,64,128]{4,3,2,1,0:T(8,128)} %param.3), kind=kLoop, calls=%fused_computation.175 | loop fusion | bytes 131072 | tf_op jit(solution)/shard_map/slice | solution.py:121
  0.9 6.2 %collective-permute-start = (f32[1,64,128]{2,1,0:T(8,128)S(1)}, f32[1,64,128]{2,1,0:T(8,128)S(1)}, u32[]{:S(2)}, u32[]{:S(2)}) collective-permute-start(f32[1,64,128]{2,1,0:T(8,128)S(1)} %get-tuple-element.41), channel_id=1, source_target_pairs={{1,0},{2,1},{3,2},{4,3},{5,4},{6,5},{7,6},{8,7},{9,8},{10,9},{11,1... | collective-permute-start | bytes 98312 | tf_op jit(solution)/shard_map/ppermute | solution.py:58
  7.1 1.9 %collective-permute-start.1 = (f32[1,64,128]{2,1,0:T(8,128)S(1)}, f32[1,64,128]{2,1,0:T(8,128)S(1)}, u32[]{:S(2)}, u32[]{:S(2)}) collective-permute-start(f32[1,64,128]{2,1,0:T(8,128)S(1)} %get-tuple-element.42), channel_id=1, source_target_pairs={{0,1},{1,2},{2,3},{3,4},{4,5},{5,6},{6,7},{7,8},{8,9},{9,10},{10,1... | collective-permute-start | bytes 98312 | tf_op jit(solution)/shard_map/ppermute | solution.py:58
  9.0 1.2 %fusion.85 = (f32[1,4,64,128]{3,2,1,0:T(8,128)S(1)}, f32[1,1,4,64,128]{4,3,2,0,1:T(8,128)S(1)}, f32[1,1,4,64,128]{4,3,2,1,0:T(8,128)S(1)}, f32[4,64,128]{2,1,0:T(8,128)S(1)}) fusion(f32[1,4,4,64,128]{4,3,2,1,0:T(8,128)} %param.3), kind=kLoop, calls=%fused_computation.180 | loop fusion | flops 655360 | bytes 917504 | tf_op jit(solution)/shard_map/div | solution.py:87
  10.2 1.0 %select_add_fusion.1 = (f32[4,64,128]{2,1,0:T(8,128)S(1)}, pred[4,64,128]{2,1,0:T(8,128)(4,1)S(1)}, pred[4,64,128]{2,1,0:T(8,128)(4,1)S(1)}, pred[4,64,128]{2,1,0:T(8,128)(4,1)S(1)}, pred[4,64,128]{2,1,0:T(8,128)(4,1)S(1)}) fusion(s32[4,64,128]{2,1,0:T(8,128)} %param.5), kind=kLoop, calls=%fused_computation.154 | loop fusion | flops 360448 | bytes 393216 | tf_op jit(solution)/shard_map/add | solution.py:34
  11.2 1.0 %select_add_fusion.4 = (f32[4,64,128]{2,1,0:T(8,128)S(1)}, f32[4,64,128]{2,1,0:T(8,128)S(1)}, f32[4,64,128]{2,1,0:T(8,128)S(1)}) fusion(s32[4,64,128]{2,1,0:T(8,128)} %param.4), kind=kLoop, calls=%fused_computation.157 | loop fusion | flops 294912 | bytes 524288 | tf_op jit(solution)/shard_map/add | solution.py:108
  12.2 0.1 fusion.93
  12.2 0.0 copy-done
  12.3 0.2 select_add_fusion
  12.4 0.0 collective-permute-done
  12.5 2.0 %collective-permute-done.1 = f32[1,64,128]{2,1,0:T(8,128)S(1)} collective-permute-done((f32[1,64,128]{2,1,0:T(8,128)S(1)}, f32[1,64,128]{2,1,0:T(8,128)S(1)}, u32[]{:S(2)}, u32[]{:S(2)}) %collective-permute-start.1) | collective-permute-done | bytes 32800 | tf_op jit(solution)/shard_map/ppermute | solution.py:58
  14.4 0.0 copy-done.1
  14.5 0.3 fusion.71
  14.8 4.1 %collective-permute-start.3 = (f32[1,64,128]{2,1,0:T(8,128)S(1)}, f32[1,64,128]{2,1,0:T(8,128)S(1)}, u32[]{:S(2)}, u32[]{:S(2)}) collective-permute-start(f32[1,64,128]{2,1,0:T(8,128)S(1)} %get-tuple-element.49), channel_id=1, source_target_pairs={{1,0},{2,1},{3,2},{4,3},{5,4},{6,5},{7,6},{8,7},{9,8},{10,9},{11,1... | collective-permute-start | bytes 98312 | tf_op jit(solution)/shard_map/ppermute | solution.py:58
  18.9 1.9 %collective-permute-start.4 = (f32[1,64,128]{2,1,0:T(8,128)S(1)}, f32[1,64,128]{2,1,0:T(8,128)S(1)}, u32[]{:S(2)}, u32[]{:S(2)}) collective-permute-start(f32[1,64,128]{2,1,0:T(8,128)S(1)} %get-tuple-element.50), channel_id=1, source_target_pairs={{0,1},{1,2},{2,3},{3,4},{4,5},{5,6},{6,7},{7,8},{8,9},{9,10},{10,1... | collective-permute-start | bytes 98312 | tf_op jit(solution)/shard_map/ppermute | solution.py:58
  20.8 0.1 fusion.60
  20.9 7.9 %collective-permute-start.2 = (f32[4,4,64,128]{3,2,1,0:T(8,128)S(1)}, f32[4,4,64,128]{3,2,1,0:T(8,128)S(1)}, u32[]{:S(2)}, u32[]{:S(2)}) collective-permute-start(f32[4,4,64,128]{3,2,1,0:T(8,128)S(1)} %fusion.60), channel_id=1, source_target_pairs={{0,16},{16,32},{32,48},{48,64},{64,80},{80,96},{96,112},{112,128},... | collective-permute-start | bytes 1572872 | tf_op jit(solution)/shard_map/ppermute | solution.py:125
  28.8 0.1 fusion.63
  28.9 0.1 fusion.64
  29.0 0.1 fusion.65
  29.1 0.1 fusion.66
  29.1 0.1 fusion.62
  29.2 0.6 slice_bitcast_fusion.1
  29.8 0.2 fusion.50
  30.0 0.2 fusion.90
  30.3 0.0 collective-permute-done.3
  30.3 0.0 collective-permute-done.4
  30.5 0.9 %fusion.5 = f32[5,1,4,64,128]{4,3,2,1,0:T(8,128)S(1)} fusion(f32[5,4,64,128]{3,2,1,0:T(8,128)S(1)} %get-tuple-element.18, f32[5,4,64,1]{3,2,1,0:T(8,128)S(1)} %get-tuple-element.34, f32[5,4,64,1]{3,2,1,0:T(8,128)S(1)} %get-tuple-element.33, f32[5,4,1,128]{3,2,1,0:T(1,128)S(1)} %get-tuple-element.32, f32[5,4,1,128]{3,2,1,0:T(1,128)S(1)} %get-tuple-element.31, ...), kind=kLoop, calls=%fused_computation.9 | loop fusion | flops 5242880 | bytes 4290560 | tf_op jit(solution)/shard_map/stack | solution.py:92
  31.4 0.2 pad_maximum_fusion
  31.6 3.4 %collective-permute-done.2 = f32[4,4,64,128]{3,2,1,0:T(8,128)S(1)} collective-permute-done((f32[4,4,64,128]{3,2,1,0:T(8,128)S(1)}, f32[4,4,64,128]{3,2,1,0:T(8,128)S(1)}, u32[]{:S(2)}, u32[]{:S(2)}) %collective-permute-start.2) | collective-permute-done | bytes 524320 | tf_op jit(solution)/shard_map/ppermute | solution.py:125
  34.9 0.4 bitcast_dynamic-update-slice_fusion.4
  35.4 0.3 bitcast_dynamic-update-slice_fusion.3
  35.7 0.3 bitcast_dynamic-update-slice_fusion.2
  36.0 0.3 bitcast_dynamic-update-slice_fusion.1
  36.4 0.3 bitcast_dynamic-update-slice_fusion
  36.7 0.2 slice_bitcast_fusion
  37.0 0.2 fusion.88
  37.3 0.6 fusion.35
  37.9 8.4 %collective-permute-start.5 = (f32[4,4,64,128]{3,2,1,0:T(8,128)S(1)}, f32[4,4,64,128]{3,2,1,0:T(8,128)S(1)}, u32[]{:S(2)}, u32[]{:S(2)}) collective-permute-start(f32[4,4,64,128]{3,2,1,0:T(8,128)S(1)} %get-tuple-element.6), channel_id=1, source_target_pairs={{0,16},{16,32},{32,48},{48,64},{64,80},{80,96},{96,112},{112,128},... | collective-permute-start | bytes 1572872 | tf_op jit(solution)/shard_map/ppermute | solution.py:138
  46.3 5.8 %collective-permute-start.6 = (f32[5,1,64,128]{3,2,1,0:T(8,128)S(1)}, f32[5,1,64,128]{3,2,1,0:T(8,128)S(1)}, u32[]{:S(2)}, u32[]{:S(2)}) collective-permute-start(f32[5,1,64,128]{3,2,1,0:T(8,128)S(1)} %get-tuple-element.23), channel_id=1, source_target_pairs={{1,0},{2,1},{3,2},{4,3},{5,4},{6,5},{7,6},{8,7},{9,8},{10,9},{11,1... | collective-permute-start | bytes 491528 | tf_op jit(solution)/shard_map/ppermute | solution.py:58
  52.1 3.2 %collective-permute-start.7 = (f32[5,1,64,128]{3,2,1,0:T(8,128)S(1)}, f32[5,1,64,128]{3,2,1,0:T(8,128)S(1)}, u32[]{:S(2)}, u32[]{:S(2)}) collective-permute-start(f32[5,1,64,128]{3,2,1,0:T(8,128)S(1)} %get-tuple-element.24), channel_id=1, source_target_pairs={{0,1},{1,2},{2,3},{3,4},{4,5},{5,6},{6,7},{7,8},{8,9},{9,10},{10,1... | collective-permute-start | bytes 491528 | tf_op jit(solution)/shard_map/ppermute | solution.py:58
  55.4 14.2 %collective-permute-done.6 = f32[5,1,64,128]{3,2,1,0:T(8,128)S(1)} collective-permute-done((f32[5,1,64,128]{3,2,1,0:T(8,128)S(1)}, f32[5,1,64,128]{3,2,1,0:T(8,128)S(1)}, u32[]{:S(2)}, u32[]{:S(2)}) %collective-permute-start.6) | collective-permute-done | bytes 163872 | tf_op jit(solution)/shard_map/ppermute | solution.py:58
  69.6 0.0 collective-permute-done.7
  69.7 0.9 %fusion.11 = f32[5,1,4,64,128]{4,3,2,1,0:T(8,128)S(1)} fusion(f32[5,4,64,128]{3,2,1,0:T(8,128)S(1)} %get-tuple-element.14, f32[5,4,64,1]{3,2,1,0:T(8,128)S(1)} %get-tuple-element.28, f32[5,4,64,1]{3,2,1,0:T(8,128)S(1)} %get-tuple-element.27, f32[5,4,1,128]{3,2,1,0:T(1,128)S(1)} %get-tuple-element.26, f32[5,4,1,128]{3,2,1,0:T(1,128)S(1)} %get-tuple-element.25, ...), kind=kLoop, calls=%fused_computation.15 | loop fusion | flops 5242880 | bytes 4290560 | tf_op jit(solution)/shard_map/stack | solution.py:92
  70.5 0.2 pad_maximum_fusion.1
  70.7 0.0 collective-permute-done.5
  70.7 1.2 %fusion.56 = f32[1,4,4,64,128]{4,3,2,1,0:T(8,128)} fusion(f32[5,4,4,64,128]{4,3,2,1,0:T(8,128)S(1)} %pad_maximum_fusion.1, f32[4,4,64,128]{3,2,1,0:T(8,128)S(1)} %collective-permute-done.5, f32[1,4,4,64,128]{4,3,2,1,0:T(8,128)S(1)} %copy-done, pred[]{:T(512)S(6)} %eq.38), kind=kLoop, calls=%fused_computation.87 | loop fusion | flops 1572864 | bytes 4194305 | tf_op jit(solution)/shard_map/broadcast_in_dim | solution.py:148
  (17 shorter events, 0.2 us)
Async XLA Ops:
  0.0 12.3 %copy-start = (f32[1,4,4,64,128]{4,3,2,1,0:T(8,128)S(1)}, f32[1,4,4,64,128]{4,3,2,1,0:T(8,128)}, u32[]{:S(2)}) copy-start(f32[1,4,4,64,128]{4,3,2,1,0:T(8,128)} %param.3) | copy-start | bytes 1572868
  0.0 14.4 %copy-start.1 = (s32[4,64,128]{2,1,0:T(8,128)S(1)}, s32[4,64,128]{2,1,0:T(8,128)}, u32[]{:S(2)}) copy-start(s32[4,64,128]{2,1,0:T(8,128)} %param.4) | copy-start | bytes 393220
  0.9 11.6 %collective-permute-start = (f32[1,64,128]{2,1,0:T(8,128)S(1)}, f32[1,64,128]{2,1,0:T(8,128)S(1)}, u32[]{:S(2)}, u32[]{:S(2)}) collective-permute-start(f32[1,64,128]{2,1,0:T(8,128)S(1)} %get-tuple-element.41), channel_id=1, source_target_pairs={{1,0},{2,1},{3,2},{4,3},{5,4},{6,5},{7,6},{8,7},{9,8},{10,9},{11,1... | collective-permute-start | bytes 98312 | tf_op jit(solution)/shard_map/ppermute | solution.py:58
  7.1 7.4 %collective-permute-start.1 = (f32[1,64,128]{2,1,0:T(8,128)S(1)}, f32[1,64,128]{2,1,0:T(8,128)S(1)}, u32[]{:S(2)}, u32[]{:S(2)}) collective-permute-start(f32[1,64,128]{2,1,0:T(8,128)S(1)} %get-tuple-element.42), channel_id=1, source_target_pairs={{0,1},{1,2},{2,3},{3,4},{4,5},{5,6},{6,7},{7,8},{8,9},{9,10},{10,1... | collective-permute-start | bytes 98312 | tf_op jit(solution)/shard_map/ppermute | solution.py:58
  14.8 15.5 %collective-permute-start.3 = (f32[1,64,128]{2,1,0:T(8,128)S(1)}, f32[1,64,128]{2,1,0:T(8,128)S(1)}, u32[]{:S(2)}, u32[]{:S(2)}) collective-permute-start(f32[1,64,128]{2,1,0:T(8,128)S(1)} %get-tuple-element.49), channel_id=1, source_target_pairs={{1,0},{2,1},{3,2},{4,3},{5,4},{6,5},{7,6},{8,7},{9,8},{10,9},{11,1... | collective-permute-start | bytes 98312 | tf_op jit(solution)/shard_map/ppermute | solution.py:58
  18.9 11.4 %collective-permute-start.4 = (f32[1,64,128]{2,1,0:T(8,128)S(1)}, f32[1,64,128]{2,1,0:T(8,128)S(1)}, u32[]{:S(2)}, u32[]{:S(2)}) collective-permute-start(f32[1,64,128]{2,1,0:T(8,128)S(1)} %get-tuple-element.50), channel_id=1, source_target_pairs={{0,1},{1,2},{2,3},{3,4},{4,5},{5,6},{6,7},{7,8},{8,9},{9,10},{10,1... | collective-permute-start | bytes 98312 | tf_op jit(solution)/shard_map/ppermute | solution.py:58
  20.9 14.0 %collective-permute-start.2 = (f32[4,4,64,128]{3,2,1,0:T(8,128)S(1)}, f32[4,4,64,128]{3,2,1,0:T(8,128)S(1)}, u32[]{:S(2)}, u32[]{:S(2)}) collective-permute-start(f32[4,4,64,128]{3,2,1,0:T(8,128)S(1)} %fusion.60), channel_id=1, source_target_pairs={{0,16},{16,32},{32,48},{48,64},{64,80},{80,96},{96,112},{112,128},... | collective-permute-start | bytes 1572872 | tf_op jit(solution)/shard_map/ppermute | solution.py:125
  37.9 32.8 %collective-permute-start.5 = (f32[4,4,64,128]{3,2,1,0:T(8,128)S(1)}, f32[4,4,64,128]{3,2,1,0:T(8,128)S(1)}, u32[]{:S(2)}, u32[]{:S(2)}) collective-permute-start(f32[4,4,64,128]{3,2,1,0:T(8,128)S(1)} %get-tuple-element.6), channel_id=1, source_target_pairs={{0,16},{16,32},{32,48},{48,64},{64,80},{80,96},{96,112},{112,128},... | collective-permute-start | bytes 1572872 | tf_op jit(solution)/shard_map/ppermute | solution.py:138
  46.3 23.3 %collective-permute-start.6 = (f32[5,1,64,128]{3,2,1,0:T(8,128)S(1)}, f32[5,1,64,128]{3,2,1,0:T(8,128)S(1)}, u32[]{:S(2)}, u32[]{:S(2)}) collective-permute-start(f32[5,1,64,128]{3,2,1,0:T(8,128)S(1)} %get-tuple-element.23), channel_id=1, source_target_pairs={{1,0},{2,1},{3,2},{4,3},{5,4},{6,5},{7,6},{8,7},{9,8},{10,9},{11,1... | collective-permute-start | bytes 491528 | tf_op jit(solution)/shard_map/ppermute | solution.py:58
  52.1 17.5 %collective-permute-start.7 = (f32[5,1,64,128]{3,2,1,0:T(8,128)S(1)}, f32[5,1,64,128]{3,2,1,0:T(8,128)S(1)}, u32[]{:S(2)}, u32[]{:S(2)}) collective-permute-start(f32[5,1,64,128]{3,2,1,0:T(8,128)S(1)} %get-tuple-element.24), channel_id=1, source_target_pairs={{0,1},{1,2},{2,3},{3,4},{4,5},{5,6},{6,7},{7,8},{8,9},{9,10},{10,1... | collective-permute-start | bytes 491528 | tf_op jit(solution)/shard_map/ppermute | solution.py:58

commit v5 on v4

--- a/solution.py
+++ b/solution.py
@@ -99,6 +99,13 @@
     return start + slice_len * total
 
 
+def edge_nodes(start, derivs, weights):
+    total = weights[:, 0] * derivs[0][None]
+    for j in range(1, 5):
+        total = total + weights[:, j] * derivs[j][None]
+    return start[None] + slice_len * total
+
+
 def steps(guess, fibre, labels):
     table = radau_table()
     sums = [sum(row) for row in table]
@@ -136,10 +143,15 @@
     start1 = jnp.where(first_slice, start0, arrived1)
     ends1 = quadrature(start1, derivs1, table[4])
     arrived2 = lax.ppermute(ends1, "tm", tm_pairs)
-    nodes1 = jnp.stack([quadrature(start1, derivs1, table[m]) for m in range(4)] + [ends1])
+    weights = jnp.array(table, jnp.float32)[:, :, None, None, None]
+    top = edge_nodes(start1[0, planes - 1 :], derivs1[:, 0, planes - 1 :], weights)
+    bottom = edge_nodes(start1[0, :1], derivs1[:, 0, :1], weights)
+    low2 = shift_space(top, True)
+    high2 = shift_space(bottom, False)
+    later_start, later_derivs, ends1 = lax.optimization_barrier((start1, derivs1, ends1))
+    nodes1 = jnp.stack([quadrature(later_start, later_derivs, table[m]) for m in range(4)] + [ends1])
 
     volts2 = nodes1[:, 0]
-    low2, high2 = halos(volts2)
     low2 = jnp.where(at_low, volts2[:, :1], low2)
     high2 = jnp.where(at_high, volts2[:, planes - 1 :], high2)
     derivs2 = rates(nodes1, laplacian(volts2, low2, high2, conduct), fast_g, slow_g, slow_tau)

time: 72.3 us -> 73.6 us (1.018)
  waiting for transfers between devices: 19.6 us -> 20.5 us
    ppermute x1, waiting for transfers between devices: 3.36 us -> 4.8 us  [steps(): arrived1 = lax.ppermute(ends0, 'tm', tm_pairs)]
    sub x1 -> x2, other arithmetic: 0.31 us -> 1.17 us  [rates(): dvolt = lap - current]
    another operation x4 -> x3, other arithmetic: 2.09 us -> 1.22 us  [rates(): return jnp.stack([dvolt, dact, dinact, dslow], axis=-4)]
  transfers between devices with their start and end apart: 8 -> 8, of which waited for: 3 -> 3; matrix products, arithmetic and copies ran while one was open for 10% -> 9% of each run, Pallas kernels for 0% -> 0%
where the time goes in v5:
time: 73.6 us; the launch traced here: 73.3 us
  starting transfers between devices  39.6 us (54%)
  waiting for transfers between devices  20.5 us (28%)
  other arithmetic  11.2 us (15%)
  local copies, waits for them, and re-layouts  1.6 us (2%)
    ppermute x6, starting transfers between devices, shift_space(): return lax.ppermute(block, 'space', pairs)  23.2 us
    ppermute x6, waiting for transfers between devices, shift_space(): return lax.ppermute(block, 'space', pairs)  15.7 us
    ppermute x1, starting transfers between devices, steps(): arrived2 = lax.ppermute(ends1, 'tm', tm_pairs)  8.4 us
    ppermute x1, starting transfers between devices, steps(): arrived1 = lax.ppermute(ends0, 'tm', tm_pairs)  7.93 us
    ppermute x1, waiting for transfers between devices, steps(): arrived1 = lax.ppermute(ends0, 'tm', tm_pairs)  4.8 us
    div x2, other arithmetic, rates(): dact = (jax.nn.sigmoid(8.0 * (volt - 0.2)) - act) / 0.5  1.78 us
    unnamed x15, other arithmetic  1.73 us
  transfers between devices with their start and end apart: 8, of which 3 were waited for; matrix products, arithmetic and copies ran while one was open for 9% of the time, Pallas kernels for 0%

profile of v5, /device:TPU:27, one launch (start us, length us, event | category | flops | bytes accessed | tf_op | source)
XLA Modules:
  0.0 73.3 jit_solution(11259410002684947006)
XLA Ops:
  0.0 0.0 copy-start
  0.0 0.0 copy-start.1
  0.0 0.8 %slice_bitcast_fusion.15 = (f32[1,64,128]{2,1,0:T(8,128)S(1)}, f32[1,64,128]{2,1,0:T(8,128)S(1)}) fusion(f32[1,4,4,64,128]{4,3,2,1,0:T(8,128)} %param.4), kind=kLoop, calls=%fused_computation.199 | loop fusion | bytes 131072 | tf_op jit(solution)/shard_map/slice | solution.py:128
  0.9 6.2 %collective-permute-start = (f32[1,64,128]{2,1,0:T(8,128)S(1)}, f32[1,64,128]{2,1,0:T(8,128)S(1)}, u32[]{:S(2)}, u32[]{:S(2)}) collective-permute-start(f32[1,64,128]{2,1,0:T(8,128)S(1)} %get-tuple-element.55), channel_id=1, source_target_pairs={{1,0},{2,1},{3,2},{4,3},{5,4},{6,5},{7,6},{8,7},{9,8},{10,9},{11,1... | collective-permute-start | bytes 98312 | tf_op jit(solution)/shard_map/ppermute | solution.py:58
  7.1 1.9 %collective-permute-start.1 = (f32[1,64,128]{2,1,0:T(8,128)S(1)}, f32[1,64,128]{2,1,0:T(8,128)S(1)}, u32[]{:S(2)}, u32[]{:S(2)}) collective-permute-start(f32[1,64,128]{2,1,0:T(8,128)S(1)} %get-tuple-element.56), channel_id=1, source_target_pairs={{0,1},{1,2},{2,3},{3,4},{4,5},{5,6},{6,7},{7,8},{8,9},{9,10},{10,1... | collective-permute-start | bytes 98312 | tf_op jit(solution)/shard_map/ppermute | solution.py:58
  9.0 1.2 %fusion.91 = (f32[1,4,64,128]{3,2,1,0:T(8,128)S(1)}, f32[1,1,4,64,128]{4,3,2,0,1:T(8,128)S(1)}, f32[1,1,4,64,128]{4,3,2,1,0:T(8,128)S(1)}, f32[4,64,128]{2,1,0:T(8,128)S(1)}) fusion(f32[1,4,4,64,128]{4,3,2,1,0:T(8,128)} %param.4), kind=kLoop, calls=%fused_computation.204 | loop fusion | flops 655360 | bytes 917504 | tf_op jit(solution)/shard_map/div | solution.py:87
  10.2 0.1 fusion.98
  10.3 1.0 %select_add_fusion.1 = (f32[4,64,128]{2,1,0:T(8,128)S(1)}, pred[4,64,128]{2,1,0:T(8,128)(4,1)S(1)}, pred[4,64,128]{2,1,0:T(8,128)(4,1)S(1)}, pred[4,64,128]{2,1,0:T(8,128)(4,1)S(1)}, pred[4,64,128]{2,1,0:T(8,128)(4,1)S(1)}) fusion(s32[4,64,128]{2,1,0:T(8,128)} %param.6), kind=kLoop, calls=%fused_computation.168 | loop fusion | flops 360448 | bytes 393216 | tf_op jit(solution)/shard_map/add | solution.py:34
  11.3 1.0 %select_add_fusion.4 = (f32[4,64,128]{2,1,0:T(8,128)S(1)}, f32[4,64,128]{2,1,0:T(8,128)S(1)}, f32[4,64,128]{2,1,0:T(8,128)S(1)}) fusion(s32[4,64,128]{2,1,0:T(8,128)} %param.5), kind=kLoop, calls=%fused_computation.171 | loop fusion | flops 294912 | bytes 524288 | tf_op jit(solution)/shard_map/add | solution.py:115
  12.3 0.0 copy-done
  12.3 0.2 select_add_fusion
  12.4 0.0 collective-permute-done
  12.5 2.0 %collective-permute-done.1 = f32[1,64,128]{2,1,0:T(8,128)S(1)} collective-permute-done((f32[1,64,128]{2,1,0:T(8,128)S(1)}, f32[1,64,128]{2,1,0:T(8,128)S(1)}, u32[]{:S(2)}, u32[]{:S(2)}) %collective-permute-start.1) | collective-permute-done | bytes 32800 | tf_op jit(solution)/shard_map/ppermute | solution.py:58
  14.4 0.0 copy-done.1
  14.5 0.3 fusion.77
  14.8 0.1 fusion.69
  14.9 0.1 fusion.70
  14.9 0.1 fusion.71
  15.0 0.1 fusion.72
  15.1 0.1 fusion.68
  15.2 0.6 slice_bitcast_fusion.1
  15.8 4.1 %collective-permute-start.3 = (f32[1,64,128]{2,1,0:T(8,128)S(1)}, f32[1,64,128]{2,1,0:T(8,128)S(1)}, u32[]{:S(2)}, u32[]{:S(2)}) collective-permute-start(f32[1,64,128]{2,1,0:T(8,128)S(1)} %get-tuple-element.63), channel_id=1, source_target_pairs={{1,0},{2,1},{3,2},{4,3},{5,4},{6,5},{7,6},{8,7},{9,8},{10,9},{11,1... | collective-permute-start | bytes 98312 | tf_op jit(solution)/shard_map/ppermute | solution.py:58
  19.9 1.9 %collective-permute-start.4 = (f32[1,64,128]{2,1,0:T(8,128)S(1)}, f32[1,64,128]{2,1,0:T(8,128)S(1)}, u32[]{:S(2)}, u32[]{:S(2)}) collective-permute-start(f32[1,64,128]{2,1,0:T(8,128)S(1)} %get-tuple-element.64), channel_id=1, source_target_pairs={{0,1},{1,2},{2,3},{3,4},{4,5},{5,6},{6,7},{7,8},{8,9},{9,10},{10,1... | collective-permute-start | bytes 98312 | tf_op jit(solution)/shard_map/ppermute | solution.py:58
  21.8 0.2 fusion.95
  22.1 0.2 fusion.49
  22.3 0.1 fusion.66
  22.4 7.9 %collective-permute-start.2 = (f32[4,4,64,128]{3,2,1,0:T(8,128)S(1)}, f32[4,4,64,128]{3,2,1,0:T(8,128)S(1)}, u32[]{:S(2)}, u32[]{:S(2)}) collective-permute-start(f32[4,4,64,128]{3,2,1,0:T(8,128)S(1)} %fusion.66), channel_id=1, source_target_pairs={{0,16},{16,32},{32,48},{48,64},{64,80},{80,96},{96,112},{112,128},... | collective-permute-start | bytes 1572872 | tf_op jit(solution)/shard_map/ppermute | solution.py:132
  30.3 0.0 collective-permute-done.3
  30.3 0.0 collective-permute-done.4
  30.5 0.9 %fusion.4 = f32[5,4,64,128]{3,2,1,0:T(8,128)S(1)} fusion(f32[5,4,64,128]{3,2,1,0:T(8,128)S(1)} %get-tuple-element.22, f32[5,4,64,1]{3,2,1,0:T(8,128)S(1)} %get-tuple-element.46, f32[5,4,64,1]{3,2,1,0:T(8,128)S(1)} %get-tuple-element.45, f32[5,4,1,128]{3,2,1,0:T(1,128)S(1)} %get-tuple-element.44, f32[5,4,1,128]{3,2,1,0:T(1,128)S(1)} %get-tuple-element.43, ...), kind=kLoop, calls=%fused_computation.8 | loop fusion | flops 5242880 | bytes 4290560 | tf_op jit(solution)/shard_map/sub | solution.py:86
  31.4 0.2 pad_maximum_fusion
  31.6 4.8 %collective-permute-done.2 = f32[4,4,64,128]{3,2,1,0:T(8,128)S(1)} collective-permute-done((f32[4,4,64,128]{3,2,1,0:T(8,128)S(1)}, f32[4,4,64,128]{3,2,1,0:T(8,128)S(1)}, u32[]{:S(2)}, u32[]{:S(2)}) %collective-permute-start.2) | collective-permute-done | bytes 524320 | tf_op jit(solution)/shard_map/ppermute | solution.py:132
  36.4 0.4 fusion.62
  36.9 0.3 bitcast_dynamic-update-slice_fusion.4
  37.2 0.3 bitcast_dynamic-update-slice_fusion.3
  37.6 0.3 bitcast_dynamic-update-slice_fusion.2
  37.9 0.3 bitcast_dynamic-update-slice_fusion.1
  38.3 0.0 copy-start.2
  38.3 0.0 copy-start.3
  38.3 0.0 copy-start.4
  38.3 0.0 copy-start.5
  38.3 0.0 copy-start.6
  38.4 0.2 slice_bitcast_fusion
  38.6 0.6 fusion.34
  39.2 8.4 %collective-permute-start.5 = (f32[4,4,64,128]{3,2,1,0:T(8,128)S(1)}, f32[4,4,64,128]{3,2,1,0:T(8,128)S(1)}, u32[]{:S(2)}, u32[]{:S(2)}) collective-permute-start(f32[4,4,64,128]{3,2,1,0:T(8,128)S(1)} %get-tuple-element.10), channel_id=1, source_target_pairs={{0,16},{16,32},{32,48},{48,64},{64,80},{80,96},{96,112},{112,128},... | collective-permute-start | bytes 1572872 | tf_op jit(solution)/shard_map/ppermute | solution.py:145
  47.6 0.0 copy-done.2
  47.6 0.0 copy-done.3
  47.6 0.0 copy-done.4
  47.6 0.0 copy-done.5
  47.7 0.0 copy-done.6
  47.7 0.2 multiply_add_fusion.1
  47.9 5.8 %collective-permute-start.6 = (f32[5,1,64,128]{3,2,1,0:T(8,128)S(1)}, f32[5,1,64,128]{3,2,1,0:T(8,128)S(1)}, u32[]{:S(2)}, u32[]{:S(2)}) collective-permute-start(f32[5,1,64,128]{3,2,1,0:T(8,128)S(1)} %get-tuple-element.69), channel_id=1, source_target_pairs={{1,0},{2,1},{3,2},{4,3},{5,4},{6,5},{7,6},{8,7},{9,8},{10,9},{11,1... | collective-permute-start | bytes 491528 | tf_op jit(solution)/shard_map/ppermute | solution.py:58
  53.7 3.2 %collective-permute-start.7 = (f32[5,1,64,128]{3,2,1,0:T(8,128)S(1)}, f32[5,1,64,128]{3,2,1,0:T(8,128)S(1)}, u32[]{:S(2)}, u32[]{:S(2)}) collective-permute-start(f32[5,1,64,128]{3,2,1,0:T(8,128)S(1)} %get-tuple-element.70), channel_id=1, source_target_pairs={{0,1},{1,2},{2,3},{3,4},{4,5},{5,6},{6,7},{7,8},{8,9},{9,10},{10,1... | collective-permute-start | bytes 491528 | tf_op jit(solution)/shard_map/ppermute | solution.py:58
  57.0 0.2 fusion.93
  57.3 13.7 %collective-permute-done.6 = f32[5,1,64,128]{3,2,1,0:T(8,128)S(1)} collective-permute-done((f32[5,1,64,128]{3,2,1,0:T(8,128)S(1)}, f32[5,1,64,128]{3,2,1,0:T(8,128)S(1)}, u32[]{:S(2)}, u32[]{:S(2)}) %collective-permute-start.6) | collective-permute-done | bytes 163872 | tf_op jit(solution)/shard_map/ppermute | solution.py:58
  71.0 0.0 collective-permute-done.7
  71.0 0.9 %fusion.10 = f32[5,1,4,64,128]{4,3,2,1,0:T(8,128)S(1)} fusion(f32[5,4,64,128]{3,2,1,0:T(8,128)S(1)} %get-tuple-element.18, f32[5,4,64,1]{3,2,1,0:T(8,128)S(1)} %get-tuple-element.40, f32[5,4,64,1]{3,2,1,0:T(8,128)S(1)} %get-tuple-element.39, f32[5,4,1,128]{3,2,1,0:T(1,128)S(1)} %get-tuple-element.38, f32[5,4,1,128]{3,2,1,0:T(1,128)S(1)} %get-tuple-element.37, ...), kind=kLoop, calls=%fused_computation.14 | loop fusion | flops 5242880 | bytes 4290560 | tf_op jit(solution)/shard_map/stack | solution.py:92
  71.9 0.2 pad_maximum_fusion.1
  72.1 0.0 collective-permute-done.5
  72.1 1.2 %fusion.55 = f32[1,4,4,64,128]{4,3,2,1,0:T(8,128)} fusion(f32[5,4,4,64,128]{4,3,2,1,0:T(8,128)S(1)} %pad_maximum_fusion.1, f32[4,4,64,128]{3,2,1,0:T(8,128)S(1)} %collective-permute-done.5, f32[1,4,4,64,128]{4,3,2,1,0:T(8,128)S(1)} %copy-done, pred[]{:T(512)S(6)} %eq.38), kind=kLoop, calls=%fused_computation.86 | loop fusion | flops 1572864 | bytes 4194305 | tf_op jit(solution)/shard_map/broadcast_in_dim | solution.py:160
  (19 shorter events, 0.3 us)
Async XLA Ops:
  0.0 12.3 %copy-start = (f32[1,4,4,64,128]{4,3,2,1,0:T(8,128)S(1)}, f32[1,4,4,64,128]{4,3,2,1,0:T(8,128)}, u32[]{:S(2)}) copy-start(f32[1,4,4,64,128]{4,3,2,1,0:T(8,128)} %param.4) | copy-start | bytes 1572868
  0.0 14.4 %copy-start.1 = (s32[4,64,128]{2,1,0:T(8,128)S(1)}, s32[4,64,128]{2,1,0:T(8,128)}, u32[]{:S(2)}) copy-start(s32[4,64,128]{2,1,0:T(8,128)} %param.5) | copy-start | bytes 393220
  0.9 11.6 %collective-permute-start = (f32[1,64,128]{2,1,0:T(8,128)S(1)}, f32[1,64,128]{2,1,0:T(8,128)S(1)}, u32[]{:S(2)}, u32[]{:S(2)}) collective-permute-start(f32[1,64,128]{2,1,0:T(8,128)S(1)} %get-tuple-element.55), channel_id=1, source_target_pairs={{1,0},{2,1},{3,2},{4,3},{5,4},{6,5},{7,6},{8,7},{9,8},{10,9},{11,1... | collective-permute-start | bytes 98312 | tf_op jit(solution)/shard_map/ppermute | solution.py:58
  7.1 7.4 %collective-permute-start.1 = (f32[1,64,128]{2,1,0:T(8,128)S(1)}, f32[1,64,128]{2,1,0:T(8,128)S(1)}, u32[]{:S(2)}, u32[]{:S(2)}) collective-permute-start(f32[1,64,128]{2,1,0:T(8,128)S(1)} %get-tuple-element.56), channel_id=1, source_target_pairs={{0,1},{1,2},{2,3},{3,4},{4,5},{5,6},{6,7},{7,8},{8,9},{9,10},{10,1... | collective-permute-start | bytes 98312 | tf_op jit(solution)/shard_map/ppermute | solution.py:58
  15.8 14.5 %collective-permute-start.3 = (f32[1,64,128]{2,1,0:T(8,128)S(1)}, f32[1,64,128]{2,1,0:T(8,128)S(1)}, u32[]{:S(2)}, u32[]{:S(2)}) collective-permute-start(f32[1,64,128]{2,1,0:T(8,128)S(1)} %get-tuple-element.63), channel_id=1, source_target_pairs={{1,0},{2,1},{3,2},{4,3},{5,4},{6,5},{7,6},{8,7},{9,8},{10,9},{11,1... | collective-permute-start | bytes 98312 | tf_op jit(solution)/shard_map/ppermute | solution.py:58
  19.9 10.4 %collective-permute-start.4 = (f32[1,64,128]{2,1,0:T(8,128)S(1)}, f32[1,64,128]{2,1,0:T(8,128)S(1)}, u32[]{:S(2)}, u32[]{:S(2)}) collective-permute-start(f32[1,64,128]{2,1,0:T(8,128)S(1)} %get-tuple-element.64), channel_id=1, source_target_pairs={{0,1},{1,2},{2,3},{3,4},{4,5},{5,6},{6,7},{7,8},{8,9},{9,10},{10,1... | collective-permute-start | bytes 98312 | tf_op jit(solution)/shard_map/ppermute | solution.py:58
  22.4 14.0 %collective-permute-start.2 = (f32[4,4,64,128]{3,2,1,0:T(8,128)S(1)}, f32[4,4,64,128]{3,2,1,0:T(8,128)S(1)}, u32[]{:S(2)}, u32[]{:S(2)}) collective-permute-start(f32[4,4,64,128]{3,2,1,0:T(8,128)S(1)} %fusion.66), channel_id=1, source_target_pairs={{0,16},{16,32},{32,48},{48,64},{64,80},{80,96},{96,112},{112,128},... | collective-permute-start | bytes 1572872 | tf_op jit(solution)/shard_map/ppermute | solution.py:132
  38.3 9.3 %copy-start.2 = (f32[5]{0:T(128)S(1)}, f32[5]{0:T(128)}, u32[]{:S(2)}) copy-start(f32[5]{0:T(128)} %constant.178) | copy-start | bytes 64
  38.3 9.3 %copy-start.3 = (f32[5]{0:T(128)S(1)}, f32[5]{0:T(128)}, u32[]{:S(2)}) copy-start(f32[5]{0:T(128)} %constant.180) | copy-start | bytes 64
  38.3 9.3 %copy-start.4 = (f32[5]{0:T(128)S(1)}, f32[5]{0:T(128)}, u32[]{:S(2)}) copy-start(f32[5]{0:T(128)} %constant.182) | copy-start | bytes 64
  38.3 9.3 %copy-start.5 = (f32[5]{0:T(128)S(1)}, f32[5]{0:T(128)}, u32[]{:S(2)}) copy-start(f32[5]{0:T(128)} %constant.184) | copy-start | bytes 64
  38.3 9.3 %copy-start.6 = (f32[5]{0:T(128)S(1)}, f32[5]{0:T(128)}, u32[]{:S(2)}) copy-start(f32[5]{0:T(128)} %constant.186) | copy-start | bytes 64
  39.2 32.8 %collective-permute-start.5 = (f32[4,4,64,128]{3,2,1,0:T(8,128)S(1)}, f32[4,4,64,128]{3,2,1,0:T(8,128)S(1)}, u32[]{:S(2)}, u32[]{:S(2)}) collective-permute-start(f32[4,4,64,128]{3,2,1,0:T(8,128)S(1)} %get-tuple-element.10), channel_id=1, source_target_pairs={{0,16},{16,32},{32,48},{48,64},{64,80},{80,96},{96,112},{112,128},... | collective-permute-start | bytes 1572872 | tf_op jit(solution)/shard_map/ppermute | solution.py:145
  47.9 23.1 %collective-permute-start.6 = (f32[5,1,64,128]{3,2,1,0:T(8,128)S(1)}, f32[5,1,64,128]{3,2,1,0:T(8,128)S(1)}, u32[]{:S(2)}, u32[]{:S(2)}) collective-permute-start(f32[5,1,64,128]{3,2,1,0:T(8,128)S(1)} %get-tuple-element.69), channel_id=1, source_target_pairs={{1,0},{2,1},{3,2},{4,3},{5,4},{6,5},{7,6},{8,7},{9,8},{10,9},{11,1... | collective-permute-start | bytes 491528 | tf_op jit(solution)/shard_map/ppermute | solution.py:58
  53.7 17.2 %collective-permute-start.7 = (f32[5,1,64,128]{3,2,1,0:T(8,128)S(1)}, f32[5,1,64,128]{3,2,1,0:T(8,128)S(1)}, u32[]{:S(2)}, u32[]{:S(2)}) collective-permute-start(f32[5,1,64,128]{3,2,1,0:T(8,128)S(1)} %get-tuple-element.70), channel_id=1, source_target_pairs={{0,1},{1,2},{2,3},{3,4},{4,5},{5,6},{6,7},{7,8},{8,9},{9,10},{10,1... | collective-permute-start | bytes 491528 | tf_op jit(solution)/shard_map/ppermute | solution.py:58

commit v6 on v5

--- a/solution.py
+++ b/solution.py
@@ -58,19 +58,42 @@
     return lax.ppermute(block, "space", pairs)
 
 
-def halos(volts):
-    planes = volts.shape[-3]
-    low = shift_space(volts[..., planes - 1 : planes, :, :], True)
-    high = shift_space(volts[..., 0:1, :, :], False)
-    return low, high
-
-
 def laplacian(volts, low, high, conduct):
     padded = jnp.concatenate([low, volts, high], axis=-3)
     lap = conduct[0] * second(padded, volts.ndim - 3)
     lap = lap + conduct[1] * second(edge_pad(volts, volts.ndim - 2), volts.ndim - 2)
     lap = lap + conduct[2] * second(edge_pad(volts, volts.ndim - 1), volts.ndim - 1)
     return lap
+
+
+def close_edges(volts, depth, at_low, at_high):
+    size = volts.shape[-3]
+    inner_low = volts[..., depth : depth + 1, :, :]
+    inner_high = volts[..., size - depth - 1 : size - depth, :, :]
+    outer_low = jnp.where(at_low, inner_low, volts[..., depth - 1 : depth, :, :])
+    outer_high = jnp.where(at_high, inner_high, volts[..., size - depth : size - depth + 1, :, :])
+    return jnp.concatenate(
+        [volts[..., : depth - 1, :, :], outer_low, volts[..., depth : size - depth, :, :], outer_high,
+         volts[..., size - depth + 1 :, :, :]],
+        axis=-3,
+    )
+
+
+def padded_laplacian(volts, conduct):
+    x = volts.ndim - 3
+    inner = lax.slice_in_dim(volts, 1, volts.shape[x] - 1, axis=x)
+    lap = conduct[0] * second(volts, x)
+    lap = lap + conduct[1] * second(edge_pad(inner, x + 1), x + 1)
+    lap = lap + conduct[2] * second(edge_pad(inner, x + 2), x + 2)
+    return lap
+
+
+def coefficients(fibre, labels):
+    fast_g = lookup(labels, [4.0, 3.0, 3.5, 1.0])
+    slow_g = lookup(labels, [0.6, 0.9, 0.75, 0.3])
+    slow_tau = 4.0 * lookup(labels, [1.0, 1.5, 1.2, 3.0])
+    conduct = [0.2 + 0.6 * (fibre == d).astype(jnp.float32) for d in range(3)]
+    return [fast_g, slow_g, slow_tau], conduct
 
 
 def rates(states, lap, fast_g, slow_g, slow_tau):
@@ -109,10 +132,6 @@
 def steps(guess, fibre, labels):
     table = radau_table()
     sums = [sum(row) for row in table]
-    fast_g = lookup(labels, [4.0, 3.0, 3.5, 1.0])
-    slow_g = lookup(labels, [0.6, 0.9, 0.75, 0.3])
-    slow_tau = 4.0 * lookup(labels, [1.0, 1.5, 1.2, 3.0])
-    conduct = [0.2 + 0.6 * (fibre == d).astype(jnp.float32) for d in range(3)]
     place = lax.axis_index("space")
     at_low = place == 0
     at_high = place == lax.axis_size("space") - 1
@@ -124,22 +143,32 @@
     volts0 = start0[0]
     planes = volts0.shape[0]
 
-    low0, high0 = halos(volts0)
-    low0 = jnp.where(at_low, volts0[:1], low0)
-    high0 = jnp.where(at_high, volts0[planes - 1 :], high0)
-    derivs0 = rates(start0, laplacian(volts0, low0, high0, conduct), fast_g, slow_g, slow_tau)
-    ends0 = start0 + slice_len * (sums[4] * derivs0)
+    code = (labels + 4 * fibre).astype(jnp.float32)
+    top = jnp.concatenate([volts0[planes - 2 :], start0[1:, planes - 1], code[planes - 1 :]])
+    bottom = jnp.concatenate([volts0[:2], start0[1:, 0], code[:1]])
+    below = shift_space(top, True)
+    above = shift_space(bottom, False)
+    coef, conduct = coefficients(fibre, labels)
+    edge_code = jnp.concatenate([below[5:6], above[5:6]]).astype(jnp.int32)
+    edge_coef, edge_conduct = coefficients(edge_code // 4, edge_code % 4)
+    widen = lambda core, edge: jnp.concatenate([edge[:1], core, edge[1:]])
+    coef_ext = [widen(c, e) for c, e in zip(coef, edge_coef)]
+    conduct_ext = [widen(c, e) for c, e in zip(conduct, edge_conduct)]
+    fast_g, slow_g, slow_tau = coef
+
+    volts_ext = jnp.concatenate([below[:2], volts0, above[:2]])
+    gates_ext = jnp.concatenate([below[2:5][:, None], start0[1:], above[2:5][:, None]], axis=1)
+    state_ext = jnp.concatenate([volts_ext[None, 1 : planes + 3], gates_ext])
+    lap0 = padded_laplacian(close_edges(volts_ext, 2, at_low, at_high), conduct_ext)
+    derivs0 = rates(state_ext, lap0, *coef_ext)
+    ends0 = start0 + slice_len * (sums[4] * derivs0[:, 1 : planes + 1])
     arrived1 = lax.ppermute(ends0, "tm", tm_pairs)
 
-    dv = derivs0[0]
-    dlow, dhigh = halos(dv)
-    nodes0 = jnp.stack([start0 + slice_len * (sums[m] * derivs0) for m in range(5)])
-    volts1 = nodes0[:, 0]
-    low1 = jnp.stack([low0 + slice_len * (sums[m] * dlow) for m in range(5)])
-    high1 = jnp.stack([high0 + slice_len * (sums[m] * dhigh) for m in range(5)])
-    low1 = jnp.where(at_low, volts1[:, :1], low1)
-    high1 = jnp.where(at_high, volts1[:, planes - 1 :], high1)
-    derivs1 = rates(nodes0, laplacian(volts1, low1, high1, conduct), fast_g, slow_g, slow_tau)
+    state_ext, derivs0, ends0 = lax.optimization_barrier((state_ext, derivs0, ends0))
+    nodes0_ext = jnp.stack([state_ext + slice_len * (sums[m] * derivs0) for m in range(5)])
+    nodes0 = nodes0_ext[:, :, 1 : planes + 1]
+    lap1 = padded_laplacian(close_edges(nodes0_ext[:, 0], 1, at_low, at_high), conduct)
+    derivs1 = rates(nodes0, lap1, fast_g, slow_g, slow_tau)
     start1 = jnp.where(first_slice, start0, arrived1)
     ends1 = quadrature(start1, derivs1, table[4])
     arrived2 = lax.ppermute(ends1, "tm", tm_pairs)

time: 73.6 us -> 70.8 us (0.962)
  the two profiles are of different devices: /device:TPU:27 before, /device:TPU:23 now
where the time goes in v6:
time: 70.8 us; the launch traced here: 70.5 us
  starting transfers between devices  30.2 us (43%)
  waiting for transfers between devices  25.7 us (36%)
  other arithmetic  10.2 us (14%)
  local copies, waits for them, and re-layouts  3.83 us (5%)
    ppermute x4, waiting for transfers between devices, shift_space(): return lax.ppermute(block, 'space', pairs)  17.7 us
    ppermute x4, starting transfers between devices, shift_space(): return lax.ppermute(block, 'space', pairs)  14.1 us
    ppermute x1, starting transfers between devices, steps(): arrived2 = lax.ppermute(ends1, 'tm', tm_pairs)  8.34 us
    ppermute x1, waiting for transfers between devices, steps(): arrived1 = lax.ppermute(ends0, 'tm', tm_pairs)  8.03 us
    ppermute x1, starting transfers between devices, steps(): arrived1 = lax.ppermute(ends0, 'tm', tm_pairs)  7.82 us
    another operation x6, other arithmetic, rates(): return jnp.stack([dvolt, dact, dinact, dslow], axis=-4)  2 us
    unnamed x8, other arithmetic  1.86 us
  transfers between devices with their start and end apart: 6, of which 5 were waited for; matrix products, arithmetic and copies ran while one was open for 12% of the time, Pallas kernels for 0%

profile of v6, /device:TPU:23, one launch (start us, length us, event | category | flops | bytes accessed | tf_op | source)
XLA Modules:
  0.0 70.5 jit_solution(7789874218201101996)
XLA Ops:
  0.0 0.0 copy-start.1
  0.0 0.0 copy-start
  0.0 1.1 %add_convert_fusion = f32[4,64,128]{2,1,0:T(8,128)S(1)} fusion(s32[4,64,128]{2,1,0:T(8,128)} %param.6, s32[4,64,128]{2,1,0:T(8,128)} %param.5), kind=kLoop, calls=%fused_computation.185 | loop fusion | flops 98304 | bytes 393216 | tf_op jit(solution)/shard_map/convert_element_type | solution.py:146
  1.1 0.9 %slice_bitcast_fusion.12 = (f32[2,64,128]{2,1,0:T(8,128)S(1)}, f32[2,64,128]{2,1,0:T(8,128)S(1)}) fusion(f32[1,4,4,64,128]{4,3,2,1,0:T(8,128)} %param.4), kind=kLoop, calls=%fused_computation.208 | loop fusion | bytes 262144 | tf_op jit(solution)/shard_map/slice | solution.py:147
  2.0 1.0 %slice_bitcast_fusion.10 = (f32[3,64,128]{2,1,0:T(8,128)S(1)}, f32[3,64,128]{2,1,0:T(8,128)S(1)}) fusion(f32[4,4,64,128]{3,2,1,0:T(8,128)} %bitcast.248), kind=kLoop, calls=%fused_computation.189 | loop fusion | bytes 393216 | tf_op jit(solution)/shard_map/squeeze | solution.py:147
  3.0 6.5 %collective-permute-start.1 = (f32[6,64,128]{2,1,0:T(8,128)S(1)}, f32[6,64,128]{2,1,0:T(8,128)S(1)}, u32[]{:S(2)}, u32[]{:S(2)}) collective-permute-start(f32[6,64,128]{2,1,0:T(8,128)S(1)} %pad_maximum_fusion.31), channel_id=1, source_target_pairs={{1,0},{2,1},{3,2},{4,3},{5,4},{6,5},{7,6},{8,7},{9,8},{10,9},{11,1... | collective-permute-start | bytes 589832 | tf_op jit(solution)/shard_map/ppermute | solution.py:58
  9.5 1.9 %collective-permute-start = (f32[6,64,128]{2,1,0:T(8,128)S(1)}, f32[6,64,128]{2,1,0:T(8,128)S(1)}, u32[]{:S(2)}, u32[]{:S(2)}) collective-permute-start(f32[6,64,128]{2,1,0:T(8,128)S(1)} %pad_maximum_fusion.30), channel_id=1, source_target_pairs={{0,1},{1,2},{2,3},{3,4},{4,5},{5,6},{6,7},{7,8},{8,9},{9,10},{10,1... | collective-permute-start | bytes 589832 | tf_op jit(solution)/shard_map/ppermute | solution.py:58
  11.4 1.0 %slice_bitcast_fusion.2 = f32[3,4,64,128]{3,2,1,0:T(8,128)S(1)} fusion(f32[1,4,4,64,128]{4,3,2,1,0:T(8,128)} %param.4), kind=kLoop, calls=%fused_computation.125 | loop fusion | bytes 786432 | tf_op jit(solution)/shard_map/slice | solution.py:160
  12.5 0.0 copy-done.1
  12.5 0.0 copy-done.2
  12.5 0.1 select_add_fusion
  12.7 0.1 select_add_fusion.1
  12.8 0.0 copy-done
  12.8 0.3 collective-permute-done.1
  13.1 6.5 %collective-permute-done = f32[6,64,128]{2,1,0:T(8,128)S(1)} collective-permute-done((f32[6,64,128]{2,1,0:T(8,128)S(1)}, f32[6,64,128]{2,1,0:T(8,128)S(1)}, u32[]{:S(2)}, u32[]{:S(2)}) %collective-permute-start) | collective-permute-done | bytes 196640 | tf_op jit(solution)/shard_map/ppermute | solution.py:58
  19.7 0.1 fusion.93
  19.8 0.1 select_add_fusion.7
  19.9 0.1 select_add_fusion.6
  20.1 0.3 multiply_bitcast_fusion.1
  20.4 0.1 maximum_maximum_fusion
  20.5 0.3 fusion.74
  20.8 0.1 pad_maximum_fusion.2
  20.9 0.1 fusion.66
  21.0 7.8 %collective-permute-start.2 = (f32[4,4,64,128]{3,2,1,0:T(8,128)S(1)}, f32[4,4,64,128]{3,2,1,0:T(8,128)S(1)}, u32[]{:S(2)}, u32[]{:S(2)}) collective-permute-start(f32[4,4,64,128]{3,2,1,0:T(8,128)S(1)} %fusion.66), channel_id=1, source_target_pairs={{0,16},{16,32},{32,48},{48,64},{64,80},{80,96},{96,112},{112,128},... | collective-permute-start | bytes 1572872 | tf_op jit(solution)/shard_map/ppermute | solution.py:165
  28.8 0.1 bitcast_dynamic-update-slice_fusion.3
  28.9 0.1 bitcast_dynamic-update-slice_fusion.2
  29.0 0.1 bitcast_dynamic-update-slice_fusion.1
  29.2 0.1 bitcast_dynamic-update-slice_fusion
  29.3 0.1 bitcast_dynamic-update-slice_fusion.4
  29.4 0.1 slice_bitcast_fusion
  29.6 0.2 fusion.89
  29.9 0.6 multiply_bitcast_fusion
  30.5 0.9 %fusion.4 = f32[5,4,64,128]{3,2,1,0:T(8,128)S(1)} fusion(f32[5,4,64,128]{3,2,1,0:T(8,128)S(1)} %slice.591, f32[5,4,64,1]{3,2,1,0:T(8,128)S(1)} %get-tuple-element.38, f32[5,4,64,1]{3,2,1,0:T(8,128)S(1)} %get-tuple-element.37, f32[5,4,1,128]{3,2,1,0:T(1,128)S(1)} %get-tuple-element.36, f32[5,4,1,128]{3,2,1,0:T(1,128)S(1)} %get-tuple-element.35, ...), kind=kLoop, calls=%fused_computation.16 | loop fusion | flops 5242880 | bytes 4945920 | tf_op jit(solution)/shard_map/sub | solution.py:109
  31.4 0.2 fusion.49
  31.6 0.3 pad_maximum_fusion
  31.9 8.0 %collective-permute-done.2 = f32[4,4,64,128]{3,2,1,0:T(8,128)S(1)} collective-permute-done((f32[4,4,64,128]{3,2,1,0:T(8,128)S(1)}, f32[4,4,64,128]{3,2,1,0:T(8,128)S(1)}, u32[]{:S(2)}, u32[]{:S(2)}) %collective-permute-start.2) | collective-permute-done | bytes 524320 | tf_op jit(solution)/shard_map/ppermute | solution.py:165
  39.9 0.4 fusion.62
  40.4 8.3 %collective-permute-start.3 = (f32[4,4,64,128]{3,2,1,0:T(8,128)S(1)}, f32[4,4,64,128]{3,2,1,0:T(8,128)S(1)}, u32[]{:S(2)}, u32[]{:S(2)}) collective-permute-start(f32[4,4,64,128]{3,2,1,0:T(8,128)S(1)} %get-tuple-element.14), channel_id=1, source_target_pairs={{0,16},{16,32},{32,48},{48,64},{64,80},{80,96},{96,112},{112,128},... | collective-permute-start | bytes 1572872 | tf_op jit(solution)/shard_map/ppermute | solution.py:174
  48.7 0.3 bitcast_dynamic-update-slice_fusion.9
  49.1 0.3 bitcast_dynamic-update-slice_fusion.8
  49.4 0.3 bitcast_dynamic-update-slice_fusion.7
  49.8 0.3 bitcast_dynamic-update-slice_fusion.6
  50.1 0.0 copy-start.3
  50.2 0.0 copy-start.4
  50.2 0.0 copy-start.5
  50.2 0.0 copy-start.6
  50.2 0.0 copy-start.7
  50.2 0.2 slice_bitcast_fusion.1
  50.4 0.6 fusion.34
  51.1 0.0 copy-done.3
  51.1 0.0 copy-done.4
  51.1 0.0 copy-done.5
  51.1 0.0 copy-done.6
  51.1 0.0 copy-done.7
  51.1 0.2 multiply_add_fusion.1
  51.3 3.7 %collective-permute-start.4 = (f32[5,1,64,128]{3,2,1,0:T(8,128)S(1)}, f32[5,1,64,128]{3,2,1,0:T(8,128)S(1)}, u32[]{:S(2)}, u32[]{:S(2)}) collective-permute-start(f32[5,1,64,128]{3,2,1,0:T(8,128)S(1)} %get-tuple-element.104), channel_id=1, source_target_pairs={{1,0},{2,1},{3,2},{4,3},{5,4},{6,5},{7,6},{8,7},{9,8},{10,9},{11,1... | collective-permute-start | bytes 491528 | tf_op jit(solution)/shard_map/ppermute | solution.py:58
  55.1 1.9 %collective-permute-start.5 = (f32[5,1,64,128]{3,2,1,0:T(8,128)S(1)}, f32[5,1,64,128]{3,2,1,0:T(8,128)S(1)}, u32[]{:S(2)}, u32[]{:S(2)}) collective-permute-start(f32[5,1,64,128]{3,2,1,0:T(8,128)S(1)} %get-tuple-element.105), channel_id=1, source_target_pairs={{0,1},{1,2},{2,3},{3,4},{4,5},{5,6},{6,7},{7,8},{8,9},{9,10},{10,1... | collective-permute-start | bytes 491528 | tf_op jit(solution)/shard_map/ppermute | solution.py:58
  57.0 0.2 fusion.91
  57.3 5.6 %collective-permute-done.4 = f32[5,1,64,128]{3,2,1,0:T(8,128)S(1)} collective-permute-done((f32[5,1,64,128]{3,2,1,0:T(8,128)S(1)}, f32[5,1,64,128]{3,2,1,0:T(8,128)S(1)}, u32[]{:S(2)}, u32[]{:S(2)}) %collective-permute-start.4) | collective-permute-done | bytes 163872 | tf_op jit(solution)/shard_map/ppermute | solution.py:58
  62.9 5.3 %collective-permute-done.5 = f32[5,1,64,128]{3,2,1,0:T(8,128)S(1)} collective-permute-done((f32[5,1,64,128]{3,2,1,0:T(8,128)S(1)}, f32[5,1,64,128]{3,2,1,0:T(8,128)S(1)}, u32[]{:S(2)}, u32[]{:S(2)}) %collective-permute-start.5) | collective-permute-done | bytes 163872 | tf_op jit(solution)/shard_map/ppermute | solution.py:58
  68.2 0.9 %fusion.10 = f32[5,1,4,64,128]{4,3,2,1,0:T(8,128)S(1)} fusion(f32[5,4,64,128]{3,2,1,0:T(8,128)S(1)} %get-tuple-element.29, f32[5,4,64,1]{3,2,1,0:T(8,128)S(1)} %get-tuple-element.57, f32[5,4,64,1]{3,2,1,0:T(8,128)S(1)} %get-tuple-element.56, f32[5,4,1,128]{3,2,1,0:T(1,128)S(1)} %get-tuple-element.55, f32[5,4,1,128]{3,2,1,0:T(1,128)S(1)} %get-tuple-element.54, ...), kind=kLoop, calls=%fused_computation.22 | loop fusion | flops 5242880 | bytes 4290560 | tf_op jit(solution)/shard_map/stack | solution.py:115
  69.1 0.2 pad_maximum_fusion.1
  69.2 0.0 collective-permute-done.3
  69.3 1.2 %fusion.55 = f32[1,4,4,64,128]{4,3,2,1,0:T(8,128)} fusion(f32[5,4,4,64,128]{4,3,2,1,0:T(8,128)S(1)} %pad_maximum_fusion.1, f32[4,4,64,128]{3,2,1,0:T(8,128)S(1)} %collective-permute-done.3, pred[]{:T(512)S(6)} %eq.69, f32[1,4,4,64,128]{4,3,2,1,0:T(8,128)S(1)} %copy-done), kind=kLoop, calls=%fused_computation.94 | loop fusion | flops 1572864 | bytes 4194305 | tf_op jit(solution)/shard_map/broadcast_in_dim | solution.py:189
  (24 shorter events, 0.4 us)
Async XLA Ops:
  0.0 12.5 %copy-start.1 = (s32[4,64,128]{2,1,0:T(8,128)S(1)}, s32[4,64,128]{2,1,0:T(8,128)}, u32[]{:S(2)}) copy-start(s32[4,64,128]{2,1,0:T(8,128)} %param.6) | copy-start | bytes 393220
  0.0 12.5 %copy-start.2 = (s32[4,64,128]{2,1,0:T(8,128)S(1)}, s32[4,64,128]{2,1,0:T(8,128)}, u32[]{:S(2)}) copy-start(s32[4,64,128]{2,1,0:T(8,128)} %param.5) | copy-start | bytes 393220
  0.0 12.8 %copy-start = (f32[1,4,4,64,128]{4,3,2,1,0:T(8,128)S(1)}, f32[1,4,4,64,128]{4,3,2,1,0:T(8,128)}, u32[]{:S(2)}) copy-start(f32[1,4,4,64,128]{4,3,2,1,0:T(8,128)} %param.4) | copy-start | bytes 1572868
  3.0 10.2 %collective-permute-start.1 = (f32[6,64,128]{2,1,0:T(8,128)S(1)}, f32[6,64,128]{2,1,0:T(8,128)S(1)}, u32[]{:S(2)}, u32[]{:S(2)}) collective-permute-start(f32[6,64,128]{2,1,0:T(8,128)S(1)} %pad_maximum_fusion.31), channel_id=1, source_target_pairs={{1,0},{2,1},{3,2},{4,3},{5,4},{6,5},{7,6},{8,7},{9,8},{10,9},{11,1... | collective-permute-start | bytes 589832 | tf_op jit(solution)/shard_map/ppermute | solution.py:58
  9.5 10.1 %collective-permute-start = (f32[6,64,128]{2,1,0:T(8,128)S(1)}, f32[6,64,128]{2,1,0:T(8,128)S(1)}, u32[]{:S(2)}, u32[]{:S(2)}) collective-permute-start(f32[6,64,128]{2,1,0:T(8,128)S(1)} %pad_maximum_fusion.30), channel_id=1, source_target_pairs={{0,1},{1,2},{2,3},{3,4},{4,5},{5,6},{6,7},{7,8},{8,9},{9,10},{10,1... | collective-permute-start | bytes 589832 | tf_op jit(solution)/shard_map/ppermute | solution.py:58
  21.0 19.0 %collective-permute-start.2 = (f32[4,4,64,128]{3,2,1,0:T(8,128)S(1)}, f32[4,4,64,128]{3,2,1,0:T(8,128)S(1)}, u32[]{:S(2)}, u32[]{:S(2)}) collective-permute-start(f32[4,4,64,128]{3,2,1,0:T(8,128)S(1)} %fusion.66), channel_id=1, source_target_pairs={{0,16},{16,32},{32,48},{48,64},{64,80},{80,96},{96,112},{112,128},... | collective-permute-start | bytes 1572872 | tf_op jit(solution)/shard_map/ppermute | solution.py:165
  40.4 28.9 %collective-permute-start.3 = (f32[4,4,64,128]{3,2,1,0:T(8,128)S(1)}, f32[4,4,64,128]{3,2,1,0:T(8,128)S(1)}, u32[]{:S(2)}, u32[]{:S(2)}) collective-permute-start(f32[4,4,64,128]{3,2,1,0:T(8,128)S(1)} %get-tuple-element.14), channel_id=1, source_target_pairs={{0,16},{16,32},{32,48},{48,64},{64,80},{80,96},{96,112},{112,128},... | collective-permute-start | bytes 1572872 | tf_op jit(solution)/shard_map/ppermute | solution.py:174
  50.1 0.9 %copy-start.3 = (f32[5]{0:T(128)S(1)}, f32[5]{0:T(128)}, u32[]{:S(2)}) copy-start(f32[5]{0:T(128)} %constant.210) | copy-start | bytes 64
  50.2 0.9 %copy-start.4 = (f32[5]{0:T(128)S(1)}, f32[5]{0:T(128)}, u32[]{:S(2)}) copy-start(f32[5]{0:T(128)} %constant.208) | copy-start | bytes 64
  50.2 0.9 %copy-start.5 = (f32[5]{0:T(128)S(1)}, f32[5]{0:T(128)}, u32[]{:S(2)}) copy-start(f32[5]{0:T(128)} %constant.206) | copy-start | bytes 64
  50.2 0.9 %copy-start.6 = (f32[5]{0:T(128)S(1)}, f32[5]{0:T(128)}, u32[]{:S(2)}) copy-start(f32[5]{0:T(128)} %constant.204) | copy-start | bytes 64
  50.2 0.9 %copy-start.7 = (f32[5]{0:T(128)S(1)}, f32[5]{0:T(128)}, u32[]{:S(2)}) copy-start(f32[5]{0:T(128)} %constant.202) | copy-start | bytes 64
  51.3 11.5 %collective-permute-start.4 = (f32[5,1,64,128]{3,2,1,0:T(8,128)S(1)}, f32[5,1,64,128]{3,2,1,0:T(8,128)S(1)}, u32[]{:S(2)}, u32[]{:S(2)}) collective-permute-start(f32[5,1,64,128]{3,2,1,0:T(8,128)S(1)} %get-tuple-element.104), channel_id=1, source_target_pairs={{1,0},{2,1},{3,2},{4,3},{5,4},{6,5},{7,6},{8,7},{9,8},{10,9},{11,1... | collective-permute-start | bytes 491528 | tf_op jit(solution)/shard_map/ppermute | solution.py:58
  55.1 13.1 %collective-permute-start.5 = (f32[5,1,64,128]{3,2,1,0:T(8,128)S(1)}, f32[5,1,64,128]{3,2,1,0:T(8,128)S(1)}, u32[]{:S(2)}, u32[]{:S(2)}) collective-permute-start(f32[5,1,64,128]{3,2,1,0:T(8,128)S(1)} %get-tuple-element.105), channel_id=1, source_target_pairs={{0,1},{1,2},{2,3},{3,4},{4,5},{5,6},{6,7},{7,8},{8,9},{9,10},{10,1... | collective-permute-start | bytes 491528 | tf_op jit(solution)/shard_map/ppermute | solution.py:58

commit v7 on v6

--- a/solution.py
+++ b/solution.py
@@ -58,14 +58,6 @@
     return lax.ppermute(block, "space", pairs)
 
 
-def laplacian(volts, low, high, conduct):
-    padded = jnp.concatenate([low, volts, high], axis=-3)
-    lap = conduct[0] * second(padded, volts.ndim - 3)
-    lap = lap + conduct[1] * second(edge_pad(volts, volts.ndim - 2), volts.ndim - 2)
-    lap = lap + conduct[2] * second(edge_pad(volts, volts.ndim - 1), volts.ndim - 1)
-    return lap
-
-
 def close_edges(volts, depth, at_low, at_high):
     size = volts.shape[-3]
     inner_low = volts[..., depth : depth + 1, :, :]
@@ -122,13 +114,6 @@
     return start + slice_len * total
 
 
-def edge_nodes(start, derivs, weights):
-    total = weights[:, 0] * derivs[0][None]
-    for j in range(1, 5):
-        total = total + weights[:, j] * derivs[j][None]
-    return start[None] + slice_len * total
-
-
 def steps(guess, fibre, labels):
     table = radau_table()
     sums = [sum(row) for row in table]
@@ -142,6 +127,7 @@
     start0 = guess[0]
     volts0 = start0[0]
     planes = volts0.shape[0]
+    rows = start0.shape[2:]
 
     code = (labels + 4 * fibre).astype(jnp.float32)
     top = jnp.concatenate([volts0[planes - 2 :], start0[1:, planes - 1], code[planes - 1 :]])
@@ -161,29 +147,37 @@
     state_ext = jnp.concatenate([volts_ext[None, 1 : planes + 3], gates_ext])
     lap0 = padded_laplacian(close_edges(volts_ext, 2, at_low, at_high), conduct_ext)
     derivs0 = rates(state_ext, lap0, *coef_ext)
-    ends0 = start0 + slice_len * (sums[4] * derivs0[:, 1 : planes + 1])
-    arrived1 = lax.ppermute(ends0, "tm", tm_pairs)
-
-    state_ext, derivs0, ends0 = lax.optimization_barrier((state_ext, derivs0, ends0))
+    ends0 = state_ext + slice_len * (sums[4] * derivs0)
+    fields = start0.shape[0]
+    message1 = jnp.concatenate(
+        [ends0[:, 1 : planes + 1].reshape(fields * planes, *rows), ends0[0, :1], ends0[0, planes + 1 :]]
+    )
+    state_ext, derivs0, message1 = lax.optimization_barrier((state_ext, derivs0, message1))
+    arrived1 = lax.ppermute(message1, "tm", tm_pairs)
     nodes0_ext = jnp.stack([state_ext + slice_len * (sums[m] * derivs0) for m in range(5)])
     nodes0 = nodes0_ext[:, :, 1 : planes + 1]
     lap1 = padded_laplacian(close_edges(nodes0_ext[:, 0], 1, at_low, at_high), conduct)
     derivs1 = rates(nodes0, lap1, fast_g, slow_g, slow_tau)
-    start1 = jnp.where(first_slice, start0, arrived1)
+    low_f = shift_space(derivs1[:, 0, planes - 1 :], True)
+    high_f = shift_space(derivs1[:, 0, :1], False)
+    block1 = arrived1[: fields * planes].reshape(start0.shape)
+    start1 = jnp.where(first_slice, start0, block1)
+    start1_volts = jnp.where(
+        first_slice,
+        volts_ext[1 : planes + 3],
+        jnp.concatenate([arrived1[fields * planes : fields * planes + 1], block1[0], arrived1[fields * planes + 1 :]]),
+    )
     ends1 = quadrature(start1, derivs1, table[4])
     arrived2 = lax.ppermute(ends1, "tm", tm_pairs)
-    weights = jnp.array(table, jnp.float32)[:, :, None, None, None]
-    top = edge_nodes(start1[0, planes - 1 :], derivs1[:, 0, planes - 1 :], weights)
-    bottom = edge_nodes(start1[0, :1], derivs1[:, 0, :1], weights)
-    low2 = shift_space(top, True)
-    high2 = shift_space(bottom, False)
-    later_start, later_derivs, ends1 = lax.optimization_barrier((start1, derivs1, ends1))
-    nodes1 = jnp.stack([quadrature(later_start, later_derivs, table[m]) for m in range(4)] + [ends1])
+    later = lax.optimization_barrier((start1, start1_volts, derivs1, low_f, high_f, ends1))
+    later_start, later_volts, later_derivs, low_f, high_f, ends1 = later
+    dvolts1 = jnp.concatenate([low_f, later_derivs[:, 0], high_f], axis=1)
+    volts1 = jnp.stack([quadrature(later_volts, dvolts1, table[m]) for m in range(5)])
+    gates1 = jnp.stack([quadrature(later_start[1:], later_derivs[:, 1:], table[m]) for m in range(5)])
+    nodes1 = jnp.concatenate([volts1[:, None, 1 : planes + 1], gates1], axis=1)
 
-    volts2 = nodes1[:, 0]
-    low2 = jnp.where(at_low, volts2[:, :1], low2)
-    high2 = jnp.where(at_high, volts2[:, planes - 1 :], high2)
-    derivs2 = rates(nodes1, laplacian(volts2, low2, high2, conduct), fast_g, slow_g, slow_tau)
+    lap2 = padded_laplacian(close_edges(volts1, 1, at_low, at_high), conduct)
+    derivs2 = rates(nodes1, lap2, fast_g, slow_g, slow_tau)
     start2 = jnp.where(first_slice, start0, arrived2)
     ends2 = quadrature(start2, derivs2, table[4])
     return ends2[None]

time: 70.8 us -> 71 us (level)
  the two profiles are of different devices: /device:TPU:23 before, /device:TPU:18 now
where the time goes in v7:
time: 71 us; the launch traced here: 70.6 us
  waiting for transfers between devices  37.7 us (53%)
  starting transfers between devices  18.1 us (25%)
  other arithmetic  10.4 us (15%)
  local copies, waits for them, and re-layouts  3.88 us (5%)
    ppermute x1, waiting for transfers between devices, steps(): arrived1 = lax.ppermute(message1, 'tm', tm_pairs)  16.2 us
    ppermute x4, starting transfers between devices, shift_space(): return lax.ppermute(block, 'space', pairs)  14.3 us
    ppermute x1, waiting for transfers between devices, steps(): arrived2 = lax.ppermute(ends1, 'tm', tm_pairs)  13.8 us
    ppermute x4, waiting for transfers between devices, shift_space(): return lax.ppermute(block, 'space', pairs)  7.67 us
    another operation x7, other arithmetic, rates(): return jnp.stack([dvolt, dact, dinact, dslow], axis=-4)  3.63 us
    ppermute x1, starting transfers between devices, steps(): arrived2 = lax.ppermute(ends1, 'tm', tm_pairs)  1.92 us
    ppermute x1, starting transfers between devices, steps(): arrived1 = lax.ppermute(message1, 'tm', tm_pairs)  1.92 us
    unnamed x12, other arithmetic  1.84 us
  transfers between devices with their start and end apart: 6, of which 4 were waited for; matrix products, arithmetic and copies ran while one was open for 11% of the time, Pallas kernels for 0%

profile of v7, /device:TPU:18, one launch (start us, length us, event | category | flops | bytes accessed | tf_op | source)
XLA Modules:
  0.0 70.6 jit_solution(7620627789454769278)
XLA Ops:
  0.0 0.0 copy-start.1
  0.0 0.0 copy-start.2
  0.0 0.0 copy-start
  0.0 1.1 %add_convert_fusion = f32[4,64,128]{2,1,0:T(8,128)S(1)} fusion(s32[4,64,128]{2,1,0:T(8,128)} %param.5, s32[4,64,128]{2,1,0:T(8,128)} %param.4), kind=kLoop, calls=%fused_computation.182 | loop fusion | flops 98304 | bytes 393216 | tf_op jit(solution)/shard_map/convert_element_type | solution.py:132
  1.1 0.9 %slice_bitcast_fusion.17 = (f32[2,64,128]{2,1,0:T(8,128)S(1)}, f32[2,64,128]{2,1,0:T(8,128)S(1)}) fusion(f32[1,4,4,64,128]{4,3,2,1,0:T(8,128)} %param.3), kind=kLoop, calls=%fused_computation.205 | loop fusion | bytes 262144 | tf_op jit(solution)/shard_map/slice | solution.py:133
  2.0 1.0 %slice_bitcast_fusion.15 = (f32[3,64,128]{2,1,0:T(8,128)S(1)}, f32[3,64,128]{2,1,0:T(8,128)S(1)}) fusion(f32[4,4,64,128]{3,2,1,0:T(8,128)} %bitcast.232), kind=kLoop, calls=%fused_computation.186 | loop fusion | bytes 393216 | tf_op jit(solution)/shard_map/squeeze | solution.py:133
  3.0 6.5 %collective-permute-start.1 = (f32[6,64,128]{2,1,0:T(8,128)S(1)}, f32[6,64,128]{2,1,0:T(8,128)S(1)}, u32[]{:S(2)}, u32[]{:S(2)}) collective-permute-start(f32[6,64,128]{2,1,0:T(8,128)S(1)} %pad_maximum_fusion.33), channel_id=1, source_target_pairs={{1,0},{2,1},{3,2},{4,3},{5,4},{6,5},{7,6},{8,7},{9,8},{10,9},{11,1... | collective-permute-start | bytes 589832 | tf_op jit(solution)/shard_map/ppermute | solution.py:58
  9.5 1.9 %collective-permute-start = (f32[6,64,128]{2,1,0:T(8,128)S(1)}, f32[6,64,128]{2,1,0:T(8,128)S(1)}, u32[]{:S(2)}, u32[]{:S(2)}) collective-permute-start(f32[6,64,128]{2,1,0:T(8,128)S(1)} %pad_maximum_fusion.32), channel_id=1, source_target_pairs={{0,1},{1,2},{2,3},{3,4},{4,5},{5,6},{6,7},{7,8},{8,9},{9,10},{10,1... | collective-permute-start | bytes 589832 | tf_op jit(solution)/shard_map/ppermute | solution.py:58
  11.4 1.0 %slice_bitcast_fusion.5 = f32[3,4,64,128]{3,2,1,0:T(8,128)S(1)} fusion(f32[1,4,4,64,128]{4,3,2,1,0:T(8,128)} %param.3), kind=kLoop, calls=%fused_computation.111 | loop fusion | bytes 786432 | tf_op jit(solution)/shard_map/slice | solution.py:146
  12.5 0.0 copy-done.1
  12.5 0.0 copy-done.2
  12.5 0.1 select_add_fusion
  12.6 0.1 select_add_fusion.1
  12.8 0.0 copy-done
  12.8 2.0 %collective-permute-done.1 = f32[6,64,128]{2,1,0:T(8,128)S(1)} collective-permute-done((f32[6,64,128]{2,1,0:T(8,128)S(1)}, f32[6,64,128]{2,1,0:T(8,128)S(1)}, u32[]{:S(2)}, u32[]{:S(2)}) %collective-permute-start.1) | collective-permute-done | bytes 196640 | tf_op jit(solution)/shard_map/ppermute | solution.py:58
  14.8 5.7 %collective-permute-done = f32[6,64,128]{2,1,0:T(8,128)S(1)} collective-permute-done((f32[6,64,128]{2,1,0:T(8,128)S(1)}, f32[6,64,128]{2,1,0:T(8,128)S(1)}, u32[]{:S(2)}, u32[]{:S(2)}) %collective-permute-start) | collective-permute-done | bytes 196640 | tf_op jit(solution)/shard_map/ppermute | solution.py:58
  20.5 0.1 fusion.76
  20.6 0.1 select_add_fusion.7
  20.8 0.1 select_add_fusion.6
  21.0 0.3 multiply_bitcast_fusion.1
  21.3 0.3 fusion.56
  21.6 0.3 multiply_add_fusion
  22.0 0.1 bitcast_dynamic-update-slice_fusion.3
  22.1 0.1 bitcast_dynamic-update-slice_fusion.2
  22.2 0.1 bitcast_dynamic-update-slice_fusion.1
  22.3 0.1 bitcast_dynamic-update-slice_fusion
  22.4 0.1 bitcast_dynamic-update-slice_fusion.4
  22.6 0.1 slice_bitcast_fusion
  22.8 0.2 fusion.73
  23.0 1.9 %collective-permute-start.2 = (f32[18,64,128]{2,1,0:T(8,128)S(1)}, f32[18,64,128]{2,1,0:T(8,128)S(1)}, u32[]{:S(2)}, u32[]{:S(2)}) collective-permute-start(f32[18,64,128]{2,1,0:T(8,128)S(1)} %pad_maximum_fusion.17), channel_id=1, source_target_pairs={{0,16},{16,32},{32,48},{48,64},{64,80},{80,96},{96,112},{112,128},... | collective-permute-start | bytes 1769480 | tf_op jit(solution)/shard_map/ppermute | solution.py:156
  24.9 0.9 %fusion.5 = f32[5,1,4,64,128]{4,3,2,0,1:T(8,128)S(1)} fusion(f32[5,4,64,128]{3,2,1,0:T(8,128)S(1)} %slice.613, f32[5,4,64,1]{3,2,1,0:T(8,128)S(1)} %get-tuple-element.51, f32[5,4,64,1]{3,2,1,0:T(8,128)S(1)} %get-tuple-element.50, f32[5,4,1,128]{3,2,1,0:T(1,128)S(1)} %get-tuple-element.49, f32[5,4,1,128]{3,2,1,0:T(1,128)S(1)} %get-tuple-element.48, ...), kind=kLoop, calls=%fused_computation.19 | loop fusion | flops 5242880 | bytes 4945920 | tf_op jit(solution)/shard_map/stack | solution.py:107
  25.8 1.9 %collective-permute-start.5 = (f32[5,1,64,128]{3,2,0,1:T(8,128)S(1)}, f32[5,1,64,128]{3,2,0,1:T(8,128)S(1)}, u32[]{:S(2)}, u32[]{:S(2)}) collective-permute-start(f32[5,1,64,128]{3,2,0,1:T(8,128)S(1)} %get-tuple-element.60), channel_id=1, source_target_pairs={{1,0},{2,1},{3,2},{4,3},{5,4},{6,5},{7,6},{8,7},{9,8},{10,9},{11,1... | collective-permute-start | bytes 491528 | tf_op jit(solution)/shard_map/ppermute | solution.py:58
  27.8 3.9 %collective-permute-start.4 = (f32[5,1,64,128]{3,2,0,1:T(8,128)S(1)}, f32[5,1,64,128]{3,2,0,1:T(8,128)S(1)}, u32[]{:S(2)}, u32[]{:S(2)}) collective-permute-start(f32[5,1,64,128]{3,2,0,1:T(8,128)S(1)} %get-tuple-element.61), channel_id=1, source_target_pairs={{0,1},{1,2},{2,3},{3,4},{4,5},{5,6},{6,7},{7,8},{8,9},{9,10},{10,1... | collective-permute-start | bytes 491528 | tf_op jit(solution)/shard_map/ppermute | solution.py:58
  31.7 0.8 %subtract_multiply_fusion = (f32[5,1,4,64,128]{4,3,2,0,1:T(8,128)S(1)}, f32[5,1,4,64,128]{4,3,2,0,1:T(8,128)S(1)}, f32[5,1,4,64,128]{4,3,2,0,1:T(8,128)S(1)}) fusion(f32[5,4,6,64,128]{4,3,2,0,1:T(8,128)S(1)} %bitcast_dynamic-update-slice_fusion.4, f32[4,64,128]{2,1,0:T(8,128)S(1)} %get-tuple-element.80), kind=kLoop, calls=%fused_computation.71 | loop fusion | flops 4423680 | bytes 4718592 | tf_op jit(solution)/shard_map/div | solution.py:102
  32.5 0.3 pad_maximum_fusion
  32.8 16.2 %collective-permute-done.2 = f32[18,64,128]{2,1,0:T(8,128)S(1)} collective-permute-done((f32[18,64,128]{2,1,0:T(8,128)S(1)}, f32[18,64,128]{2,1,0:T(8,128)S(1)}, u32[]{:S(2)}, u32[]{:S(2)}) %collective-permute-start.2) | collective-permute-done | bytes 589856 | tf_op jit(solution)/shard_map/ppermute | solution.py:156
  49.0 0.4 fusion.45
  49.4 1.9 %collective-permute-start.3 = (f32[4,4,64,128]{3,2,1,0:T(8,128)S(1)}, f32[4,4,64,128]{3,2,1,0:T(8,128)S(1)}, u32[]{:S(2)}, u32[]{:S(2)}) collective-permute-start(f32[4,4,64,128]{3,2,1,0:T(8,128)S(1)} %get-tuple-element.21), channel_id=1, source_target_pairs={{0,16},{16,32},{32,48},{48,64},{64,80},{80,96},{96,112},{112,128},... | collective-permute-start | bytes 1572872 | tf_op jit(solution)/shard_map/ppermute | solution.py:171
  51.4 0.0 collective-permute-done.5
  51.4 0.0 collective-permute-done.4
  51.5 0.1 pad_maximum_fusion.2
  51.6 0.1 bitcast_dynamic-update-slice_fusion.14
  51.7 0.1 bitcast_dynamic-update-slice_fusion.13
  51.8 0.1 bitcast_dynamic-update-slice_fusion.12
  51.9 0.1 bitcast_dynamic-update-slice_fusion.11
  52.0 0.1 bitcast_dynamic-update-slice_fusion.10
  52.2 0.2 fusion.71
  52.4 0.3 bitcast_dynamic-update-slice_fusion.9
  52.7 0.3 bitcast_dynamic-update-slice_fusion.8
  52.9 0.3 bitcast_dynamic-update-slice_fusion.7
  53.2 0.3 bitcast_dynamic-update-slice_fusion.6
  53.4 0.3 bitcast_dynamic-update-slice_fusion.5
  53.7 0.8 %multiply_bitcast_fusion = (f32[5,1,4,64,128]{4,3,2,0,1:T(8,128)S(1)}, f32[5,1,4,64,128]{4,3,2,0,1:T(8,128)S(1)}, f32[5,1,4,64,128]{4,3,2,0,1:T(8,128)S(1)}, f32[5,4,64,128]{3,2,1,0:T(8,128)S(1)}) fusion(f32[5,3,4,64,128]{4,3,2,1,0:T(8,128)S(1)} %bitcast_dynamic-update-slice_fusion.5, f32[5,6,64,128]{3,2,1,0:T(8,128)S(1)} %bitcast_dynamic-update-slice_fusion.10, ...), kind=kLoop, calls=%fused_computation.67 | loop fusion | flops 4423680 | bytes 5373952 | tf_op jit(solution)/shard_map/stack | solution.py:107
  54.5 0.9 %fusion.11 = f32[5,1,4,64,128]{4,3,2,0,1:T(8,128)S(1)} fusion(f32[5,4,64,128]{3,2,1,0:T(8,128)S(1)} %get-tuple-element.45, f32[5,4,64,1]{3,2,1,0:T(8,128)S(1)} %get-tuple-element.44, f32[5,4,64,1]{3,2,1,0:T(8,128)S(1)} %get-tuple-element.43, f32[5,4,1,128]{3,2,1,0:T(1,128)S(1)} %get-tuple-element.42, f32[5,4,1,128]{3,2,1,0:T(1,128)S(1)} %get-tuple-element.41, ...), kind=kLoop, calls=%fused_computation.25 | loop fusion | flops 5242880 | bytes 4290560 | tf_op jit(solution)/shard_map/stack | solution.py:107
  55.4 0.2 pad_maximum_fusion.1
  55.6 13.8 %collective-permute-done.3 = f32[4,4,64,128]{3,2,1,0:T(8,128)S(1)} collective-permute-done((f32[4,4,64,128]{3,2,1,0:T(8,128)S(1)}, f32[4,4,64,128]{3,2,1,0:T(8,128)S(1)}, u32[]{:S(2)}, u32[]{:S(2)}) %collective-permute-start.3) | collective-permute-done | bytes 524320 | tf_op jit(solution)/shard_map/ppermute | solution.py:171
  69.4 1.2 %fusion.37 = f32[1,4,4,64,128]{4,3,2,1,0:T(8,128)} fusion(f32[5,4,4,64,128]{4,3,2,0,1:T(8,128)S(1)} %pad_maximum_fusion.1, f32[4,4,64,128]{3,2,1,0:T(8,128)S(1)} %collective-permute-done.3, pred[]{:T(512)S(6)} %eq.69, f32[1,4,4,64,128]{4,3,2,1,0:T(8,128)S(1)} %copy-done), kind=kLoop, calls=%fused_computation.80 | loop fusion | flops 1572864 | bytes 4194305 | tf_op jit(solution)/shard_map/broadcast_in_dim | solution.py:183
  (29 shorter events, 0.6 us)
Async XLA Ops:
  0.0 12.5 %copy-start.1 = (s32[4,64,128]{2,1,0:T(8,128)S(1)}, s32[4,64,128]{2,1,0:T(8,128)}, u32[]{:S(2)}) copy-start(s32[4,64,128]{2,1,0:T(8,128)} %param.5) | copy-start | bytes 393220
  0.0 12.5 %copy-start.2 = (s32[4,64,128]{2,1,0:T(8,128)S(1)}, s32[4,64,128]{2,1,0:T(8,128)}, u32[]{:S(2)}) copy-start(s32[4,64,128]{2,1,0:T(8,128)} %param.4) | copy-start | bytes 393220
  0.0 12.8 %copy-start = (f32[1,4,4,64,128]{4,3,2,1,0:T(8,128)S(1)}, f32[1,4,4,64,128]{4,3,2,1,0:T(8,128)}, u32[]{:S(2)}) copy-start(f32[1,4,4,64,128]{4,3,2,1,0:T(8,128)} %param.3) | copy-start | bytes 1572868
  3.0 11.8 %collective-permute-start.1 = (f32[6,64,128]{2,1,0:T(8,128)S(1)}, f32[6,64,128]{2,1,0:T(8,128)S(1)}, u32[]{:S(2)}, u32[]{:S(2)}) collective-permute-start(f32[6,64,128]{2,1,0:T(8,128)S(1)} %pad_maximum_fusion.33), channel_id=1, source_target_pairs={{1,0},{2,1},{3,2},{4,3},{5,4},{6,5},{7,6},{8,7},{9,8},{10,9},{11,1... | collective-permute-start | bytes 589832 | tf_op jit(solution)/shard_map/ppermute | solution.py:58
  9.5 11.0 %collective-permute-start = (f32[6,64,128]{2,1,0:T(8,128)S(1)}, f32[6,64,128]{2,1,0:T(8,128)S(1)}, u32[]{:S(2)}, u32[]{:S(2)}) collective-permute-start(f32[6,64,128]{2,1,0:T(8,128)S(1)} %pad_maximum_fusion.32), channel_id=1, source_target_pairs={{0,1},{1,2},{2,3},{3,4},{4,5},{5,6},{6,7},{7,8},{8,9},{9,10},{10,1... | collective-permute-start | bytes 589832 | tf_op jit(solution)/shard_map/ppermute | solution.py:58
  23.0 26.0 %collective-permute-start.2 = (f32[18,64,128]{2,1,0:T(8,128)S(1)}, f32[18,64,128]{2,1,0:T(8,128)S(1)}, u32[]{:S(2)}, u32[]{:S(2)}) collective-permute-start(f32[18,64,128]{2,1,0:T(8,128)S(1)} %pad_maximum_fusion.17), channel_id=1, source_target_pairs={{0,16},{16,32},{32,48},{48,64},{64,80},{80,96},{96,112},{112,128},... | collective-permute-start | bytes 1769480 | tf_op jit(solution)/shard_map/ppermute | solution.py:156
  25.8 25.6 %collective-permute-start.5 = (f32[5,1,64,128]{3,2,0,1:T(8,128)S(1)}, f32[5,1,64,128]{3,2,0,1:T(8,128)S(1)}, u32[]{:S(2)}, u32[]{:S(2)}) collective-permute-start(f32[5,1,64,128]{3,2,0,1:T(8,128)S(1)} %get-tuple-element.60), channel_id=1, source_target_pairs={{1,0},{2,1},{3,2},{4,3},{5,4},{6,5},{7,6},{8,7},{9,8},{10,9},{11,1... | collective-permute-start | bytes 491528 | tf_op jit(solution)/shard_map/ppermute | solution.py:58
  27.8 23.7 %collective-permute-start.4 = (f32[5,1,64,128]{3,2,0,1:T(8,128)S(1)}, f32[5,1,64,128]{3,2,0,1:T(8,128)S(1)}, u32[]{:S(2)}, u32[]{:S(2)}) collective-permute-start(f32[5,1,64,128]{3,2,0,1:T(8,128)S(1)} %get-tuple-element.61), channel_id=1, source_target_pairs={{0,1},{1,2},{2,3},{3,4},{4,5},{5,6},{6,7},{7,8},{8,9},{9,10},{10,1... | collective-permute-start | bytes 491528 | tf_op jit(solution)/shard_map/ppermute | solution.py:58
  49.4 20.0 %collective-permute-start.3 = (f32[4,4,64,128]{3,2,1,0:T(8,128)S(1)}, f32[4,4,64,128]{3,2,1,0:T(8,128)S(1)}, u32[]{:S(2)}, u32[]{:S(2)}) collective-permute-start(f32[4,4,64,128]{3,2,1,0:T(8,128)S(1)} %get-tuple-element.21), channel_id=1, source_target_pairs={{0,16},{16,32},{32,48},{48,64},{64,80},{80,96},{96,112},{112,128},... | collective-permute-start | bytes 1572872 | tf_op jit(solution)/shard_map/ppermute | solution.py:171

commit v8 on v4

--- a/solution.py
+++ b/solution.py
@@ -92,11 +92,15 @@
     return jnp.stack([dvolt, dact, dinact, dslow], axis=-4)
 
 
-def quadrature(start, derivs, row):
+def increment(derivs, row):
     total = row[0] * derivs[0]
     for j in range(1, 5):
         total = total + row[j] * derivs[j]
-    return start + slice_len * total
+    return slice_len * total
+
+
+def quadrature(start, derivs, row):
+    return start + increment(derivs, row)
 
 
 def steps(guess, fibre, labels):
@@ -133,18 +137,21 @@
     low1 = jnp.where(at_low, volts1[:, :1], low1)
     high1 = jnp.where(at_high, volts1[:, planes - 1 :], high1)
     derivs1 = rates(nodes0, laplacian(volts1, low1, high1, conduct), fast_g, slow_g, slow_tau)
+    step1 = lax.optimization_barrier(increment(derivs1, table[4]))
     start1 = jnp.where(first_slice, start0, arrived1)
-    ends1 = quadrature(start1, derivs1, table[4])
+    ends1 = start1 + step1
     arrived2 = lax.ppermute(ends1, "tm", tm_pairs)
-    nodes1 = jnp.stack([quadrature(start1, derivs1, table[m]) for m in range(4)] + [ends1])
+    later_start, later_derivs, ends1 = lax.optimization_barrier((start1, derivs1, ends1))
+    nodes1 = jnp.stack([quadrature(later_start, later_derivs, table[m]) for m in range(4)] + [ends1])
 
     volts2 = nodes1[:, 0]
     low2, high2 = halos(volts2)
     low2 = jnp.where(at_low, volts2[:, :1], low2)
     high2 = jnp.where(at_high, volts2[:, planes - 1 :], high2)
     derivs2 = rates(nodes1, laplacian(volts2, low2, high2, conduct), fast_g, slow_g, slow_tau)
+    step2 = lax.optimization_barrier(increment(derivs2, table[4]))
     start2 = jnp.where(first_slice, start0, arrived2)
-    ends2 = quadrature(start2, derivs2, table[4])
+    ends2 = start2 + step2
     return ends2[None]
 
 

time: 72.3 us -> 73.5 us (1.017)
  waiting for transfers between devices: 19.6 us -> 20.7 us
    ppermute x1, waiting for transfers between devices: 3.36 us -> 4.55 us  [steps(): arrived1 = lax.ppermute(ends0, 'tm', tm_pairs)]
  transfers between devices with their start and end apart: 8 -> 8, of which waited for: 3 -> 3; matrix products, arithmetic and copies ran while one was open for 10% -> 9% of each run, Pallas kernels for 0% -> 0%
where the time goes in v8:
time: 73.5 us; the launch traced here: 73.2 us
  starting transfers between devices  39.6 us (54%)
  waiting for transfers between devices  20.7 us (28%)
  other arithmetic  10.9 us (15%)
  local copies, waits for them, and re-layouts  1.55 us (2%)
    ppermute x6, starting transfers between devices, shift_space(): return lax.ppermute(block, 'space', pairs)  23.2 us
    ppermute x6, waiting for transfers between devices, shift_space(): return lax.ppermute(block, 'space', pairs)  16.2 us
    ppermute x1, starting transfers between devices, steps(): arrived2 = lax.ppermute(ends1, 'tm', tm_pairs)  8.4 us
    ppermute x1, starting transfers between devices, steps(): arrived1 = lax.ppermute(ends0, 'tm', tm_pairs)  7.93 us
    ppermute x1, waiting for transfers between devices, steps(): arrived1 = lax.ppermute(ends0, 'tm', tm_pairs)  4.55 us
    another operation x4, other arithmetic, rates(): return jnp.stack([dvolt, dact, dinact, dslow], axis=-4)  2.09 us
    div x2, other arithmetic, rates(): dact = (jax.nn.sigmoid(8.0 * (volt - 0.2)) - act) / 0.5  1.78 us
    unnamed x15, other arithmetic  1.73 us
  transfers between devices with their start and end apart: 8, of which 3 were waited for; matrix products, arithmetic and copies ran while one was open for 9% of the time, Pallas kernels for 0%

profile of v8, /device:TPU:27, one launch (start us, length us, event | category | flops | bytes accessed | tf_op | source)
XLA Modules:
  0.0 73.2 jit_solution(12685021891678352741)
XLA Ops:
  0.0 0.0 copy-start
  0.0 0.0 copy-start.1
  0.0 0.8 %slice_bitcast_fusion.3 = (f32[1,64,128]{2,1,0:T(8,128)S(1)}, f32[1,64,128]{2,1,0:T(8,128)S(1)}) fusion(f32[1,4,4,64,128]{4,3,2,1,0:T(8,128)} %param.3), kind=kLoop, calls=%fused_computation.185 | loop fusion | bytes 131072 | tf_op jit(solution)/shard_map/slice | solution.py:125
  0.9 6.2 %collective-permute-start = (f32[1,64,128]{2,1,0:T(8,128)S(1)}, f32[1,64,128]{2,1,0:T(8,128)S(1)}, u32[]{:S(2)}, u32[]{:S(2)}) collective-permute-start(f32[1,64,128]{2,1,0:T(8,128)S(1)} %get-tuple-element.45), channel_id=1, source_target_pairs={{1,0},{2,1},{3,2},{4,3},{5,4},{6,5},{7,6},{8,7},{9,8},{10,9},{11,1... | collective-permute-start | bytes 98312 | tf_op jit(solution)/shard_map/ppermute | solution.py:58
  7.1 1.9 %collective-permute-start.1 = (f32[1,64,128]{2,1,0:T(8,128)S(1)}, f32[1,64,128]{2,1,0:T(8,128)S(1)}, u32[]{:S(2)}, u32[]{:S(2)}) collective-permute-start(f32[1,64,128]{2,1,0:T(8,128)S(1)} %get-tuple-element.46), channel_id=1, source_target_pairs={{0,1},{1,2},{2,3},{3,4},{4,5},{5,6},{6,7},{7,8},{8,9},{9,10},{10,1... | collective-permute-start | bytes 98312 | tf_op jit(solution)/shard_map/ppermute | solution.py:58
  9.0 1.2 %fusion.91 = (f32[1,4,64,128]{3,2,1,0:T(8,128)S(1)}, f32[1,1,4,64,128]{4,3,2,0,1:T(8,128)S(1)}, f32[1,1,4,64,128]{4,3,2,1,0:T(8,128)S(1)}, f32[4,64,128]{2,1,0:T(8,128)S(1)}) fusion(f32[1,4,4,64,128]{4,3,2,1,0:T(8,128)} %param.3), kind=kLoop, calls=%fused_computation.190 | loop fusion | flops 655360 | bytes 917504 | tf_op jit(solution)/shard_map/div | solution.py:87
  10.2 0.1 fusion.100
  10.3 1.0 %select_add_fusion.1 = (f32[4,64,128]{2,1,0:T(8,128)S(1)}, pred[4,64,128]{2,1,0:T(8,128)(4,1)S(1)}, pred[4,64,128]{2,1,0:T(8,128)(4,1)S(1)}, pred[4,64,128]{2,1,0:T(8,128)(4,1)S(1)}, pred[4,64,128]{2,1,0:T(8,128)(4,1)S(1)}) fusion(s32[4,64,128]{2,1,0:T(8,128)} %param.5), kind=kLoop, calls=%fused_computation.164 | loop fusion | flops 360448 | bytes 393216 | tf_op jit(solution)/shard_map/add | solution.py:34
  11.3 1.0 %select_add_fusion.4 = (f32[4,64,128]{2,1,0:T(8,128)S(1)}, f32[4,64,128]{2,1,0:T(8,128)S(1)}, f32[4,64,128]{2,1,0:T(8,128)S(1)}) fusion(s32[4,64,128]{2,1,0:T(8,128)} %param.4), kind=kLoop, calls=%fused_computation.167 | loop fusion | flops 294912 | bytes 524288 | tf_op jit(solution)/shard_map/add | solution.py:112
  12.3 0.0 copy-done
  12.3 0.2 select_add_fusion
  12.4 0.0 collective-permute-done
  12.5 2.0 %collective-permute-done.1 = f32[1,64,128]{2,1,0:T(8,128)S(1)} collective-permute-done((f32[1,64,128]{2,1,0:T(8,128)S(1)}, f32[1,64,128]{2,1,0:T(8,128)S(1)}, u32[]{:S(2)}, u32[]{:S(2)}) %collective-permute-start.1) | collective-permute-done | bytes 32800 | tf_op jit(solution)/shard_map/ppermute | solution.py:58
  14.4 0.0 copy-done.1
  14.5 0.3 fusion.77
  14.8 0.1 fusion.67
  14.9 0.1 fusion.68
  14.9 0.1 fusion.69
  15.0 0.1 fusion.70
  15.1 0.1 fusion.66
  15.2 0.6 slice_bitcast_fusion.1
  15.8 4.1 %collective-permute-start.3 = (f32[1,64,128]{2,1,0:T(8,128)S(1)}, f32[1,64,128]{2,1,0:T(8,128)S(1)}, u32[]{:S(2)}, u32[]{:S(2)}) collective-permute-start(f32[1,64,128]{2,1,0:T(8,128)S(1)} %get-tuple-element.53), channel_id=1, source_target_pairs={{1,0},{2,1},{3,2},{4,3},{5,4},{6,5},{7,6},{8,7},{9,8},{10,9},{11,1... | collective-permute-start | bytes 98312 | tf_op jit(solution)/shard_map/ppermute | solution.py:58
  19.9 1.9 %collective-permute-start.4 = (f32[1,64,128]{2,1,0:T(8,128)S(1)}, f32[1,64,128]{2,1,0:T(8,128)S(1)}, u32[]{:S(2)}, u32[]{:S(2)}) collective-permute-start(f32[1,64,128]{2,1,0:T(8,128)S(1)} %get-tuple-element.54), channel_id=1, source_target_pairs={{0,1},{1,2},{2,3},{3,4},{4,5},{5,6},{6,7},{7,8},{8,9},{9,10},{10,1... | collective-permute-start | bytes 98312 | tf_op jit(solution)/shard_map/ppermute | solution.py:58
  21.8 0.2 fusion.97
  22.1 0.2 fusion.50
  22.3 0.1 fusion.64
  22.4 7.9 %collective-permute-start.2 = (f32[4,4,64,128]{3,2,1,0:T(8,128)S(1)}, f32[4,4,64,128]{3,2,1,0:T(8,128)S(1)}, u32[]{:S(2)}, u32[]{:S(2)}) collective-permute-start(f32[4,4,64,128]{3,2,1,0:T(8,128)S(1)} %fusion.64), channel_id=1, source_target_pairs={{0,16},{16,32},{32,48},{48,64},{64,80},{80,96},{96,112},{112,128},... | collective-permute-start | bytes 1572872 | tf_op jit(solution)/shard_map/ppermute | solution.py:129
  30.3 0.0 collective-permute-done.3
  30.3 0.0 collective-permute-done.4
  30.5 0.9 %fusion.5 = f32[5,1,4,64,128]{4,3,2,1,0:T(8,128)S(1)} fusion(f32[5,4,64,128]{3,2,1,0:T(8,128)S(1)} %get-tuple-element.22, f32[5,4,64,1]{3,2,1,0:T(8,128)S(1)} %get-tuple-element.38, f32[5,4,64,1]{3,2,1,0:T(8,128)S(1)} %get-tuple-element.37, f32[5,4,1,128]{3,2,1,0:T(1,128)S(1)} %get-tuple-element.36, f32[5,4,1,128]{3,2,1,0:T(1,128)S(1)} %get-tuple-element.35, ...), kind=kLoop, calls=%fused_computation.9 | loop fusion | flops 5242880 | bytes 4290560 | tf_op jit(solution)/shard_map/stack | solution.py:92
  31.4 0.2 pad_maximum_fusion
  31.6 0.3 fusion.60
  31.9 4.5 %collective-permute-done.2 = f32[4,4,64,128]{3,2,1,0:T(8,128)S(1)} collective-permute-done((f32[4,4,64,128]{3,2,1,0:T(8,128)S(1)}, f32[4,4,64,128]{3,2,1,0:T(8,128)S(1)}, u32[]{:S(2)}, u32[]{:S(2)}) %collective-permute-start.2) | collective-permute-done | bytes 524320 | tf_op jit(solution)/shard_map/ppermute | solution.py:129
  36.4 0.1 fusion.92
  36.6 0.3 bitcast_dynamic-update-slice_fusion.4
  36.9 0.3 bitcast_dynamic-update-slice_fusion.3
  37.3 0.3 bitcast_dynamic-update-slice_fusion.2
  37.6 0.3 bitcast_dynamic-update-slice_fusion.1
  38.0 0.2 slice_bitcast_fusion
  38.3 0.2 fusion.95
  38.5 0.6 fusion.35
  39.1 8.4 %collective-permute-start.5 = (f32[4,4,64,128]{3,2,1,0:T(8,128)S(1)}, f32[4,4,64,128]{3,2,1,0:T(8,128)S(1)}, u32[]{:S(2)}, u32[]{:S(2)}) collective-permute-start(f32[4,4,64,128]{3,2,1,0:T(8,128)S(1)} %get-tuple-element.10), channel_id=1, source_target_pairs={{0,16},{16,32},{32,48},{48,64},{64,80},{80,96},{96,112},{112,128},... | collective-permute-start | bytes 1572872 | tf_op jit(solution)/shard_map/ppermute | solution.py:143
  47.5 5.8 %collective-permute-start.6 = (f32[5,1,64,128]{3,2,1,0:T(8,128)S(1)}, f32[5,1,64,128]{3,2,1,0:T(8,128)S(1)}, u32[]{:S(2)}, u32[]{:S(2)}) collective-permute-start(f32[5,1,64,128]{3,2,1,0:T(8,128)S(1)} %get-tuple-element.27), channel_id=1, source_target_pairs={{1,0},{2,1},{3,2},{4,3},{5,4},{6,5},{7,6},{8,7},{9,8},{10,9},{11,1... | collective-permute-start | bytes 491528 | tf_op jit(solution)/shard_map/ppermute | solution.py:58
  53.4 3.2 %collective-permute-start.7 = (f32[5,1,64,128]{3,2,1,0:T(8,128)S(1)}, f32[5,1,64,128]{3,2,1,0:T(8,128)S(1)}, u32[]{:S(2)}, u32[]{:S(2)}) collective-permute-start(f32[5,1,64,128]{3,2,1,0:T(8,128)S(1)} %get-tuple-element.28), channel_id=1, source_target_pairs={{0,1},{1,2},{2,3},{3,4},{4,5},{5,6},{6,7},{7,8},{8,9},{9,10},{10,1... | collective-permute-start | bytes 491528 | tf_op jit(solution)/shard_map/ppermute | solution.py:58
  56.7 14.2 %collective-permute-done.6 = f32[5,1,64,128]{3,2,1,0:T(8,128)S(1)} collective-permute-done((f32[5,1,64,128]{3,2,1,0:T(8,128)S(1)}, f32[5,1,64,128]{3,2,1,0:T(8,128)S(1)}, u32[]{:S(2)}, u32[]{:S(2)}) %collective-permute-start.6) | collective-permute-done | bytes 163872 | tf_op jit(solution)/shard_map/ppermute | solution.py:58
  70.9 0.0 collective-permute-done.7
  70.9 0.9 %fusion.11 = f32[5,1,4,64,128]{4,3,2,1,0:T(8,128)S(1)} fusion(f32[5,4,64,128]{3,2,1,0:T(8,128)S(1)} %get-tuple-element.18, f32[5,4,64,1]{3,2,1,0:T(8,128)S(1)} %get-tuple-element.32, f32[5,4,64,1]{3,2,1,0:T(8,128)S(1)} %get-tuple-element.31, f32[5,4,1,128]{3,2,1,0:T(1,128)S(1)} %get-tuple-element.30, f32[5,4,1,128]{3,2,1,0:T(1,128)S(1)} %get-tuple-element.29, ...), kind=kLoop, calls=%fused_computation.15 | loop fusion | flops 5242880 | bytes 4290560 | tf_op jit(solution)/shard_map/stack | solution.py:92
  71.8 0.2 pad_maximum_fusion.1
  72.0 0.3 fusion.54
  72.3 0.0 collective-permute-done.5
  72.3 0.9 %fusion.72 = f32[1,4,4,64,128]{4,3,2,1,0:T(8,128)} fusion(f32[4,4,64,128]{3,2,1,0:T(8,128)S(1)} %fusion.54, f32[4,4,64,128]{3,2,1,0:T(8,128)S(1)} %collective-permute-done.5, f32[1,4,4,64,128]{4,3,2,1,0:T(8,128)S(1)} %copy-done, pred[]{:T(512)S(6)} %eq.38), kind=kLoop, calls=%fused_computation.130 | loop fusion | flops 262144 | bytes 2097153 | tf_op jit(solution)/shard_map/broadcast_in_dim | solution.py:155
  (18 shorter events, 0.3 us)
Async XLA Ops:
  0.0 12.3 %copy-start = (f32[1,4,4,64,128]{4,3,2,1,0:T(8,128)S(1)}, f32[1,4,4,64,128]{4,3,2,1,0:T(8,128)}, u32[]{:S(2)}) copy-start(f32[1,4,4,64,128]{4,3,2,1,0:T(8,128)} %param.3) | copy-start | bytes 1572868
  0.0 14.4 %copy-start.1 = (s32[4,64,128]{2,1,0:T(8,128)S(1)}, s32[4,64,128]{2,1,0:T(8,128)}, u32[]{:S(2)}) copy-start(s32[4,64,128]{2,1,0:T(8,128)} %param.4) | copy-start | bytes 393220
  0.9 11.6 %collective-permute-start = (f32[1,64,128]{2,1,0:T(8,128)S(1)}, f32[1,64,128]{2,1,0:T(8,128)S(1)}, u32[]{:S(2)}, u32[]{:S(2)}) collective-permute-start(f32[1,64,128]{2,1,0:T(8,128)S(1)} %get-tuple-element.45), channel_id=1, source_target_pairs={{1,0},{2,1},{3,2},{4,3},{5,4},{6,5},{7,6},{8,7},{9,8},{10,9},{11,1... | collective-permute-start | bytes 98312 | tf_op jit(solution)/shard_map/ppermute | solution.py:58
  7.1 7.4 %collective-permute-start.1 = (f32[1,64,128]{2,1,0:T(8,128)S(1)}, f32[1,64,128]{2,1,0:T(8,128)S(1)}, u32[]{:S(2)}, u32[]{:S(2)}) collective-permute-start(f32[1,64,128]{2,1,0:T(8,128)S(1)} %get-tuple-element.46), channel_id=1, source_target_pairs={{0,1},{1,2},{2,3},{3,4},{4,5},{5,6},{6,7},{7,8},{8,9},{9,10},{10,1... | collective-permute-start | bytes 98312 | tf_op jit(solution)/shard_map/ppermute | solution.py:58
  15.8 14.5 %collective-permute-start.3 = (f32[1,64,128]{2,1,0:T(8,128)S(1)}, f32[1,64,128]{2,1,0:T(8,128)S(1)}, u32[]{:S(2)}, u32[]{:S(2)}) collective-permute-start(f32[1,64,128]{2,1,0:T(8,128)S(1)} %get-tuple-element.53), channel_id=1, source_target_pairs={{1,0},{2,1},{3,2},{4,3},{5,4},{6,5},{7,6},{8,7},{9,8},{10,9},{11,1... | collective-permute-start | bytes 98312 | tf_op jit(solution)/shard_map/ppermute | solution.py:58
  19.9 10.4 %collective-permute-start.4 = (f32[1,64,128]{2,1,0:T(8,128)S(1)}, f32[1,64,128]{2,1,0:T(8,128)S(1)}, u32[]{:S(2)}, u32[]{:S(2)}) collective-permute-start(f32[1,64,128]{2,1,0:T(8,128)S(1)} %get-tuple-element.54), channel_id=1, source_target_pairs={{0,1},{1,2},{2,3},{3,4},{4,5},{5,6},{6,7},{7,8},{8,9},{9,10},{10,1... | collective-permute-start | bytes 98312 | tf_op jit(solution)/shard_map/ppermute | solution.py:58
  22.4 14.0 %collective-permute-start.2 = (f32[4,4,64,128]{3,2,1,0:T(8,128)S(1)}, f32[4,4,64,128]{3,2,1,0:T(8,128)S(1)}, u32[]{:S(2)}, u32[]{:S(2)}) collective-permute-start(f32[4,4,64,128]{3,2,1,0:T(8,128)S(1)} %fusion.64), channel_id=1, source_target_pairs={{0,16},{16,32},{32,48},{48,64},{64,80},{80,96},{96,112},{112,128},... | collective-permute-start | bytes 1572872 | tf_op jit(solution)/shard_map/ppermute | solution.py:129
  39.1 33.1 %collective-permute-start.5 = (f32[4,4,64,128]{3,2,1,0:T(8,128)S(1)}, f32[4,4,64,128]{3,2,1,0:T(8,128)S(1)}, u32[]{:S(2)}, u32[]{:S(2)}) collective-permute-start(f32[4,4,64,128]{3,2,1,0:T(8,128)S(1)} %get-tuple-element.10), channel_id=1, source_target_pairs={{0,16},{16,32},{32,48},{48,64},{64,80},{80,96},{96,112},{112,128},... | collective-permute-start | bytes 1572872 | tf_op jit(solution)/shard_map/ppermute | solution.py:143
  47.5 23.3 %collective-permute-start.6 = (f32[5,1,64,128]{3,2,1,0:T(8,128)S(1)}, f32[5,1,64,128]{3,2,1,0:T(8,128)S(1)}, u32[]{:S(2)}, u32[]{:S(2)}) collective-permute-start(f32[5,1,64,128]{3,2,1,0:T(8,128)S(1)} %get-tuple-element.27), channel_id=1, source_target_pairs={{1,0},{2,1},{3,2},{4,3},{5,4},{6,5},{7,6},{8,7},{9,8},{10,9},{11,1... | collective-permute-start | bytes 491528 | tf_op jit(solution)/shard_map/ppermute | solution.py:58
  53.4 17.5 %collective-permute-start.7 = (f32[5,1,64,128]{3,2,1,0:T(8,128)S(1)}, f32[5,1,64,128]{3,2,1,0:T(8,128)S(1)}, u32[]{:S(2)}, u32[]{:S(2)}) collective-permute-start(f32[5,1,64,128]{3,2,1,0:T(8,128)S(1)} %get-tuple-element.28), channel_id=1, source_target_pairs={{0,1},{1,2},{2,3},{3,4},{4,5},{5,6},{6,7},{7,8},{8,9},{9,10},{10,1... | collective-permute-start | bytes 491528 | tf_op jit(solution)/shard_map/ppermute | solution.py:58

commit v9 on v8

--- a/solution.py
+++ b/solution.py
@@ -103,6 +103,13 @@
     return start + increment(derivs, row)
 
 
+def edge_nodes(start, derivs, weights):
+    total = weights[:, 0] * derivs[0][None]
+    for j in range(1, 5):
+        total = total + weights[:, j] * derivs[j][None]
+    return start[None] + slice_len * total
+
+
 def steps(guess, fibre, labels):
     table = radau_table()
     sums = [sum(row) for row in table]
@@ -142,10 +149,14 @@
     ends1 = start1 + step1
     arrived2 = lax.ppermute(ends1, "tm", tm_pairs)
     later_start, later_derivs, ends1 = lax.optimization_barrier((start1, derivs1, ends1))
+    weights = jnp.array(table, jnp.float32)[:, :, None, None, None]
+    top = edge_nodes(later_start[0, planes - 1 :], later_derivs[:, 0, planes - 1 :], weights)
+    bottom = edge_nodes(later_start[0, :1], later_derivs[:, 0, :1], weights)
+    low2 = shift_space(top, True)
+    high2 = shift_space(bottom, False)
     nodes1 = jnp.stack([quadrature(later_start, later_derivs, table[m]) for m in range(4)] + [ends1])
 
     volts2 = nodes1[:, 0]
-    low2, high2 = halos(volts2)
     low2 = jnp.where(at_low, volts2[:, :1], low2)
     high2 = jnp.where(at_high, volts2[:, planes - 1 :], high2)
     derivs2 = rates(nodes1, laplacian(volts2, low2, high2, conduct), fast_g, slow_g, slow_tau)

time: 73.5 us -> 73.4 us (level)
  transfers between devices with their start and end apart: 8 -> 8, of which waited for: 3 -> 3; matrix products, arithmetic and copies ran while one was open for 9% -> 10% of each run, Pallas kernels for 0% -> 0%
where the time goes in v9:
time: 73.4 us; the launch traced here: 73 us
  starting transfers between devices  39.6 us (54%)
  waiting for transfers between devices  20.2 us (28%)
  other arithmetic  11.2 us (15%)
  local copies, waits for them, and re-layouts  1.6 us (2%)
    ppermute x6, starting transfers between devices, shift_space(): return lax.ppermute(block, 'space', pairs)  23.2 us
    ppermute x6, waiting for transfers between devices, shift_space(): return lax.ppermute(block, 'space', pairs)  15.7 us
    ppermute x1, starting transfers between devices, steps(): arrived2 = lax.ppermute(ends1, 'tm', tm_pairs)  8.4 us
    ppermute x1, starting transfers between devices, steps(): arrived1 = lax.ppermute(ends0, 'tm', tm_pairs)  7.93 us
    ppermute x1, waiting for transfers between devices, steps(): arrived1 = lax.ppermute(ends0, 'tm', tm_pairs)  4.55 us
    another operation x4, other arithmetic, rates(): return jnp.stack([dvolt, dact, dinact, dslow], axis=-4)  2.09 us
    div x2, other arithmetic, rates(): dact = (jax.nn.sigmoid(8.0 * (volt - 0.2)) - act) / 0.5  1.78 us
    unnamed x15, other arithmetic  1.73 us
  transfers between devices with their start and end apart: 8, of which 3 were waited for; matrix products, arithmetic and copies ran while one was open for 10% of the time, Pallas kernels for 0%

profile of v9, /device:TPU:27, one launch (start us, length us, event | category | flops | bytes accessed | tf_op | source)
XLA Modules:
  0.0 73.0 jit_solution(8620335235345023539)
XLA Ops:
  0.0 0.0 copy-start
  0.0 0.0 copy-start.1
  0.0 0.8 %slice_bitcast_fusion.15 = (f32[1,64,128]{2,1,0:T(8,128)S(1)}, f32[1,64,128]{2,1,0:T(8,128)S(1)}) fusion(f32[1,4,4,64,128]{4,3,2,1,0:T(8,128)} %param.4), kind=kLoop, calls=%fused_computation.199 | loop fusion | bytes 131072 | tf_op jit(solution)/shard_map/slice | solution.py:132
  0.9 6.2 %collective-permute-start = (f32[1,64,128]{2,1,0:T(8,128)S(1)}, f32[1,64,128]{2,1,0:T(8,128)S(1)}, u32[]{:S(2)}, u32[]{:S(2)}) collective-permute-start(f32[1,64,128]{2,1,0:T(8,128)S(1)} %get-tuple-element.55), channel_id=1, source_target_pairs={{1,0},{2,1},{3,2},{4,3},{5,4},{6,5},{7,6},{8,7},{9,8},{10,9},{11,1... | collective-permute-start | bytes 98312 | tf_op jit(solution)/shard_map/ppermute | solution.py:58
  7.1 1.9 %collective-permute-start.1 = (f32[1,64,128]{2,1,0:T(8,128)S(1)}, f32[1,64,128]{2,1,0:T(8,128)S(1)}, u32[]{:S(2)}, u32[]{:S(2)}) collective-permute-start(f32[1,64,128]{2,1,0:T(8,128)S(1)} %get-tuple-element.56), channel_id=1, source_target_pairs={{0,1},{1,2},{2,3},{3,4},{4,5},{5,6},{6,7},{7,8},{8,9},{9,10},{10,1... | collective-permute-start | bytes 98312 | tf_op jit(solution)/shard_map/ppermute | solution.py:58
  9.0 1.2 %fusion.91 = (f32[1,4,64,128]{3,2,1,0:T(8,128)S(1)}, f32[1,1,4,64,128]{4,3,2,0,1:T(8,128)S(1)}, f32[1,1,4,64,128]{4,3,2,1,0:T(8,128)S(1)}, f32[4,64,128]{2,1,0:T(8,128)S(1)}) fusion(f32[1,4,4,64,128]{4,3,2,1,0:T(8,128)} %param.4), kind=kLoop, calls=%fused_computation.204 | loop fusion | flops 655360 | bytes 917504 | tf_op jit(solution)/shard_map/div | solution.py:87
  10.2 0.1 fusion.99
  10.3 1.0 %select_add_fusion.1 = (f32[4,64,128]{2,1,0:T(8,128)S(1)}, pred[4,64,128]{2,1,0:T(8,128)(4,1)S(1)}, pred[4,64,128]{2,1,0:T(8,128)(4,1)S(1)}, pred[4,64,128]{2,1,0:T(8,128)(4,1)S(1)}, pred[4,64,128]{2,1,0:T(8,128)(4,1)S(1)}) fusion(s32[4,64,128]{2,1,0:T(8,128)} %param.6), kind=kLoop, calls=%fused_computation.168 | loop fusion | flops 360448 | bytes 393216 | tf_op jit(solution)/shard_map/add | solution.py:34
  11.3 1.0 %select_add_fusion.4 = (f32[4,64,128]{2,1,0:T(8,128)S(1)}, f32[4,64,128]{2,1,0:T(8,128)S(1)}, f32[4,64,128]{2,1,0:T(8,128)S(1)}) fusion(s32[4,64,128]{2,1,0:T(8,128)} %param.5), kind=kLoop, calls=%fused_computation.171 | loop fusion | flops 294912 | bytes 524288 | tf_op jit(solution)/shard_map/add | solution.py:119
  12.3 0.0 copy-done
  12.3 0.2 select_add_fusion
  12.4 0.0 collective-permute-done
  12.5 2.0 %collective-permute-done.1 = f32[1,64,128]{2,1,0:T(8,128)S(1)} collective-permute-done((f32[1,64,128]{2,1,0:T(8,128)S(1)}, f32[1,64,128]{2,1,0:T(8,128)S(1)}, u32[]{:S(2)}, u32[]{:S(2)}) %collective-permute-start.1) | collective-permute-done | bytes 32800 | tf_op jit(solution)/shard_map/ppermute | solution.py:58
  14.4 0.0 copy-done.1
  14.5 0.3 fusion.77
  14.8 0.1 fusion.67
  14.9 0.1 fusion.68
  14.9 0.1 fusion.69
  15.0 0.1 fusion.70
  15.1 0.1 fusion.66
  15.2 0.6 slice_bitcast_fusion.1
  15.8 4.1 %collective-permute-start.3 = (f32[1,64,128]{2,1,0:T(8,128)S(1)}, f32[1,64,128]{2,1,0:T(8,128)S(1)}, u32[]{:S(2)}, u32[]{:S(2)}) collective-permute-start(f32[1,64,128]{2,1,0:T(8,128)S(1)} %get-tuple-element.63), channel_id=1, source_target_pairs={{1,0},{2,1},{3,2},{4,3},{5,4},{6,5},{7,6},{8,7},{9,8},{10,9},{11,1... | collective-permute-start | bytes 98312 | tf_op jit(solution)/shard_map/ppermute | solution.py:58
  19.9 1.9 %collective-permute-start.4 = (f32[1,64,128]{2,1,0:T(8,128)S(1)}, f32[1,64,128]{2,1,0:T(8,128)S(1)}, u32[]{:S(2)}, u32[]{:S(2)}) collective-permute-start(f32[1,64,128]{2,1,0:T(8,128)S(1)} %get-tuple-element.64), channel_id=1, source_target_pairs={{0,1},{1,2},{2,3},{3,4},{4,5},{5,6},{6,7},{7,8},{8,9},{9,10},{10,1... | collective-permute-start | bytes 98312 | tf_op jit(solution)/shard_map/ppermute | solution.py:58
  21.8 0.2 fusion.96
  22.1 0.2 fusion.50
  22.3 0.1 fusion.64
  22.4 7.9 %collective-permute-start.2 = (f32[4,4,64,128]{3,2,1,0:T(8,128)S(1)}, f32[4,4,64,128]{3,2,1,0:T(8,128)S(1)}, u32[]{:S(2)}, u32[]{:S(2)}) collective-permute-start(f32[4,4,64,128]{3,2,1,0:T(8,128)S(1)} %fusion.64), channel_id=1, source_target_pairs={{0,16},{16,32},{32,48},{48,64},{64,80},{80,96},{96,112},{112,128},... | collective-permute-start | bytes 1572872 | tf_op jit(solution)/shard_map/ppermute | solution.py:136
  30.3 0.0 collective-permute-done.3
  30.3 0.0 collective-permute-done.4
  30.5 0.9 %fusion.5 = f32[5,1,4,64,128]{4,3,2,1,0:T(8,128)S(1)} fusion(f32[5,4,64,128]{3,2,1,0:T(8,128)S(1)} %get-tuple-element.32, f32[5,4,64,1]{3,2,1,0:T(8,128)S(1)} %get-tuple-element.46, f32[5,4,64,1]{3,2,1,0:T(8,128)S(1)} %get-tuple-element.45, f32[5,4,1,128]{3,2,1,0:T(1,128)S(1)} %get-tuple-element.44, f32[5,4,1,128]{3,2,1,0:T(1,128)S(1)} %get-tuple-element.43, ...), kind=kLoop, calls=%fused_computation.9 | loop fusion | flops 5242880 | bytes 4290560 | tf_op jit(solution)/shard_map/stack | solution.py:92
  31.4 0.2 pad_maximum_fusion
  31.6 0.3 fusion.60
  31.9 4.5 %collective-permute-done.2 = f32[4,4,64,128]{3,2,1,0:T(8,128)S(1)} collective-permute-done((f32[4,4,64,128]{3,2,1,0:T(8,128)S(1)}, f32[4,4,64,128]{3,2,1,0:T(8,128)S(1)}, u32[]{:S(2)}, u32[]{:S(2)}) %collective-permute-start.2) | collective-permute-done | bytes 524320 | tf_op jit(solution)/shard_map/ppermute | solution.py:136
  36.4 0.1 fusion.92
  36.6 0.3 bitcast_dynamic-update-slice_fusion.4
  37.0 0.3 bitcast_dynamic-update-slice_fusion.3
  37.3 0.3 bitcast_dynamic-update-slice_fusion.2
  37.6 0.3 bitcast_dynamic-update-slice_fusion.1
  38.0 0.0 copy-start.2
  38.1 0.0 copy-start.3
  38.1 0.0 copy-start.4
  38.1 0.0 copy-start.5
  38.1 0.0 copy-start.6
  38.1 0.2 slice_bitcast_fusion
  38.3 0.6 fusion.35
  39.0 8.4 %collective-permute-start.5 = (f32[4,4,64,128]{3,2,1,0:T(8,128)S(1)}, f32[4,4,64,128]{3,2,1,0:T(8,128)S(1)}, u32[]{:S(2)}, u32[]{:S(2)}) collective-permute-start(f32[4,4,64,128]{3,2,1,0:T(8,128)S(1)} %get-tuple-element.10), channel_id=1, source_target_pairs={{0,16},{16,32},{32,48},{48,64},{64,80},{80,96},{96,112},{112,128},... | collective-permute-start | bytes 1572872 | tf_op jit(solution)/shard_map/ppermute | solution.py:150
  47.4 0.0 copy-done.2
  47.4 0.0 copy-done.3
  47.4 0.0 copy-done.4
  47.4 0.0 copy-done.5
  47.4 0.0 copy-done.6
  47.4 0.2 multiply_add_fusion.1
  47.6 5.8 %collective-permute-start.6 = (f32[5,1,64,128]{3,2,1,0:T(8,128)S(1)}, f32[5,1,64,128]{3,2,1,0:T(8,128)S(1)}, u32[]{:S(2)}, u32[]{:S(2)}) collective-permute-start(f32[5,1,64,128]{3,2,1,0:T(8,128)S(1)} %get-tuple-element.69), channel_id=1, source_target_pairs={{1,0},{2,1},{3,2},{4,3},{5,4},{6,5},{7,6},{8,7},{9,8},{10,9},{11,1... | collective-permute-start | bytes 491528 | tf_op jit(solution)/shard_map/ppermute | solution.py:58
  53.5 3.2 %collective-permute-start.7 = (f32[5,1,64,128]{3,2,1,0:T(8,128)S(1)}, f32[5,1,64,128]{3,2,1,0:T(8,128)S(1)}, u32[]{:S(2)}, u32[]{:S(2)}) collective-permute-start(f32[5,1,64,128]{3,2,1,0:T(8,128)S(1)} %get-tuple-element.70), channel_id=1, source_target_pairs={{0,1},{1,2},{2,3},{3,4},{4,5},{5,6},{6,7},{7,8},{8,9},{9,10},{10,1... | collective-permute-start | bytes 491528 | tf_op jit(solution)/shard_map/ppermute | solution.py:58
  56.7 0.2 fusion.94
  57.0 13.7 %collective-permute-done.6 = f32[5,1,64,128]{3,2,1,0:T(8,128)S(1)} collective-permute-done((f32[5,1,64,128]{3,2,1,0:T(8,128)S(1)}, f32[5,1,64,128]{3,2,1,0:T(8,128)S(1)}, u32[]{:S(2)}, u32[]{:S(2)}) %collective-permute-start.6) | collective-permute-done | bytes 163872 | tf_op jit(solution)/shard_map/ppermute | solution.py:58
  70.7 0.0 collective-permute-done.7
  70.8 0.9 %fusion.11 = f32[5,1,4,64,128]{4,3,2,1,0:T(8,128)S(1)} fusion(f32[5,4,64,128]{3,2,1,0:T(8,128)S(1)} %get-tuple-element.28, f32[5,4,64,1]{3,2,1,0:T(8,128)S(1)} %get-tuple-element.40, f32[5,4,64,1]{3,2,1,0:T(8,128)S(1)} %get-tuple-element.39, f32[5,4,1,128]{3,2,1,0:T(1,128)S(1)} %get-tuple-element.38, f32[5,4,1,128]{3,2,1,0:T(1,128)S(1)} %get-tuple-element.37, ...), kind=kLoop, calls=%fused_computation.15 | loop fusion | flops 5242880 | bytes 4290560 | tf_op jit(solution)/shard_map/stack | solution.py:92
  71.6 0.2 pad_maximum_fusion.1
  71.8 0.3 fusion.54
  72.1 0.0 collective-permute-done.5
  72.1 0.9 %fusion.72 = f32[1,4,4,64,128]{4,3,2,1,0:T(8,128)} fusion(f32[4,4,64,128]{3,2,1,0:T(8,128)S(1)} %fusion.54, f32[4,4,64,128]{3,2,1,0:T(8,128)S(1)} %collective-permute-done.5, f32[1,4,4,64,128]{4,3,2,1,0:T(8,128)S(1)} %copy-done, pred[]{:T(512)S(6)} %eq.38), kind=kLoop, calls=%fused_computation.130 | loop fusion | flops 262144 | bytes 2097153 | tf_op jit(solution)/shard_map/broadcast_in_dim | solution.py:166
  (19 shorter events, 0.3 us)
Async XLA Ops:
  0.0 12.3 %copy-start = (f32[1,4,4,64,128]{4,3,2,1,0:T(8,128)S(1)}, f32[1,4,4,64,128]{4,3,2,1,0:T(8,128)}, u32[]{:S(2)}) copy-start(f32[1,4,4,64,128]{4,3,2,1,0:T(8,128)} %param.4) | copy-start | bytes 1572868
  0.0 14.4 %copy-start.1 = (s32[4,64,128]{2,1,0:T(8,128)S(1)}, s32[4,64,128]{2,1,0:T(8,128)}, u32[]{:S(2)}) copy-start(s32[4,64,128]{2,1,0:T(8,128)} %param.5) | copy-start | bytes 393220
  0.9 11.6 %collective-permute-start = (f32[1,64,128]{2,1,0:T(8,128)S(1)}, f32[1,64,128]{2,1,0:T(8,128)S(1)}, u32[]{:S(2)}, u32[]{:S(2)}) collective-permute-start(f32[1,64,128]{2,1,0:T(8,128)S(1)} %get-tuple-element.55), channel_id=1, source_target_pairs={{1,0},{2,1},{3,2},{4,3},{5,4},{6,5},{7,6},{8,7},{9,8},{10,9},{11,1... | collective-permute-start | bytes 98312 | tf_op jit(solution)/shard_map/ppermute | solution.py:58
  7.1 7.4 %collective-permute-start.1 = (f32[1,64,128]{2,1,0:T(8,128)S(1)}, f32[1,64,128]{2,1,0:T(8,128)S(1)}, u32[]{:S(2)}, u32[]{:S(2)}) collective-permute-start(f32[1,64,128]{2,1,0:T(8,128)S(1)} %get-tuple-element.56), channel_id=1, source_target_pairs={{0,1},{1,2},{2,3},{3,4},{4,5},{5,6},{6,7},{7,8},{8,9},{9,10},{10,1... | collective-permute-start | bytes 98312 | tf_op jit(solution)/shard_map/ppermute | solution.py:58
  15.8 14.5 %collective-permute-start.3 = (f32[1,64,128]{2,1,0:T(8,128)S(1)}, f32[1,64,128]{2,1,0:T(8,128)S(1)}, u32[]{:S(2)}, u32[]{:S(2)}) collective-permute-start(f32[1,64,128]{2,1,0:T(8,128)S(1)} %get-tuple-element.63), channel_id=1, source_target_pairs={{1,0},{2,1},{3,2},{4,3},{5,4},{6,5},{7,6},{8,7},{9,8},{10,9},{11,1... | collective-permute-start | bytes 98312 | tf_op jit(solution)/shard_map/ppermute | solution.py:58
  19.9 10.4 %collective-permute-start.4 = (f32[1,64,128]{2,1,0:T(8,128)S(1)}, f32[1,64,128]{2,1,0:T(8,128)S(1)}, u32[]{:S(2)}, u32[]{:S(2)}) collective-permute-start(f32[1,64,128]{2,1,0:T(8,128)S(1)} %get-tuple-element.64), channel_id=1, source_target_pairs={{0,1},{1,2},{2,3},{3,4},{4,5},{5,6},{6,7},{7,8},{8,9},{9,10},{10,1... | collective-permute-start | bytes 98312 | tf_op jit(solution)/shard_map/ppermute | solution.py:58
  22.4 14.0 %collective-permute-start.2 = (f32[4,4,64,128]{3,2,1,0:T(8,128)S(1)}, f32[4,4,64,128]{3,2,1,0:T(8,128)S(1)}, u32[]{:S(2)}, u32[]{:S(2)}) collective-permute-start(f32[4,4,64,128]{3,2,1,0:T(8,128)S(1)} %fusion.64), channel_id=1, source_target_pairs={{0,16},{16,32},{32,48},{48,64},{64,80},{80,96},{96,112},{112,128},... | collective-permute-start | bytes 1572872 | tf_op jit(solution)/shard_map/ppermute | solution.py:136
  38.0 9.3 %copy-start.2 = (f32[5]{0:T(128)S(1)}, f32[5]{0:T(128)}, u32[]{:S(2)}) copy-start(f32[5]{0:T(128)} %constant.178) | copy-start | bytes 64
  38.1 9.3 %copy-start.3 = (f32[5]{0:T(128)S(1)}, f32[5]{0:T(128)}, u32[]{:S(2)}) copy-start(f32[5]{0:T(128)} %constant.180) | copy-start | bytes 64
  38.1 9.3 %copy-start.4 = (f32[5]{0:T(128)S(1)}, f32[5]{0:T(128)}, u32[]{:S(2)}) copy-start(f32[5]{0:T(128)} %constant.182) | copy-start | bytes 64
  38.1 9.3 %copy-start.5 = (f32[5]{0:T(128)S(1)}, f32[5]{0:T(128)}, u32[]{:S(2)}) copy-start(f32[5]{0:T(128)} %constant.184) | copy-start | bytes 64
  38.1 9.3 %copy-start.6 = (f32[5]{0:T(128)S(1)}, f32[5]{0:T(128)}, u32[]{:S(2)}) copy-start(f32[5]{0:T(128)} %constant.186) | copy-start | bytes 64
  39.0 33.1 %collective-permute-start.5 = (f32[4,4,64,128]{3,2,1,0:T(8,128)S(1)}, f32[4,4,64,128]{3,2,1,0:T(8,128)S(1)}, u32[]{:S(2)}, u32[]{:S(2)}) collective-permute-start(f32[4,4,64,128]{3,2,1,0:T(8,128)S(1)} %get-tuple-element.10), channel_id=1, source_target_pairs={{0,16},{16,32},{32,48},{48,64},{64,80},{80,96},{96,112},{112,128},... | collective-permute-start | bytes 1572872 | tf_op jit(solution)/shard_map/ppermute | solution.py:150
  47.6 23.1 %collective-permute-start.6 = (f32[5,1,64,128]{3,2,1,0:T(8,128)S(1)}, f32[5,1,64,128]{3,2,1,0:T(8,128)S(1)}, u32[]{:S(2)}, u32[]{:S(2)}) collective-permute-start(f32[5,1,64,128]{3,2,1,0:T(8,128)S(1)} %get-tuple-element.69), channel_id=1, source_target_pairs={{1,0},{2,1},{3,2},{4,3},{5,4},{6,5},{7,6},{8,7},{9,8},{10,9},{11,1... | collective-permute-start | bytes 491528 | tf_op jit(solution)/shard_map/ppermute | solution.py:58
  53.5 17.2 %collective-permute-start.7 = (f32[5,1,64,128]{3,2,1,0:T(8,128)S(1)}, f32[5,1,64,128]{3,2,1,0:T(8,128)S(1)}, u32[]{:S(2)}, u32[]{:S(2)}) collective-permute-start(f32[5,1,64,128]{3,2,1,0:T(8,128)S(1)} %get-tuple-element.70), channel_id=1, source_target_pairs={{0,1},{1,2},{2,3},{3,4},{4,5},{5,6},{6,7},{7,8},{8,9},{9,10},{10,1... | collective-permute-start | bytes 491528 | tf_op jit(solution)/shard_map/ppermute | solution.py:58

commit v10 on v9

--- a/solution.py
+++ b/solution.py
@@ -99,10 +99,6 @@
     return slice_len * total
 
 
-def quadrature(start, derivs, row):
-    return start + increment(derivs, row)
-
-
 def edge_nodes(start, derivs, weights):
     total = weights[:, 0] * derivs[0][None]
     for j in range(1, 5):
@@ -133,6 +129,7 @@
     high0 = jnp.where(at_high, volts0[planes - 1 :], high0)
     derivs0 = rates(start0, laplacian(volts0, low0, high0, conduct), fast_g, slow_g, slow_tau)
     ends0 = start0 + slice_len * (sums[4] * derivs0)
+    derivs0, ends0 = lax.optimization_barrier((derivs0, ends0))
     arrived1 = lax.ppermute(ends0, "tm", tm_pairs)
 
     dv = derivs0[0]
@@ -154,7 +151,7 @@
     bottom = edge_nodes(later_start[0, :1], later_derivs[:, 0, :1], weights)
     low2 = shift_space(top, True)
     high2 = shift_space(bottom, False)
-    nodes1 = jnp.stack([quadrature(later_start, later_derivs, table[m]) for m in range(4)] + [ends1])
+    nodes1 = edge_nodes(later_start, later_derivs, weights[..., None])
 
     volts2 = nodes1[:, 0]
     low2 = jnp.where(at_low, volts2[:, :1], low2)

time: 73.4 us -> 74.4 us (1.014)
    unnamed x15 -> x11, other arithmetic: 1.73 us -> 0.33 us
    div x2 -> x1, other arithmetic: 1.78 us -> 0.61 us  [rates(): dact = (jax.nn.sigmoid(8.0 * (volt - 0.2)) - act) / 0.5]
    squeeze x0 -> x1, other arithmetic: none -> 1.17 us  [steps(): volts0 = start0[0]]
    add x1 -> x2, other arithmetic: 0.23 us -> 1.22 us  [edge_nodes(): return start[None] + slice_len * total]
    add x2, other arithmetic: 1.16 us -> 2.13 us  [lookup(): total + jnp.where(labels == level, values[level], 0.0).astype(jnp.float32)]
    another operation x4 -> x5, other arithmetic: 2.09 us -> 2.38 us  [rates(): return jnp.stack([dvolt, dact, dinact, dslow], axis=-4)]
  transfers between devices with their start and end apart: 8 -> 8, of which waited for: 3 -> 3; matrix products, arithmetic and copies ran while one was open for 10% -> 12% of each run, Pallas kernels for 0% -> 0%
where the time goes in v10:
time: 74.4 us; the launch traced here: 74.1 us
  starting transfers between devices  39.6 us (53%)
  waiting for transfers between devices  20.2 us (27%)
  other arithmetic  11.7 us (16%)
  local copies, waits for them, and re-layouts  2.18 us (3%)
    ppermute x6, starting transfers between devices, shift_space(): return lax.ppermute(block, 'space', pairs)  23.6 us
    ppermute x6, waiting for transfers between devices, shift_space(): return lax.ppermute(block, 'space', pairs)  15.6 us
    ppermute x1, starting transfers between devices, steps(): arrived2 = lax.ppermute(ends1, 'tm', tm_pairs)  8.4 us
    ppermute x1, starting transfers between devices, steps(): arrived1 = lax.ppermute(ends0, 'tm', tm_pairs)  7.52 us
    ppermute x1, waiting for transfers between devices, steps(): arrived1 = lax.ppermute(ends0, 'tm', tm_pairs)  4.53 us
    another operation x5, other arithmetic, rates(): return jnp.stack([dvolt, dact, dinact, dslow], axis=-4)  2.38 us
    add x2, other arithmetic, lookup(): total + jnp.where(labels == level, values[level], 0.0).astype(jnp.float32)  2.13 us
  transfers between devices with their start and end apart: 8, of which 3 were waited for; matrix products, arithmetic and copies ran while one was open for 12% of the time, Pallas kernels for 0%

profile of v10, /device:TPU:27, one launch (start us, length us, event | category | flops | bytes accessed | tf_op | source)
XLA Modules:
  0.0 74.1 jit_solution(17645894928856895586)
XLA Ops:
  0.0 0.0 copy-start
  0.0 0.0 copy-start.1
  0.0 0.8 %slice_bitcast_fusion.22 = (f32[1,64,128]{2,1,0:T(8,128)S(1)}, f32[1,64,128]{2,1,0:T(8,128)S(1)}) fusion(f32[1,4,4,64,128]{4,3,2,1,0:T(8,128)} %param.4), kind=kLoop, calls=%fused_computation.198 | loop fusion | bytes 131072 | tf_op jit(solution)/shard_map/slice | solution.py:128
  0.9 6.2 %collective-permute-start = (f32[1,64,128]{2,1,0:T(8,128)S(1)}, f32[1,64,128]{2,1,0:T(8,128)S(1)}, u32[]{:S(2)}, u32[]{:S(2)}) collective-permute-start(f32[1,64,128]{2,1,0:T(8,128)S(1)} %get-tuple-element.62), channel_id=1, source_target_pairs={{1,0},{2,1},{3,2},{4,3},{5,4},{6,5},{7,6},{8,7},{9,8},{10,9},{11,1... | collective-permute-start | bytes 98312 | tf_op jit(solution)/shard_map/ppermute | solution.py:58
  7.1 1.9 %collective-permute-start.1 = (f32[1,64,128]{2,1,0:T(8,128)S(1)}, f32[1,64,128]{2,1,0:T(8,128)S(1)}, u32[]{:S(2)}, u32[]{:S(2)}) collective-permute-start(f32[1,64,128]{2,1,0:T(8,128)S(1)} %get-tuple-element.63), channel_id=1, source_target_pairs={{0,1},{1,2},{2,3},{3,4},{4,5},{5,6},{6,7},{7,8},{8,9},{9,10},{10,1... | collective-permute-start | bytes 98312 | tf_op jit(solution)/shard_map/ppermute | solution.py:58
  9.0 1.2 %slice_bitcast_fusion.7 = (f32[4,64,128]{2,1,0:T(8,128)S(1)}, f32[1,4,64,128]{3,2,1,0:T(8,128)S(1)}, f32[1,4,64,128]{3,2,1,0:T(8,128)S(1)}) fusion(f32[1,4,4,64,128]{4,3,2,1,0:T(8,128)} %param.4), kind=kLoop, calls=%fused_computation.169 | loop fusion | flops 655360 | bytes 786432 | tf_op jit(solution)/shard_map/squeeze | solution.py:124
  10.2 0.1 fusion.91
  10.3 1.0 %select_add_fusion.1 = (f32[4,64,128]{2,1,0:T(8,128)S(1)}, pred[4,64,128]{2,1,0:T(8,128)(4,1)S(1)}, pred[4,64,128]{2,1,0:T(8,128)(4,1)S(1)}, pred[4,64,128]{2,1,0:T(8,128)(4,1)S(1)}, pred[4,64,128]{2,1,0:T(8,128)(4,1)S(1)}) fusion(s32[4,64,128]{2,1,0:T(8,128)} %param.6), kind=kLoop, calls=%fused_computation.165 | loop fusion | flops 360448 | bytes 393216 | tf_op jit(solution)/shard_map/add | solution.py:34
  11.3 1.0 %select_add_fusion.4 = (f32[4,64,128]{2,1,0:T(8,128)S(1)}, f32[4,64,128]{2,1,0:T(8,128)S(1)}, f32[4,64,128]{2,1,0:T(8,128)S(1)}) fusion(s32[4,64,128]{2,1,0:T(8,128)} %param.5), kind=kLoop, calls=%fused_computation.168 | loop fusion | flops 294912 | bytes 524288 | tf_op jit(solution)/shard_map/add | solution.py:115
  12.3 1.1 %select_add_fusion = (f32[4,64,128]{2,1,0:T(8,128)S(1)}, f32[4,64,128]{2,1,0:T(8,128)S(1)}, f32[1,4,64,128]{3,2,1,0:T(8,128)S(1)}) fusion(pred[4,64,128]{2,1,0:T(8,128)(4,1)S(1)} %get-tuple-element.19, pred[4,64,128]{2,1,0:T(8,128)(4,1)S(1)} %get-tuple-element.18, pred[4,64,128]{2,1,0:T(8,128)(4,1)S(1)} %get-tuple-element.17, ...), kind=kLoop, calls=%fused_computation.164 | loop fusion | flops 720896 | bytes 786432 | tf_op jit(solution)/shard_map/add | solution.py:34
  13.4 0.0 collective-permute-done
  13.4 1.0 %collective-permute-done.1 = f32[1,64,128]{2,1,0:T(8,128)S(1)} collective-permute-done((f32[1,64,128]{2,1,0:T(8,128)S(1)}, f32[1,64,128]{2,1,0:T(8,128)S(1)}, u32[]{:S(2)}, u32[]{:S(2)}) %collective-permute-start.1) | collective-permute-done | bytes 32800 | tf_op jit(solution)/shard_map/ppermute | solution.py:58
  14.4 0.0 copy-done
  14.4 0.0 copy-done.1
  14.5 0.3 fusion.71
  14.8 0.1 bitcast_add_fusion.8
  14.9 0.1 bitcast_dynamic-update-slice_fusion.4
  14.9 5.1 %collective-permute-start.3 = (f32[1,64,128]{2,1,0:T(8,128)S(1)}, f32[1,64,128]{2,1,0:T(8,128)S(1)}, u32[]{:S(2)}, u32[]{:S(2)}) collective-permute-start(f32[1,64,128]{2,1,0:T(8,128)S(1)} %get-tuple-element.56), channel_id=1, source_target_pairs={{1,0},{2,1},{3,2},{4,3},{5,4},{6,5},{7,6},{8,7},{9,8},{10,9},{11,1... | collective-permute-start | bytes 98312 | tf_op jit(solution)/shard_map/ppermute | solution.py:58
  20.0 0.1 bitcast_dynamic-update-slice_fusion.3
  20.1 0.1 bitcast_dynamic-update-slice_fusion.2
  20.2 0.1 bitcast_dynamic-update-slice_fusion.1
  20.2 0.1 bitcast_dynamic-update-slice_fusion
  20.3 0.6 fusion.37
  20.9 0.2 slice_bitcast_fusion.1
  21.2 0.2 fusion.89
  21.4 1.9 %collective-permute-start.4 = (f32[1,64,128]{2,1,0:T(8,128)S(1)}, f32[1,64,128]{2,1,0:T(8,128)S(1)}, u32[]{:S(2)}, u32[]{:S(2)}) collective-permute-start(f32[1,64,128]{2,1,0:T(8,128)S(1)} %get-tuple-element.57), channel_id=1, source_target_pairs={{0,1},{1,2},{2,3},{3,4},{4,5},{5,6},{6,7},{7,8},{8,9},{9,10},{10,1... | collective-permute-start | bytes 98312 | tf_op jit(solution)/shard_map/ppermute | solution.py:58
  23.4 7.5 %collective-permute-start.2 = (f32[4,4,64,128]{3,2,1,0:T(8,128)S(1)}, f32[4,4,64,128]{3,2,1,0:T(8,128)S(1)}, u32[]{:S(2)}, u32[]{:S(2)}) collective-permute-start(f32[4,4,64,128]{3,2,1,0:T(8,128)S(1)} %get-tuple-element.9), channel_id=1, source_target_pairs={{0,16},{16,32},{32,48},{48,64},{64,80},{80,96},{96,112},{112,128},... | collective-permute-start | bytes 1572872 | tf_op jit(solution)/shard_map/ppermute | solution.py:133
  30.9 0.0 collective-permute-done.3
  30.9 0.0 collective-permute-done.4
  31.1 0.9 %fusion.5 = f32[5,1,4,64,128]{4,3,2,1,0:T(8,128)S(1)} fusion(f32[5,4,64,128]{3,2,1,0:T(8,128)S(1)} %get-tuple-element.38, f32[5,4,64,1]{3,2,1,0:T(8,128)S(1)} %get-tuple-element.53, f32[5,4,64,1]{3,2,1,0:T(8,128)S(1)} %get-tuple-element.52, f32[5,4,1,128]{3,2,1,0:T(1,128)S(1)} %get-tuple-element.51, f32[5,4,1,128]{3,2,1,0:T(1,128)S(1)} %get-tuple-element.50, ...), kind=kLoop, calls=%fused_computation.10 | loop fusion | flops 5242880 | bytes 4290560 | tf_op jit(solution)/shard_map/stack | solution.py:92
  32.0 0.2 pad_maximum_fusion
  32.2 0.3 fusion.60
  32.5 4.5 %collective-permute-done.2 = f32[4,4,64,128]{3,2,1,0:T(8,128)S(1)} collective-permute-done((f32[4,4,64,128]{3,2,1,0:T(8,128)S(1)}, f32[4,4,64,128]{3,2,1,0:T(8,128)S(1)}, u32[]{:S(2)}, u32[]{:S(2)}) %collective-permute-start.2) | collective-permute-done | bytes 524320 | tf_op jit(solution)/shard_map/ppermute | solution.py:133
  37.0 0.1 fusion.85
  37.2 0.0 copy-start.2
  37.2 0.0 copy-start.3
  37.2 0.0 copy-start.4
  37.2 0.0 copy-start.5
  37.2 0.0 copy-start.6
  37.2 0.2 slice_bitcast_fusion.6
  37.4 0.4 copy-done.2
  37.8 0.0 copy-done.3
  37.8 0.0 copy-done.4
  37.8 0.0 copy-done.5
  37.9 0.0 copy-done.6
  37.9 1.0 %multiply_add_fusion = f32[5,4,4,64,128]{4,3,2,0,1:T(8,128)S(1)} fusion(f32[4,4,64,128]{3,2,1,0:T(8,128)S(1)} %get-tuple-element.34, f32[5]{0:T(128)S(1)} %copy-done.6, f32[4,4,64,128]{3,2,1,0:T(8,128)S(1)} %get-tuple-element.35, f32[5]{0:T(128)S(1)} %copy-done.5, f32[4,4,64,128]{3,2,1,0:T(8,128)S(1)} %get-tuple-element.36, f32[5]{0:T(128)S(1)} %copy-done.4, ...), kind=kLoop, calls=%fused_computation.2 | loop fusion | flops 7208960 | bytes 5767268 | tf_op jit(solution)/shard_map/add | solution.py:106
  38.9 0.6 slice_bitcast_fusion
  39.5 0.2 fusion.33
  39.7 8.4 %collective-permute-start.5 = (f32[4,4,64,128]{3,2,1,0:T(8,128)S(1)}, f32[4,4,64,128]{3,2,1,0:T(8,128)S(1)}, u32[]{:S(2)}, u32[]{:S(2)}) collective-permute-start(f32[4,4,64,128]{3,2,1,0:T(8,128)S(1)} %get-tuple-element.13), channel_id=1, source_target_pairs={{0,16},{16,32},{32,48},{48,64},{64,80},{80,96},{96,112},{112,128},... | collective-permute-start | bytes 1572872 | tf_op jit(solution)/shard_map/ppermute | solution.py:147
  48.1 0.2 multiply_add_fusion.2
  48.3 6.2 %collective-permute-start.6 = (f32[5,1,64,128]{3,2,1,0:T(8,128)S(1)}, f32[5,1,64,128]{3,2,1,0:T(8,128)S(1)}, u32[]{:S(2)}, u32[]{:S(2)}) collective-permute-start(f32[5,1,64,128]{3,2,1,0:T(8,128)S(1)} %get-tuple-element.77), channel_id=1, source_target_pairs={{1,0},{2,1},{3,2},{4,3},{5,4},{6,5},{7,6},{8,7},{9,8},{10,9},{11,1... | collective-permute-start | bytes 491528 | tf_op jit(solution)/shard_map/ppermute | solution.py:58
  54.6 2.3 %collective-permute-start.7 = (f32[5,1,64,128]{3,2,1,0:T(8,128)S(1)}, f32[5,1,64,128]{3,2,1,0:T(8,128)S(1)}, u32[]{:S(2)}, u32[]{:S(2)}) collective-permute-start(f32[5,1,64,128]{3,2,1,0:T(8,128)S(1)} %get-tuple-element.78), channel_id=1, source_target_pairs={{0,1},{1,2},{2,3},{3,4},{4,5},{5,6},{6,7},{7,8},{8,9},{9,10},{10,1... | collective-permute-start | bytes 491528 | tf_op jit(solution)/shard_map/ppermute | solution.py:58
  56.9 0.2 fusion.87
  57.2 14.6 %collective-permute-done.6 = f32[5,1,64,128]{3,2,1,0:T(8,128)S(1)} collective-permute-done((f32[5,1,64,128]{3,2,1,0:T(8,128)S(1)}, f32[5,1,64,128]{3,2,1,0:T(8,128)S(1)}, u32[]{:S(2)}, u32[]{:S(2)}) %collective-permute-start.6) | collective-permute-done | bytes 163872 | tf_op jit(solution)/shard_map/ppermute | solution.py:58
  71.8 0.0 collective-permute-done.7
  71.8 0.9 %fusion.11 = f32[5,1,4,64,128]{4,3,2,1,0:T(8,128)S(1)} fusion(f32[5,4,64,128]{3,2,1,0:T(8,128)S(1)} %get-tuple-element.30, f32[5,4,64,1]{3,2,1,0:T(8,128)S(1)} %get-tuple-element.47, f32[5,4,64,1]{3,2,1,0:T(8,128)S(1)} %get-tuple-element.46, f32[5,4,1,128]{3,2,1,0:T(1,128)S(1)} %get-tuple-element.45, f32[5,4,1,128]{3,2,1,0:T(1,128)S(1)} %get-tuple-element.44, ...), kind=kLoop, calls=%fused_computation.16 | loop fusion | flops 5242880 | bytes 4290560 | tf_op jit(solution)/shard_map/stack | solution.py:92
  72.7 0.2 pad_maximum_fusion.1
  72.9 0.3 fusion.54
  73.1 0.0 collective-permute-done.5
  73.2 0.9 %fusion.65 = f32[1,4,4,64,128]{4,3,2,1,0:T(8,128)} fusion(f32[4,4,64,128]{3,2,1,0:T(8,128)S(1)} %fusion.54, f32[4,4,64,128]{3,2,1,0:T(8,128)S(1)} %collective-permute-done.5, f32[1,4,4,64,128]{4,3,2,1,0:T(8,128)S(1)} %copy-done, pred[]{:T(512)S(6)} %eq.38), kind=kLoop, calls=%fused_computation.120 | loop fusion | flops 262144 | bytes 2097153 | tf_op jit(solution)/shard_map/broadcast_in_dim | solution.py:163
  (18 shorter events, 0.2 us)
Async XLA Ops:
  0.0 14.4 %copy-start = (f32[1,4,4,64,128]{4,3,2,1,0:T(8,128)S(1)}, f32[1,4,4,64,128]{4,3,2,1,0:T(8,128)}, u32[]{:S(2)}) copy-start(f32[1,4,4,64,128]{4,3,2,1,0:T(8,128)} %param.4) | copy-start | bytes 1572868
  0.0 14.4 %copy-start.1 = (s32[4,64,128]{2,1,0:T(8,128)S(1)}, s32[4,64,128]{2,1,0:T(8,128)}, u32[]{:S(2)}) copy-start(s32[4,64,128]{2,1,0:T(8,128)} %param.5) | copy-start | bytes 393220
  0.9 12.6 %collective-permute-start = (f32[1,64,128]{2,1,0:T(8,128)S(1)}, f32[1,64,128]{2,1,0:T(8,128)S(1)}, u32[]{:S(2)}, u32[]{:S(2)}) collective-permute-start(f32[1,64,128]{2,1,0:T(8,128)S(1)} %get-tuple-element.62), channel_id=1, source_target_pairs={{1,0},{2,1},{3,2},{4,3},{5,4},{6,5},{7,6},{8,7},{9,8},{10,9},{11,1... | collective-permute-start | bytes 98312 | tf_op jit(solution)/shard_map/ppermute | solution.py:58
  7.1 7.4 %collective-permute-start.1 = (f32[1,64,128]{2,1,0:T(8,128)S(1)}, f32[1,64,128]{2,1,0:T(8,128)S(1)}, u32[]{:S(2)}, u32[]{:S(2)}) collective-permute-start(f32[1,64,128]{2,1,0:T(8,128)S(1)} %get-tuple-element.63), channel_id=1, source_target_pairs={{0,1},{1,2},{2,3},{3,4},{4,5},{5,6},{6,7},{7,8},{8,9},{9,10},{10,1... | collective-permute-start | bytes 98312 | tf_op jit(solution)/shard_map/ppermute | solution.py:58
  14.9 16.0 %collective-permute-start.3 = (f32[1,64,128]{2,1,0:T(8,128)S(1)}, f32[1,64,128]{2,1,0:T(8,128)S(1)}, u32[]{:S(2)}, u32[]{:S(2)}) collective-permute-start(f32[1,64,128]{2,1,0:T(8,128)S(1)} %get-tuple-element.56), channel_id=1, source_target_pairs={{1,0},{2,1},{3,2},{4,3},{5,4},{6,5},{7,6},{8,7},{9,8},{10,9},{11,1... | collective-permute-start | bytes 98312 | tf_op jit(solution)/shard_map/ppermute | solution.py:58
  21.4 9.5 %collective-permute-start.4 = (f32[1,64,128]{2,1,0:T(8,128)S(1)}, f32[1,64,128]{2,1,0:T(8,128)S(1)}, u32[]{:S(2)}, u32[]{:S(2)}) collective-permute-start(f32[1,64,128]{2,1,0:T(8,128)S(1)} %get-tuple-element.57), channel_id=1, source_target_pairs={{0,1},{1,2},{2,3},{3,4},{4,5},{5,6},{6,7},{7,8},{8,9},{9,10},{10,1... | collective-permute-start | bytes 98312 | tf_op jit(solution)/shard_map/ppermute | solution.py:58
  23.4 13.6 %collective-permute-start.2 = (f32[4,4,64,128]{3,2,1,0:T(8,128)S(1)}, f32[4,4,64,128]{3,2,1,0:T(8,128)S(1)}, u32[]{:S(2)}, u32[]{:S(2)}) collective-permute-start(f32[4,4,64,128]{3,2,1,0:T(8,128)S(1)} %get-tuple-element.9), channel_id=1, source_target_pairs={{0,16},{16,32},{32,48},{48,64},{64,80},{80,96},{96,112},{112,128},... | collective-permute-start | bytes 1572872 | tf_op jit(solution)/shard_map/ppermute | solution.py:133
  37.2 0.7 copy-start.2
  37.2 0.7 copy-start.3
  37.2 0.7 copy-start.4
  37.2 0.7 copy-start.5
  37.2 0.7 copy-start.6
  39.7 33.4 %collective-permute-start.5 = (f32[4,4,64,128]{3,2,1,0:T(8,128)S(1)}, f32[4,4,64,128]{3,2,1,0:T(8,128)S(1)}, u32[]{:S(2)}, u32[]{:S(2)}) collective-permute-start(f32[4,4,64,128]{3,2,1,0:T(8,128)S(1)} %get-tuple-element.13), channel_id=1, source_target_pairs={{0,16},{16,32},{32,48},{48,64},{64,80},{80,96},{96,112},{112,128},... | collective-permute-start | bytes 1572872 | tf_op jit(solution)/shard_map/ppermute | solution.py:147
  48.3 23.4 %collective-permute-start.6 = (f32[5,1,64,128]{3,2,1,0:T(8,128)S(1)}, f32[5,1,64,128]{3,2,1,0:T(8,128)S(1)}, u32[]{:S(2)}, u32[]{:S(2)}) collective-permute-start(f32[5,1,64,128]{3,2,1,0:T(8,128)S(1)} %get-tuple-element.77), channel_id=1, source_target_pairs={{1,0},{2,1},{3,2},{4,3},{5,4},{6,5},{7,6},{8,7},{9,8},{10,9},{11,1... | collective-permute-start | bytes 491528 | tf_op jit(solution)/shard_map/ppermute | solution.py:58
  54.6 17.2 %collective-permute-start.7 = (f32[5,1,64,128]{3,2,1,0:T(8,128)S(1)}, f32[5,1,64,128]{3,2,1,0:T(8,128)S(1)}, u32[]{:S(2)}, u32[]{:S(2)}) collective-permute-start(f32[5,1,64,128]{3,2,1,0:T(8,128)S(1)} %get-tuple-element.78), channel_id=1, source_target_pairs={{0,1},{1,2},{2,3},{3,4},{4,5},{5,6},{6,7},{7,8},{8,9},{9,10},{10,1... | collective-permute-start | bytes 491528 | tf_op jit(solution)/shard_map/ppermute | solution.py:58

commit v11 on v10

--- a/solution.py
+++ b/solution.py
@@ -156,8 +156,18 @@
     volts2 = nodes1[:, 0]
     low2 = jnp.where(at_low, volts2[:, :1], low2)
     high2 = jnp.where(at_high, volts2[:, planes - 1 :], high2)
-    derivs2 = rates(nodes1, laplacian(volts2, low2, high2, conduct), fast_g, slow_g, slow_tau)
-    step2 = lax.optimization_barrier(increment(derivs2, table[4]))
+    rough = rates(nodes1, laplacian(volts2, volts2[:, :1], volts2[:, planes - 1 :], conduct), fast_g, slow_g, slow_tau)
+    step2 = lax.optimization_barrier(increment(rough, table[4]))
+
+    def edge_plane(lo, hi, below, above):
+        part = lambda c: c[lo:hi]
+        lap = laplacian(volts2[:, lo:hi], below, above, [part(c) for c in conduct])
+        derivs = rates(nodes1[:, :, lo:hi], lap, part(fast_g), part(slow_g), part(slow_tau))
+        return increment(derivs, table[4])
+
+    first = edge_plane(0, 1, low2, volts2[:, 1:2])
+    last = edge_plane(planes - 1, planes, volts2[:, planes - 2 : planes - 1], high2)
+    step2 = jnp.concatenate([first, step2[:, 1 : planes - 1], last], axis=1)
     start2 = jnp.where(first_slice, start0, arrived2)
     ends2 = start2 + step2
     return ends2[None]

time: 74.4 us -> 69.8 us (0.938)
  the two profiles are of different devices: /device:TPU:27 before, /device:TPU:1 now
where the time goes in v11:
time: 69.8 us; the launch traced here: 69.4 us
  starting transfers between devices  37 us (53%)
  waiting for transfers between devices  15.3 us (22%)
  other arithmetic  13.6 us (19%)
  local copies, waits for them, and re-layouts  2.78 us (4%)
    ppermute x6, starting transfers between devices, shift_space(): return lax.ppermute(block, 'space', pairs)  22.7 us
    ppermute x6, waiting for transfers between devices, shift_space(): return lax.ppermute(block, 'space', pairs)  15.3 us
    ppermute x1, starting transfers between devices, steps(): arrived1 = lax.ppermute(ends0, 'tm', tm_pairs)  9.14 us
    ppermute x1, starting transfers between devices, steps(): arrived2 = lax.ppermute(ends1, 'tm', tm_pairs)  5.21 us
    another operation x9, other arithmetic, rates(): return jnp.stack([dvolt, dact, dinact, dslow], axis=-4)  3 us
    add x2, other arithmetic, lookup(): total + jnp.where(labels == level, values[level], 0.0).astype(jnp.float32)  2.13 us
    div x3, other arithmetic, rates(): dact = (jax.nn.sigmoid(8.0 * (volt - 0.2)) - act) / 0.5  1.62 us
    add x2, other arithmetic, edge_nodes(): return start[None] + slice_len * total  1.56 us
  transfers between devices with their start and end apart: 8, of which 2 were waited for; matrix products, arithmetic and copies ran while one was open for 19% of the time, Pallas kernels for 0%

profile of v11, /device:TPU:1, one launch (start us, length us, event | category | flops | bytes accessed | tf_op | source)
XLA Modules:
  0.0 69.4 jit_solution(7738213242388997421)
XLA Ops:
  0.0 0.8 %slice_bitcast_fusion.44 = (f32[1,64,128]{2,1,0:T(8,128)S(1)}, f32[1,64,128]{2,1,0:T(8,128)S(1)}) fusion(f32[1,4,4,64,128]{4,3,2,1,0:T(8,128)} %param.4), kind=kLoop, calls=%fused_computation.291 | loop fusion | bytes 131072 | tf_op jit(solution)/shard_map/slice | solution.py:128
  0.9 1.3 %collective-permute-start = (f32[1,64,128]{2,1,0:T(8,128)S(1)}, f32[1,64,128]{2,1,0:T(8,128)S(1)}, u32[]{:S(2)}, u32[]{:S(2)}) collective-permute-start(f32[1,64,128]{2,1,0:T(8,128)S(1)} %get-tuple-element.82), channel_id=1, source_target_pairs={{1,0},{2,1},{3,2},{4,3},{5,4},{6,5},{7,6},{8,7},{9,8},{10,9},{11,1... | collective-permute-start | bytes 98312 | tf_op jit(solution)/shard_map/ppermute | solution.py:58
  2.1 5.0 %collective-permute-start.1 = (f32[1,64,128]{2,1,0:T(8,128)S(1)}, f32[1,64,128]{2,1,0:T(8,128)S(1)}, u32[]{:S(2)}, u32[]{:S(2)}) collective-permute-start(f32[1,64,128]{2,1,0:T(8,128)S(1)} %get-tuple-element.83), channel_id=1, source_target_pairs={{0,1},{1,2},{2,3},{3,4},{4,5},{5,6},{6,7},{7,8},{8,9},{9,10},{10,1... | collective-permute-start | bytes 98312 | tf_op jit(solution)/shard_map/ppermute | solution.py:58
  7.1 1.2 %slice_bitcast_fusion.17 = (f32[4,64,128]{2,1,0:T(8,128)S(1)}, f32[1,4,64,128]{3,2,1,0:T(8,128)S(1)}, f32[1,4,64,128]{3,2,1,0:T(8,128)S(1)}) fusion(f32[1,4,4,64,128]{4,3,2,1,0:T(8,128)} %param.4), kind=kLoop, calls=%fused_computation.250 | loop fusion | flops 655360 | bytes 786432 | tf_op jit(solution)/shard_map/squeeze | solution.py:124
  8.3 1.0 %select_add_fusion = (f32[4,64,128]{2,1,0:T(8,128)S(1)}, pred[4,64,128]{2,1,0:T(8,128)(4,1)S(1)}, pred[4,64,128]{2,1,0:T(8,128)(4,1)S(1)}, pred[4,64,128]{2,1,0:T(8,128)(4,1)S(1)}, pred[4,64,128]{2,1,0:T(8,128)(4,1)S(1)}) fusion(s32[4,64,128]{2,1,0:T(8,128)} %param.6), kind=kLoop, calls=%fused_computation.245 | loop fusion | flops 360448 | bytes 393216 | tf_op jit(solution)/shard_map/add | solution.py:34
  9.3 1.1 %select_add_fusion.1 = (f32[4,64,128]{2,1,0:T(8,128)S(1)}, f32[4,64,128]{2,1,0:T(8,128)S(1)}, f32[1,4,64,128]{3,2,1,0:T(8,128)S(1)}) fusion(pred[4,64,128]{2,1,0:T(8,128)(4,1)S(1)} %get-tuple-element.19, pred[4,64,128]{2,1,0:T(8,128)(4,1)S(1)} %get-tuple-element.18, pred[4,64,128]{2,1,0:T(8,128)(4,1)S(1)} %get-tuple-element.17, ...), kind=kLoop, calls=%fused_computation.246 | loop fusion | flops 720896 | bytes 786432 | tf_op jit(solution)/shard_map/add | solution.py:34
  10.5 1.0 %select_add_fusion.4 = (f32[4,64,128]{2,1,0:T(8,128)S(1)}, f32[4,64,128]{2,1,0:T(8,128)S(1)}, f32[4,64,128]{2,1,0:T(8,128)S(1)}) fusion(s32[4,64,128]{2,1,0:T(8,128)} %param.5), kind=kLoop, calls=%fused_computation.249 | loop fusion | flops 294912 | bytes 524288 | tf_op jit(solution)/shard_map/add | solution.py:115
  11.4 0.1 fusion.133
  11.6 0.0 collective-permute-done
  11.6 0.0 collective-permute-done.1
  11.7 0.3 fusion.93
  12.0 0.1 bitcast_add_fusion.5
  12.1 0.1 bitcast_dynamic-update-slice_fusion.4
  12.1 3.5 %collective-permute-start.4 = (f32[1,64,128]{2,1,0:T(8,128)S(1)}, f32[1,64,128]{2,1,0:T(8,128)S(1)}, u32[]{:S(2)}, u32[]{:S(2)}) collective-permute-start(f32[1,64,128]{2,1,0:T(8,128)S(1)} %get-tuple-element.77), channel_id=1, source_target_pairs={{0,1},{1,2},{2,3},{3,4},{4,5},{5,6},{6,7},{7,8},{8,9},{9,10},{10,1... | collective-permute-start | bytes 98312 | tf_op jit(solution)/shard_map/ppermute | solution.py:58
  15.7 9.1 %collective-permute-start.2 = (f32[4,4,64,128]{3,2,1,0:T(8,128)S(1)}, f32[4,4,64,128]{3,2,1,0:T(8,128)S(1)}, u32[]{:S(2)}, u32[]{:S(2)}) collective-permute-start(f32[4,4,64,128]{3,2,1,0:T(8,128)S(1)} %get-tuple-element.9), channel_id=1, source_target_pairs={{0,16},{16,32},{32,48},{48,64},{64,80},{80,96},{96,112},{112,128},... | collective-permute-start | bytes 1572872 | tf_op jit(solution)/shard_map/ppermute | solution.py:133
  24.8 0.1 bitcast_dynamic-update-slice_fusion.3
  24.9 0.1 bitcast_dynamic-update-slice_fusion.2
  25.0 0.1 bitcast_dynamic-update-slice_fusion.1
  25.1 0.1 bitcast_dynamic-update-slice_fusion
  25.1 0.4 slice_bitcast_fusion.48
  25.6 0.2 fusion.131
  25.8 0.5 subtract_multiply_fusion.1
  26.4 0.1 copy_divide_fusion.1
  26.5 1.3 %collective-permute-start.3 = (f32[1,64,128]{2,1,0:T(8,128)S(1)}, f32[1,64,128]{2,1,0:T(8,128)S(1)}, u32[]{:S(2)}, u32[]{:S(2)}) collective-permute-start(f32[1,64,128]{2,1,0:T(8,128)S(1)} %get-tuple-element.76), channel_id=1, source_target_pairs={{1,0},{2,1},{3,2},{4,3},{5,4},{6,5},{7,6},{8,7},{9,8},{10,9},{11,1... | collective-permute-start | bytes 98312 | tf_op jit(solution)/shard_map/ppermute | solution.py:58
  27.8 0.0 collective-permute-done.4
  27.8 4.8 %collective-permute-done.3 = f32[1,64,128]{2,1,0:T(8,128)S(1)} collective-permute-done((f32[1,64,128]{2,1,0:T(8,128)S(1)}, f32[1,64,128]{2,1,0:T(8,128)S(1)}, u32[]{:S(2)}, u32[]{:S(2)}) %collective-permute-start.3) | collective-permute-done | bytes 32800 | tf_op jit(solution)/shard_map/ppermute | solution.py:58
  32.8 0.9 %fusion.17 = f32[5,1,4,64,128]{4,3,2,1,0:T(8,128)S(1)} fusion(f32[5,4,64,128]{3,2,1,0:T(8,128)S(1)} %get-tuple-element.45, f32[5,4,64,1]{3,2,1,0:T(8,128)S(1)} %get-tuple-element.70, f32[5,4,64,1]{3,2,1,0:T(8,128)S(1)} %get-tuple-element.69, f32[5,4,1,128]{3,2,1,0:T(1,128)S(1)} %get-tuple-element.68, f32[5,4,1,128]{3,2,1,0:T(1,128)S(1)} %get-tuple-element.67, ...), kind=kLoop, calls=%fused_computation.30 | loop fusion | flops 5242880 | bytes 4290560 | tf_op jit(solution)/shard_map/stack | solution.py:92
  33.6 0.2 pad_maximum_fusion
  33.8 0.3 fusion.47
  34.1 0.1 fusion.124
  34.3 0.0 copy-start.3
  34.3 0.0 copy-start.4
  34.3 0.0 copy-start.5
  34.3 0.0 copy-start.6
  34.3 0.0 copy-start.7
  34.4 0.2 slice_bitcast_fusion.9
  34.6 5.2 %collective-permute-start.5 = (f32[4,4,64,128]{3,2,1,0:T(8,128)S(1)}, f32[4,4,64,128]{3,2,1,0:T(8,128)S(1)}, u32[]{:S(2)}, u32[]{:S(2)}) collective-permute-start(f32[4,4,64,128]{3,2,1,0:T(8,128)S(1)} %get-tuple-element.13), channel_id=1, source_target_pairs={{0,16},{16,32},{32,48},{48,64},{64,80},{80,96},{96,112},{112,128},... | collective-permute-start | bytes 1572872 | tf_op jit(solution)/shard_map/ppermute | solution.py:147
  39.9 1.3 %multiply_add_fusion = f32[5,4,4,64,128]{4,3,0,2,1:T(8,128)S(1)} fusion(f32[4,4,64,128]{3,2,1,0:T(8,128)S(1)} %get-tuple-element.41, f32[5]{0:T(128)S(1)} %copy-done.3, f32[4,4,64,128]{3,2,1,0:T(8,128)S(1)} %get-tuple-element.42, f32[5]{0:T(128)S(1)} %copy-done.4, f32[4,4,64,128]{3,2,1,0:T(8,128)S(1)} %get-tuple-element.43, f32[5]{0:T(128)S(1)} %copy-done.5, ...), kind=kLoop, calls=%fused_computation.2 | loop fusion | flops 7208960 | bytes 5767268 | tf_op jit(solution)/shard_map/add | solution.py:106
  41.2 0.7 %subtract_multiply_fusion = (f32[5,1,4,64,128]{4,3,0,2,1:T(8,128)S(1)}, f32[5,1,4,64,128]{4,3,0,2,1:T(8,128)S(1)}, f32[5,1,4,64,128]{4,3,0,2,1:T(8,128)S(1)}, f3...) fusion(f32[5,4,4,64,128]{4,3,0,2,1:T(8,128)S(1)} %multiply_add_fusion), kind=kLoop, calls=%fused_computation.66 | loop fusion | flops 3932160 | bytes 5898240 | tf_op jit(solution)/shard_map/div | solution.py:87
  41.9 0.1 slice_bitcast_fusion.11
  42.0 0.4 fusion.25
  42.4 0.1 fusion.126
  42.6 0.2 fusion.129
  42.8 0.1 fusion.87
  42.9 0.2 multiply_add_fusion.2
  43.1 10.3 %collective-permute-start.6 = (f32[5,1,64,128]{3,2,1,0:T(8,128)S(1)}, f32[5,1,64,128]{3,2,1,0:T(8,128)S(1)}, u32[]{:S(2)}, u32[]{:S(2)}) collective-permute-start(f32[5,1,64,128]{3,2,1,0:T(8,128)S(1)} %get-tuple-element.109), channel_id=1, source_target_pairs={{0,1},{1,2},{2,3},{3,4},{4,5},{5,6},{6,7},{7,8},{8,9},{9,10},{10,1... | collective-permute-start | bytes 491528 | tf_op jit(solution)/shard_map/ppermute | solution.py:58
  53.4 1.3 %collective-permute-start.7 = (f32[5,1,64,128]{3,2,1,0:T(8,128)S(1)}, f32[5,1,64,128]{3,2,1,0:T(8,128)S(1)}, u32[]{:S(2)}, u32[]{:S(2)}) collective-permute-start(f32[5,1,64,128]{3,2,1,0:T(8,128)S(1)} %get-tuple-element.110), channel_id=1, source_target_pairs={{1,0},{2,1},{3,2},{4,3},{5,4},{6,5},{7,6},{8,7},{9,8},{10,9},{11,1... | collective-permute-start | bytes 491528 | tf_op jit(solution)/shard_map/ppermute | solution.py:58
  54.7 0.4 subtract_multiply_fusion.2
  55.1 0.7 %fusion.31 = f32[5,1,4,64,128]{4,3,0,2,1:T(8,128)S(1)} fusion(f32[5,4,64,128]{3,2,1,0:T(8,128)S(1)} %get-tuple-element.53, f32[5,4,4,64,128]{4,3,0,2,1:T(8,128)S(1)} %multiply_add_fusion, f32[5,4,64,128]{3,2,1,0:T(8,128)S(1)} %get-tuple-element.54, f32[5,4,64,1]{3,2,1,0:T(8,128)S(1)} %get-tuple-element.60, f32[5,4,64,1]{3,2,1,0:T(8,128)S(1)} %get-tuple-element.59, ...), kind=kLoop, calls=%fused_computation.56 | loop fusion | flops 3604480 | bytes 3373056 | tf_op jit(solution)/shard_map/stack | solution.py:92
  55.8 0.3 pad_maximum_fusion.1
  56.1 0.3 fusion.35
  56.4 0.0 copy-start.1
  56.5 0.0 collective-permute-done.6
  56.5 0.2 fusion.58
  56.7 0.1 pad_maximum_fusion.14
  56.8 10.5 %collective-permute-done.7 = f32[5,1,64,128]{3,2,1,0:T(8,128)S(1)} collective-permute-done((f32[5,1,64,128]{3,2,1,0:T(8,128)S(1)}, f32[5,1,64,128]{3,2,1,0:T(8,128)S(1)}, u32[]{:S(2)}, u32[]{:S(2)}) %collective-permute-start.7) | collective-permute-done | bytes 163872 | tf_op jit(solution)/shard_map/ppermute | solution.py:58
  67.3 0.2 fusion.64
  67.6 0.0 slice-start
  67.6 0.1 pad_maximum_fusion.15
  67.6 0.1 fusion.103
  67.7 0.1 fusion.96
  67.8 0.0 collective-permute-done.5
  67.8 0.7 %slice-done = f32[4,2,64,128]{3,2,1,0:T(8,128)S(1)} async-done(((f32[4,4,64,128]{3,2,1,0:T(8,128)}), f32[4,2,64,128]{3,2,1,0:T(8,128)S(1)}, s32[]{:S(2)}) %slice-start) | async-done | bytes 262168 | tf_op jit(solution)/shard_map/slice | solution.py:170
  68.5 0.9 %fusion.51 = f32[1,4,4,64,128]{4,3,2,1,0:T(8,128)} fusion(f32[4,1,64,128]{3,2,1,0:T(8,128)S(1)} %fusion.96, f32[4,2,64,128]{3,2,1,0:T(8,128)S(1)} %slice-done, f32[4,1,64,128]{3,2,1,0:T(8,128)S(1)} %fusion.103, f32[4,4,64,128]{3,2,1,0:T(8,128)S(1)} %collective-permute-done.5, f32[1,4,4,64,128]{4,3,2,1,0:T(8,128)S(1)} %copy-done, pred[]{:T(512)S(6)} %eq.38), kind=kLoop, calls=%fused_computation.102 | loop fusion | flops 524288 | bytes 2097153 | tf_op jit(solution)/shard_map/broadcast_in_dim | solution.py:173
  (35 shorter events, 0.3 us)
Async XLA Ops:
  0.0 11.6 %copy-start = (f32[1,4,4,64,128]{4,3,2,1,0:T(8,128)S(1)}, f32[1,4,4,64,128]{4,3,2,1,0:T(8,128)}, u32[]{:S(2)}) copy-start(f32[1,4,4,64,128]{4,3,2,1,0:T(8,128)} %param.4) | copy-start | bytes 1572868
  0.0 11.7 %copy-start.2 = (s32[4,64,128]{2,1,0:T(8,128)S(1)}, s32[4,64,128]{2,1,0:T(8,128)}, u32[]{:S(2)}) copy-start(s32[4,64,128]{2,1,0:T(8,128)} %param.5) | copy-start | bytes 393220
  0.9 10.8 %collective-permute-start = (f32[1,64,128]{2,1,0:T(8,128)S(1)}, f32[1,64,128]{2,1,0:T(8,128)S(1)}, u32[]{:S(2)}, u32[]{:S(2)}) collective-permute-start(f32[1,64,128]{2,1,0:T(8,128)S(1)} %get-tuple-element.82), channel_id=1, source_target_pairs={{1,0},{2,1},{3,2},{4,3},{5,4},{6,5},{7,6},{8,7},{9,8},{10,9},{11,1... | collective-permute-start | bytes 98312 | tf_op jit(solution)/shard_map/ppermute | solution.py:58
  2.1 9.5 %collective-permute-start.1 = (f32[1,64,128]{2,1,0:T(8,128)S(1)}, f32[1,64,128]{2,1,0:T(8,128)S(1)}, u32[]{:S(2)}, u32[]{:S(2)}) collective-permute-start(f32[1,64,128]{2,1,0:T(8,128)S(1)} %get-tuple-element.83), channel_id=1, source_target_pairs={{0,1},{1,2},{2,3},{3,4},{4,5},{5,6},{6,7},{7,8},{8,9},{9,10},{10,1... | collective-permute-start | bytes 98312 | tf_op jit(solution)/shard_map/ppermute | solution.py:58
  12.1 15.6 %collective-permute-start.4 = (f32[1,64,128]{2,1,0:T(8,128)S(1)}, f32[1,64,128]{2,1,0:T(8,128)S(1)}, u32[]{:S(2)}, u32[]{:S(2)}) collective-permute-start(f32[1,64,128]{2,1,0:T(8,128)S(1)} %get-tuple-element.77), channel_id=1, source_target_pairs={{0,1},{1,2},{2,3},{3,4},{4,5},{5,6},{6,7},{7,8},{8,9},{9,10},{10,1... | collective-permute-start | bytes 98312 | tf_op jit(solution)/shard_map/ppermute | solution.py:58
  15.7 18.4 %collective-permute-start.2 = (f32[4,4,64,128]{3,2,1,0:T(8,128)S(1)}, f32[4,4,64,128]{3,2,1,0:T(8,128)S(1)}, u32[]{:S(2)}, u32[]{:S(2)}) collective-permute-start(f32[4,4,64,128]{3,2,1,0:T(8,128)S(1)} %get-tuple-element.9), channel_id=1, source_target_pairs={{0,16},{16,32},{32,48},{48,64},{64,80},{80,96},{96,112},{112,128},... | collective-permute-start | bytes 1572872 | tf_op jit(solution)/shard_map/ppermute | solution.py:133
  26.5 6.1 %collective-permute-start.3 = (f32[1,64,128]{2,1,0:T(8,128)S(1)}, f32[1,64,128]{2,1,0:T(8,128)S(1)}, u32[]{:S(2)}, u32[]{:S(2)}) collective-permute-start(f32[1,64,128]{2,1,0:T(8,128)S(1)} %get-tuple-element.76), channel_id=1, source_target_pairs={{1,0},{2,1},{3,2},{4,3},{5,4},{6,5},{7,6},{8,7},{9,8},{10,9},{11,1... | collective-permute-start | bytes 98312 | tf_op jit(solution)/shard_map/ppermute | solution.py:58
  34.3 5.5 %copy-start.3 = (f32[5]{0:T(128)S(1)}, f32[5]{0:T(128)}, u32[]{:S(2)}) copy-start(f32[5]{0:T(128)} %constant.174) | copy-start | bytes 64
  34.3 5.5 %copy-start.4 = (f32[5]{0:T(128)S(1)}, f32[5]{0:T(128)}, u32[]{:S(2)}) copy-start(f32[5]{0:T(128)} %constant.172) | copy-start | bytes 64
  34.3 5.5 %copy-start.5 = (f32[5]{0:T(128)S(1)}, f32[5]{0:T(128)}, u32[]{:S(2)}) copy-start(f32[5]{0:T(128)} %constant.170) | copy-start | bytes 64
  34.3 5.5 %copy-start.6 = (f32[5]{0:T(128)S(1)}, f32[5]{0:T(128)}, u32[]{:S(2)}) copy-start(f32[5]{0:T(128)} %constant.168) | copy-start | bytes 64
  34.3 5.5 %copy-start.7 = (f32[5]{0:T(128)S(1)}, f32[5]{0:T(128)}, u32[]{:S(2)}) copy-start(f32[5]{0:T(128)} %constant.166) | copy-start | bytes 64
  34.6 33.2 %collective-permute-start.5 = (f32[4,4,64,128]{3,2,1,0:T(8,128)S(1)}, f32[4,4,64,128]{3,2,1,0:T(8,128)S(1)}, u32[]{:S(2)}, u32[]{:S(2)}) collective-permute-start(f32[4,4,64,128]{3,2,1,0:T(8,128)S(1)} %get-tuple-element.13), channel_id=1, source_target_pairs={{0,16},{16,32},{32,48},{48,64},{64,80},{80,96},{96,112},{112,128},... | collective-permute-start | bytes 1572872 | tf_op jit(solution)/shard_map/ppermute | solution.py:147
  43.1 13.3 %collective-permute-start.6 = (f32[5,1,64,128]{3,2,1,0:T(8,128)S(1)}, f32[5,1,64,128]{3,2,1,0:T(8,128)S(1)}, u32[]{:S(2)}, u32[]{:S(2)}) collective-permute-start(f32[5,1,64,128]{3,2,1,0:T(8,128)S(1)} %get-tuple-element.109), channel_id=1, source_target_pairs={{0,1},{1,2},{2,3},{3,4},{4,5},{5,6},{6,7},{7,8},{8,9},{9,10},{10,1... | collective-permute-start | bytes 491528 | tf_op jit(solution)/shard_map/ppermute | solution.py:58
  53.4 13.9 %collective-permute-start.7 = (f32[5,1,64,128]{3,2,1,0:T(8,128)S(1)}, f32[5,1,64,128]{3,2,1,0:T(8,128)S(1)}, u32[]{:S(2)}, u32[]{:S(2)}) collective-permute-start(f32[5,1,64,128]{3,2,1,0:T(8,128)S(1)} %get-tuple-element.110), channel_id=1, source_target_pairs={{1,0},{2,1},{3,2},{4,3},{5,4},{6,5},{7,6},{8,7},{9,8},{10,9},{11,1... | collective-permute-start | bytes 491528 | tf_op jit(solution)/shard_map/ppermute | solution.py:58
  56.4 11.1 %copy-start.1 = (f32[4,4,64,128]{3,2,1,0:T(8,128)}, f32[4,4,64,128]{3,2,1,0:T(8,128)S(1)}, u32[]{:S(2)}) copy-start(f32[4,4,64,128]{3,2,1,0:T(8,128)S(1)} %fusion.35) | copy-start | bytes 1572868
  67.6 1.0 %slice-start = ((f32[4,4,64,128]{3,2,1,0:T(8,128)}), f32[4,2,64,128]{3,2,1,0:T(8,128)S(1)}, s32[]{:S(2)}) async-start(f32[4,4,64,128]{3,2,1,0:T(8,128)} %copy-done.1), calls=%async_computation | async-start | bytes 524288 | tf_op jit(solution)/shard_map/slice | solution.py:170

commit v12 on v11

--- a/solution.py
+++ b/solution.py
@@ -106,6 +106,12 @@
     return start[None] + slice_len * total
 
 
+def edge_rates(nodes, volts, plane, below, above, conduct, fast_g, slow_g, slow_tau):
+    part = lambda c: c[plane : plane + 1]
+    lap = laplacian(volts[:, plane : plane + 1], below, above, [part(c) for c in conduct])
+    return rates(nodes[:, :, plane : plane + 1], lap, part(fast_g), part(slow_g), part(slow_tau))
+
+
 def steps(guess, fibre, labels):
     table = radau_table()
     sums = [sum(row) for row in table]
@@ -140,8 +146,16 @@
     high1 = jnp.stack([high0 + slice_len * (sums[m] * dhigh) for m in range(5)])
     low1 = jnp.where(at_low, volts1[:, :1], low1)
     high1 = jnp.where(at_high, volts1[:, planes - 1 :], high1)
-    derivs1 = rates(nodes0, laplacian(volts1, low1, high1, conduct), fast_g, slow_g, slow_tau)
-    step1 = lax.optimization_barrier(increment(derivs1, table[4]))
+    rough1 = rates(nodes0, laplacian(volts1, volts1[:, :1], volts1[:, planes - 1 :], conduct), fast_g, slow_g, slow_tau)
+    inner1 = lax.optimization_barrier(increment(rough1, table[4]))
+    first1 = edge_rates(nodes0, volts1, 0, low1, volts1[:, 1:2], conduct, fast_g, slow_g, slow_tau)
+    last1 = edge_rates(
+        nodes0, volts1, planes - 1, volts1[:, planes - 2 : planes - 1], high1, conduct, fast_g, slow_g, slow_tau
+    )
+    derivs1 = jnp.concatenate([first1, rough1[:, :, 1 : planes - 1], last1], axis=2)
+    step1 = jnp.concatenate(
+        [increment(first1, table[4]), inner1[:, 1 : planes - 1], increment(last1, table[4])], axis=1
+    )
     start1 = jnp.where(first_slice, start0, arrived1)
     ends1 = start1 + step1
     arrived2 = lax.ppermute(ends1, "tm", tm_pairs)

time: 69.8 us -> 72.9 us (1.044)
  the two profiles are of different devices: /device:TPU:1 before, /device:TPU:27 now
where the time goes in v12:
time: 72.9 us; the launch traced here: 71.8 us
  starting transfers between devices  41.2 us (57%)
  other arithmetic  14.8 us (20%)
  waiting for transfers between devices  9.72 us (13%)
  local copies, waits for them, and re-layouts  5.45 us (7%)
    ppermute x6, starting transfers between devices, shift_space(): return lax.ppermute(block, 'space', pairs)  24.1 us
    ppermute x1, starting transfers between devices, steps(): arrived1 = lax.ppermute(ends0, 'tm', tm_pairs)  8.67 us
    ppermute x6, waiting for transfers between devices, shift_space(): return lax.ppermute(block, 'space', pairs)  8.65 us
    ppermute x1, starting transfers between devices, steps(): arrived2 = lax.ppermute(ends1, 'tm', tm_pairs)  8.4 us
    another operation x13, other arithmetic, rates(): return jnp.stack([dvolt, dact, dinact, dslow], axis=-4)  3.86 us
    add x2, other arithmetic, lookup(): total + jnp.where(labels == level, values[level], 0.0).astype(jnp.float32)  2.13 us
    div x4, other arithmetic, rates(): dact = (jax.nn.sigmoid(8.0 * (volt - 0.2)) - act) / 0.5  1.94 us
    add x2, other arithmetic, edge_nodes(): return start[None] + slice_len * total  1.61 us
  transfers between devices with their start and end apart: 8, of which 3 were waited for; matrix products, arithmetic and copies ran while one was open for 15% of the time, Pallas kernels for 0%

profile of v12, /device:TPU:27, one launch (start us, length us, event | category | flops | bytes accessed | tf_op | source)
XLA Modules:
  0.0 71.8 jit_solution(4341440587877809468)
XLA Ops:
  0.0 0.8 %slice_bitcast_fusion.40 = (f32[1,64,128]{2,1,0:T(8,128)S(1)}, f32[1,64,128]{2,1,0:T(8,128)S(1)}) fusion(f32[1,4,4,64,128]{4,3,2,1,0:T(8,128)} %param.4), kind=kLoop, calls=%fused_computation.432 | loop fusion | bytes 131072 | tf_op jit(solution)/shard_map/slice | solution.py:134
  0.9 6.2 %collective-permute-start = (f32[1,64,128]{2,1,0:T(8,128)S(1)}, f32[1,64,128]{2,1,0:T(8,128)S(1)}, u32[]{:S(2)}, u32[]{:S(2)}) collective-permute-start(f32[1,64,128]{2,1,0:T(8,128)S(1)} %get-tuple-element.94), channel_id=1, source_target_pairs={{1,0},{2,1},{3,2},{4,3},{5,4},{6,5},{7,6},{8,7},{9,8},{10,9},{11,1... | collective-permute-start | bytes 98312 | tf_op jit(solution)/shard_map/ppermute | solution.py:58
  7.1 1.9 %collective-permute-start.1 = (f32[1,64,128]{2,1,0:T(8,128)S(1)}, f32[1,64,128]{2,1,0:T(8,128)S(1)}, u32[]{:S(2)}, u32[]{:S(2)}) collective-permute-start(f32[1,64,128]{2,1,0:T(8,128)S(1)} %get-tuple-element.95), channel_id=1, source_target_pairs={{0,1},{1,2},{2,3},{3,4},{4,5},{5,6},{6,7},{7,8},{8,9},{9,10},{10,1... | collective-permute-start | bytes 98312 | tf_op jit(solution)/shard_map/ppermute | solution.py:58
  9.0 1.2 %slice_bitcast_fusion.13 = (f32[4,64,128]{2,1,0:T(8,128)S(1)}, f32[1,4,64,128]{3,2,1,0:T(8,128)S(1)}, f32[1,4,64,128]{3,2,1,0:T(8,128)S(1)}) fusion(f32[1,4,4,64,128]{4,3,2,1,0:T(8,128)} %param.4), kind=kLoop, calls=%fused_computation.391 | loop fusion | flops 655360 | bytes 786432 | tf_op jit(solution)/shard_map/squeeze | solution.py:130
  10.2 1.0 %select_add_fusion.1 = (f32[4,64,128]{2,1,0:T(8,128)S(1)}, pred[4,64,128]{2,1,0:T(8,128)(4,1)S(1)}, pred[4,64,128]{2,1,0:T(8,128)(4,1)S(1)}, pred[4,64,128]{2,1,0:T(8,128)(4,1)S(1)}, pred[4,64,128]{2,1,0:T(8,128)(4,1)S(1)}) fusion(s32[4,64,128]{2,1,0:T(8,128)} %param.6), kind=kLoop, calls=%fused_computation.387 | loop fusion | flops 360448 | bytes 393216 | tf_op jit(solution)/shard_map/add | solution.py:34
  11.2 1.1 %select_add_fusion = (f32[4,64,128]{2,1,0:T(8,128)S(1)}, f32[4,64,128]{2,1,0:T(8,128)S(1)}, f32[1,4,64,128]{3,2,1,0:T(8,128)S(1)}) fusion(pred[4,64,128]{2,1,0:T(8,128)(4,1)S(1)} %get-tuple-element.19, pred[4,64,128]{2,1,0:T(8,128)(4,1)S(1)} %get-tuple-element.18, pred[4,64,128]{2,1,0:T(8,128)(4,1)S(1)} %get-tuple-element.17, ...), kind=kLoop, calls=%fused_computation.386 | loop fusion | flops 720896 | bytes 786432 | tf_op jit(solution)/shard_map/add | solution.py:34
  12.3 1.0 %select_add_fusion.4 = (f32[4,64,128]{2,1,0:T(8,128)S(1)}, f32[4,64,128]{2,1,0:T(8,128)S(1)}, f32[4,64,128]{2,1,0:T(8,128)S(1)}) fusion(s32[4,64,128]{2,1,0:T(8,128)} %param.5), kind=kLoop, calls=%fused_computation.390 | loop fusion | flops 294912 | bytes 524288 | tf_op jit(solution)/shard_map/add | solution.py:121
  13.3 0.1 fusion.224
  13.5 1.0 %collective-permute-done.1 = f32[1,64,128]{2,1,0:T(8,128)S(1)} collective-permute-done((f32[1,64,128]{2,1,0:T(8,128)S(1)}, f32[1,64,128]{2,1,0:T(8,128)S(1)}, u32[]{:S(2)}, u32[]{:S(2)}) %collective-permute-start.1) | collective-permute-done | bytes 32800 | tf_op jit(solution)/shard_map/ppermute | solution.py:58
  14.5 0.3 fusion.169
  14.8 0.1 bitcast_add_fusion.19
  14.9 0.1 bitcast_dynamic-update-slice_fusion.4
  14.9 0.1 bitcast_dynamic-update-slice_fusion.3
  15.0 0.1 bitcast_dynamic-update-slice_fusion.2
  15.1 0.1 bitcast_dynamic-update-slice_fusion.1
  15.2 0.1 bitcast_dynamic-update-slice_fusion
  15.2 0.3 fusion.212
  15.6 0.8 %subtract_multiply_fusion.1 = (f32[5,1,4,64,128]{4,3,0,2,1:T(8,128)S(1)}, f32[5,1,4,64,128]{4,3,0,2,1:T(8,128)S(1)}, f32[5,1,4,64,128]{4,3,0,2,1:T(8,128)S(1)}, f32[5,4,64,128]{3,2,0,1:T(8,128)S(1)}) fusion(f32[5,1,4,64,128]{4,3,2,1,0:T(8,128)S(1)} %get-tuple-element.48, f32[5,1,4,64,128]{4,3,2,1,0:T(8,128)S(1)} %get-tuple-element.51, ...), kind=kLoop, calls=%fused_computation.92 | loop fusion | flops 4423680 | bytes 5373952 | tf_op jit(solution)/shard_map/div | solution.py:87
  16.4 0.2 fusion.219
  16.6 0.3 fusion.222
  16.8 1.9 %collective-permute-start.3 = (f32[1,64,128]{2,1,0:T(8,128)S(1)}, f32[1,64,128]{2,1,0:T(8,128)S(1)}, u32[]{:S(2)}, u32[]{:S(2)}) collective-permute-start(f32[1,64,128]{2,1,0:T(8,128)S(1)} %get-tuple-element.88), channel_id=1, source_target_pairs={{0,1},{1,2},{2,3},{3,4},{4,5},{5,6},{6,7},{7,8},{8,9},{9,10},{10,1... | collective-permute-start | bytes 98312 | tf_op jit(solution)/shard_map/ppermute | solution.py:58
  18.8 6.1 %collective-permute-start.4 = (f32[1,64,128]{2,1,0:T(8,128)S(1)}, f32[1,64,128]{2,1,0:T(8,128)S(1)}, u32[]{:S(2)}, u32[]{:S(2)}) collective-permute-start(f32[1,64,128]{2,1,0:T(8,128)S(1)} %get-tuple-element.89), channel_id=1, source_target_pairs={{1,0},{2,1},{3,2},{4,3},{5,4},{6,5},{7,6},{8,7},{9,8},{10,9},{11,1... | collective-permute-start | bytes 98312 | tf_op jit(solution)/shard_map/ppermute | solution.py:58
  24.8 8.7 %collective-permute-start.2 = (f32[4,4,64,128]{3,2,1,0:T(8,128)S(1)}, f32[4,4,64,128]{3,2,1,0:T(8,128)S(1)}, u32[]{:S(2)}, u32[]{:S(2)}) collective-permute-start(f32[4,4,64,128]{3,2,1,0:T(8,128)S(1)} %get-tuple-element.9), channel_id=1, source_target_pairs={{0,16},{16,32},{32,48},{48,64},{64,80},{80,96},{96,112},{112,128},... | collective-permute-start | bytes 1572872 | tf_op jit(solution)/shard_map/ppermute | solution.py:139
  33.5 0.2 fusion.73
  33.7 0.3 fusion.87
  33.9 0.9 %fusion.5 = f32[5,1,4,64,128]{4,3,0,2,1:T(8,128)S(1)} fusion(f32[5,4,64,128]{3,2,0,1:T(8,128)S(1)} %get-tuple-element.85, f32[5,4,64,1]{3,2,0,1:T(8,128)S(1)} %get-tuple-element.81, f32[5,4,64,1]{3,2,0,1:T(8,128)S(1)} %get-tuple-element.80, f32[5,4,1,128]{3,2,0,1:T(1,128)S(1)} %get-tuple-element.79, f32[5,4,1,128]{3,2,0,1:T(1,128)S(1)} %get-tuple-element.78, ...), kind=kLoop, calls=%fused_computation.38 | loop fusion | flops 5242880 | bytes 4290560 | tf_op jit(solution)/shard_map/stack | solution.py:92
  34.9 0.3 pad_maximum_fusion
  35.2 0.3 fusion.42
  35.5 1.1 %copy-done.1 = f32[5,4,4,64,128]{4,3,0,2,1:T(8,128)} copy-done((f32[5,4,4,64,128]{4,3,0,2,1:T(8,128)}, f32[5,4,4,64,128]{4,3,0,2,1:T(8,128)S(1)}, u32[]{:S(2)}) %copy-start.1) | copy-done | bytes 2621464
  36.7 0.3 fusion.52
  37.0 0.1 pad_maximum_fusion.15
  37.2 0.3 fusion.58
  37.4 0.6 slice-done
  38.0 0.3 pad_maximum_fusion.1
  38.4 0.1 pad_maximum_fusion.16
  38.4 0.1 fusion.195
  38.5 0.1 fusion.189
  38.5 1.1 %collective-permute-done.2 = f32[4,4,64,128]{3,2,1,0:T(8,128)S(1)} collective-permute-done((f32[4,4,64,128]{3,2,1,0:T(8,128)S(1)}, f32[4,4,64,128]{3,2,1,0:T(8,128)S(1)}, u32[]{:S(2)}, u32[]{:S(2)}) %collective-permute-start.2) | collective-permute-done | bytes 524320 | tf_op jit(solution)/shard_map/ppermute | solution.py:139
  39.6 0.1 maximum_add_fusion
  39.8 0.3 slice_bitcast_fusion.5
  40.2 0.3 copy-done.5
  40.5 0.0 copy-done.9
  40.5 1.4 %multiply_add_fusion = f32[5,4,4,64,128]{4,3,0,2,1:T(8,128)S(1)} fusion(f32[4,4,64,128]{3,2,1,0:T(8,128)S(1)} %get-tuple-element.40, f32[5]{0:T(128)S(1)} %copy-done.5, f32[4,4,64,128]{3,2,1,0:T(8,128)S(1)} %get-tuple-element.41, f32[5]{0:T(128)S(1)} %copy-done.6, f32[4,4,64,128]{3,2,1,0:T(8,128)S(1)} %get-tuple-element.42, f32[5]{0:T(128)S(1)} %copy-done.7, ...), kind=kLoop, calls=%fused_computation.3 | loop fusion | flops 7208960 | bytes 5767268 | tf_op jit(solution)/shard_map/add | solution.py:106
  41.9 0.1 fusion.152
  42.0 0.1 fusion.99
  42.1 0.3 fusion.102
  42.4 8.4 %collective-permute-start.5 = (f32[4,4,64,128]{3,2,1,0:T(8,128)S(1)}, f32[4,4,64,128]{3,2,1,0:T(8,128)S(1)}, u32[]{:S(2)}, u32[]{:S(2)}) collective-permute-start(f32[4,4,64,128]{3,2,1,0:T(8,128)S(1)} %get-tuple-element.13), channel_id=1, source_target_pairs={{0,16},{16,32},{32,48},{48,64},{64,80},{80,96},{96,112},{112,128},... | collective-permute-start | bytes 1572872 | tf_op jit(solution)/shard_map/ppermute | solution.py:161
  50.8 0.8 %subtract_multiply_fusion = (f32[5,1,4,64,128]{4,3,0,2,1:T(8,128)S(1)}, f32[5,1,4,64,128]{4,3,0,2,1:T(8,128)S(1)}, f32[5,1,4,64,128]{4,3,0,2,1:T(8,128)S(1)}, f32[5,4,64,128]{3,2,0,1:T(8,128)S(1)}) fusion(f32[5,4,4,64,128]{4,3,0,2,1:T(8,128)S(1)} %multiply_add_fusion, f32[4,64,128]{2,1,0:T(8,128)S(1)} %get-tuple-element.115), kind=kLoop, calls=%fused_computation.89 | loop fusion | flops 4423680 | bytes 5373952 | tf_op jit(solution)/shard_map/div | solution.py:87
  51.6 0.2 fusion.214
  51.8 0.3 fusion.217
  52.0 0.2 multiply_add_fusion.2
  52.3 4.5 %collective-permute-start.6 = (f32[5,1,64,128]{3,2,0,1:T(8,128)S(1)}, f32[5,1,64,128]{3,2,0,1:T(8,128)S(1)}, u32[]{:S(2)}, u32[]{:S(2)}) collective-permute-start(f32[5,1,64,128]{3,2,0,1:T(8,128)S(1)} %get-tuple-element.121), channel_id=1, source_target_pairs={{0,1},{1,2},{2,3},{3,4},{4,5},{5,6},{6,7},{7,8},{8,9},{9,10},{10,1... | collective-permute-start | bytes 491528 | tf_op jit(solution)/shard_map/ppermute | solution.py:58
  56.8 3.5 %collective-permute-start.7 = (f32[5,1,64,128]{3,2,0,1:T(8,128)S(1)}, f32[5,1,64,128]{3,2,0,1:T(8,128)S(1)}, u32[]{:S(2)}, u32[]{:S(2)}) collective-permute-start(f32[5,1,64,128]{3,2,0,1:T(8,128)S(1)} %get-tuple-element.122), channel_id=1, source_target_pairs={{1,0},{2,1},{3,2},{4,3},{5,4},{6,5},{7,6},{8,7},{9,8},{10,9},{11,1... | collective-permute-start | bytes 491528 | tf_op jit(solution)/shard_map/ppermute | solution.py:58
  60.3 0.9 %fusion.11 = f32[5,1,4,64,128]{4,3,0,2,1:T(8,128)S(1)} fusion(f32[5,4,64,128]{3,2,0,1:T(8,128)S(1)} %get-tuple-element.38, f32[5,4,64,1]{3,2,0,1:T(8,128)S(1)} %get-tuple-element.67, f32[5,4,64,1]{3,2,0,1:T(8,128)S(1)} %get-tuple-element.66, f32[5,4,1,128]{3,2,0,1:T(1,128)S(1)} %get-tuple-element.65, f32[5,4,1,128]{3,2,0,1:T(1,128)S(1)} %get-tuple-element.64, ...), kind=kLoop, calls=%fused_computation.44 | loop fusion | flops 5242880 | bytes 4290560 | tf_op jit(solution)/shard_map/stack | solution.py:92
  61.2 0.2 pad_maximum_fusion.2
  61.4 0.3 fusion.36
  61.7 0.3 fusion.64
  62.0 0.1 pad_maximum_fusion.17
  62.0 7.7 %collective-permute-done.7 = f32[5,1,64,128]{3,2,0,1:T(8,128)S(1)} collective-permute-done((f32[5,1,64,128]{3,2,0,1:T(8,128)S(1)}, f32[5,1,64,128]{3,2,0,1:T(8,128)S(1)}, u32[]{:S(2)}, u32[]{:S(2)}) %collective-permute-start.7) | collective-permute-done | bytes 163872 | tf_op jit(solution)/shard_map/ppermute | solution.py:58
  69.7 0.3 fusion.70
  70.0 0.1 fusion.179
  70.1 0.1 fusion.172
  70.2 0.7 %slice-done.2 = f32[4,2,64,128]{3,2,1,0:T(8,128)S(1)} async-done(((f32[4,4,64,128]{3,2,1,0:T(8,128)}), f32[4,2,64,128]{3,2,1,0:T(8,128)S(1)}, s32[]{:S(2)}) %slice-start.2) | async-done | bytes 262168 | tf_op jit(solution)/shard_map/slice | solution.py:184
  70.9 0.9 %fusion.46 = f32[1,4,4,64,128]{4,3,2,1,0:T(8,128)} fusion(f32[4,1,64,128]{3,2,1,0:T(8,128)S(1)} %fusion.172, f32[4,2,64,128]{3,2,1,0:T(8,128)S(1)} %slice-done.2, f32[4,1,64,128]{3,2,1,0:T(8,128)S(1)} %fusion.179, f32[4,4,64,128]{3,2,1,0:T(8,128)S(1)} %collective-permute-done.5, f32[1,4,4,64,128]{4,3,2,1,0:T(8,128)S(1)} %copy-done, pred[]{:T(512)S(6)} %eq.38), kind=kLoop, calls=%fused_computation.120 | loop fusion | flops 524288 | bytes 2097153 | tf_op jit(solution)/shard_map/broadcast_in_dim | solution.py:187
  (52 shorter events, 0.4 us)
Async XLA Ops:
  0.0 14.4 %copy-start = (f32[1,4,4,64,128]{4,3,2,1,0:T(8,128)S(1)}, f32[1,4,4,64,128]{4,3,2,1,0:T(8,128)}, u32[]{:S(2)}) copy-start(f32[1,4,4,64,128]{4,3,2,1,0:T(8,128)} %param.4) | copy-start | bytes 1572868
  0.0 14.4 %copy-start.4 = (s32[4,64,128]{2,1,0:T(8,128)S(1)}, s32[4,64,128]{2,1,0:T(8,128)}, u32[]{:S(2)}) copy-start(s32[4,64,128]{2,1,0:T(8,128)} %param.5) | copy-start | bytes 393220
  0.9 12.6 %collective-permute-start = (f32[1,64,128]{2,1,0:T(8,128)S(1)}, f32[1,64,128]{2,1,0:T(8,128)S(1)}, u32[]{:S(2)}, u32[]{:S(2)}) collective-permute-start(f32[1,64,128]{2,1,0:T(8,128)S(1)} %get-tuple-element.94), channel_id=1, source_target_pairs={{1,0},{2,1},{3,2},{4,3},{5,4},{6,5},{7,6},{8,7},{9,8},{10,9},{11,1... | collective-permute-start | bytes 98312 | tf_op jit(solution)/shard_map/ppermute | solution.py:58
  7.1 7.4 %collective-permute-start.1 = (f32[1,64,128]{2,1,0:T(8,128)S(1)}, f32[1,64,128]{2,1,0:T(8,128)S(1)}, u32[]{:S(2)}, u32[]{:S(2)}) collective-permute-start(f32[1,64,128]{2,1,0:T(8,128)S(1)} %get-tuple-element.95), channel_id=1, source_target_pairs={{0,1},{1,2},{2,3},{3,4},{4,5},{5,6},{6,7},{7,8},{8,9},{9,10},{10,1... | collective-permute-start | bytes 98312 | tf_op jit(solution)/shard_map/ppermute | solution.py:58
  16.8 19.8 %collective-permute-start.3 = (f32[1,64,128]{2,1,0:T(8,128)S(1)}, f32[1,64,128]{2,1,0:T(8,128)S(1)}, u32[]{:S(2)}, u32[]{:S(2)}) collective-permute-start(f32[1,64,128]{2,1,0:T(8,128)S(1)} %get-tuple-element.88), channel_id=1, source_target_pairs={{0,1},{1,2},{2,3},{3,4},{4,5},{5,6},{6,7},{7,8},{8,9},{9,10},{10,1... | collective-permute-start | bytes 98312 | tf_op jit(solution)/shard_map/ppermute | solution.py:58
  18.8 18.3 %collective-permute-start.4 = (f32[1,64,128]{2,1,0:T(8,128)S(1)}, f32[1,64,128]{2,1,0:T(8,128)S(1)}, u32[]{:S(2)}, u32[]{:S(2)}) collective-permute-start(f32[1,64,128]{2,1,0:T(8,128)S(1)} %get-tuple-element.89), channel_id=1, source_target_pairs={{1,0},{2,1},{3,2},{4,3},{5,4},{6,5},{7,6},{8,7},{9,8},{10,9},{11,1... | collective-permute-start | bytes 98312 | tf_op jit(solution)/shard_map/ppermute | solution.py:58
  24.8 14.8 %collective-permute-start.2 = (f32[4,4,64,128]{3,2,1,0:T(8,128)S(1)}, f32[4,4,64,128]{3,2,1,0:T(8,128)S(1)}, u32[]{:S(2)}, u32[]{:S(2)}) collective-permute-start(f32[4,4,64,128]{3,2,1,0:T(8,128)S(1)} %get-tuple-element.9), channel_id=1, source_target_pairs={{0,16},{16,32},{32,48},{48,64},{64,80},{80,96},{96,112},{112,128},... | collective-permute-start | bytes 1572872 | tf_op jit(solution)/shard_map/ppermute | solution.py:139
  35.2 1.5 %copy-start.1 = (f32[5,4,4,64,128]{4,3,0,2,1:T(8,128)}, f32[5,4,4,64,128]{4,3,0,2,1:T(8,128)S(1)}, u32[]{:S(2)}) copy-start(f32[5,4,4,64,128]{4,3,0,2,1:T(8,128)S(1)} %pad_maximum_fusion) | copy-start | bytes 7864324
  35.5 1.5 %copy-start.2 = (f32[4,4,64,128]{3,2,1,0:T(8,128)}, f32[4,4,64,128]{3,2,1,0:T(8,128)S(1)}, u32[]{:S(2)}) copy-start(f32[4,4,64,128]{3,2,1,0:T(8,128)S(1)} %fusion.42) | copy-start | bytes 1572868
  36.7 1.3 %slice-start = ((f32[5,4,4,64,128]{4,3,0,2,1:T(8,128)}), f32[5,4,2,64,128]{4,3,0,2,1:T(8,128)S(1)}, s32[]{:S(2)}) async-start(f32[5,4,4,64,128]{4,3,0,2,1:T(8,128)} %copy-done.1), calls=%async_computation | async-start | bytes 2621440 | tf_op jit(solution)/shard_map/slice | solution.py:155
  38.3 1.3 %slice-start.1 = ((f32[4,4,64,128]{3,2,1,0:T(8,128)}), f32[4,2,64,128]{3,2,1,0:T(8,128)S(1)}, s32[]{:S(2)}) async-start(f32[4,4,64,128]{3,2,1,0:T(8,128)} %copy-done.2), calls=%async_computation.1 | async-start | bytes 524288 | tf_op jit(solution)/shard_map/slice | solution.py:157
  39.8 0.7 copy-start.5
  39.8 0.7 copy-start.6
  39.8 0.7 copy-start.7
  39.8 0.7 copy-start.8
  39.8 0.7 copy-start.9
  42.4 27.8 %collective-permute-start.5 = (f32[4,4,64,128]{3,2,1,0:T(8,128)S(1)}, f32[4,4,64,128]{3,2,1,0:T(8,128)S(1)}, u32[]{:S(2)}, u32[]{:S(2)}) collective-permute-start(f32[4,4,64,128]{3,2,1,0:T(8,128)S(1)} %get-tuple-element.13), channel_id=1, source_target_pairs={{0,16},{16,32},{32,48},{48,64},{64,80},{80,96},{96,112},{112,128},... | collective-permute-start | bytes 1572872 | tf_op jit(solution)/shard_map/ppermute | solution.py:161
  52.3 9.4 %collective-permute-start.6 = (f32[5,1,64,128]{3,2,0,1:T(8,128)S(1)}, f32[5,1,64,128]{3,2,0,1:T(8,128)S(1)}, u32[]{:S(2)}, u32[]{:S(2)}) collective-permute-start(f32[5,1,64,128]{3,2,0,1:T(8,128)S(1)} %get-tuple-element.121), channel_id=1, source_target_pairs={{0,1},{1,2},{2,3},{3,4},{4,5},{5,6},{6,7},{7,8},{8,9},{9,10},{10,1... | collective-permute-start | bytes 491528 | tf_op jit(solution)/shard_map/ppermute | solution.py:58
  56.8 12.9 %collective-permute-start.7 = (f32[5,1,64,128]{3,2,0,1:T(8,128)S(1)}, f32[5,1,64,128]{3,2,0,1:T(8,128)S(1)}, u32[]{:S(2)}, u32[]{:S(2)}) collective-permute-start(f32[5,1,64,128]{3,2,0,1:T(8,128)S(1)} %get-tuple-element.122), channel_id=1, source_target_pairs={{1,0},{2,1},{3,2},{4,3},{5,4},{6,5},{7,6},{8,7},{9,8},{10,9},{11,1... | collective-permute-start | bytes 491528 | tf_op jit(solution)/shard_map/ppermute | solution.py:58
  61.7 8.3 %copy-start.3 = (f32[4,4,64,128]{3,2,1,0:T(8,128)}, f32[4,4,64,128]{3,2,1,0:T(8,128)S(1)}, u32[]{:S(2)}) copy-start(f32[4,4,64,128]{3,2,1,0:T(8,128)S(1)} %fusion.36) | copy-start | bytes 1572868
  70.0 1.0 %slice-start.2 = ((f32[4,4,64,128]{3,2,1,0:T(8,128)}), f32[4,2,64,128]{3,2,1,0:T(8,128)S(1)}, s32[]{:S(2)}) async-start(f32[4,4,64,128]{3,2,1,0:T(8,128)} %copy-done.3), calls=%async_computation.2 | async-start | bytes 524288 | tf_op jit(solution)/shard_map/slice | solution.py:184

commit v13 on v11

--- a/solution.py
+++ b/solution.py
@@ -106,6 +106,12 @@
     return start[None] + slice_len * total
 
 
+def edge_rates(nodes, volts, plane, below, above, conduct, fast_g, slow_g, slow_tau):
+    part = lambda c: c[plane : plane + 1]
+    lap = laplacian(volts[:, plane : plane + 1], below, above, [part(c) for c in conduct])
+    return rates(nodes[:, :, plane : plane + 1], lap, part(fast_g), part(slow_g), part(slow_tau))
+
+
 def steps(guess, fibre, labels):
     table = radau_table()
     sums = [sum(row) for row in table]
@@ -127,9 +133,17 @@
     low0, high0 = halos(volts0)
     low0 = jnp.where(at_low, volts0[:1], low0)
     high0 = jnp.where(at_high, volts0[planes - 1 :], high0)
-    derivs0 = rates(start0, laplacian(volts0, low0, high0, conduct), fast_g, slow_g, slow_tau)
+    rough0 = rates(start0, laplacian(volts0, volts0[:1], volts0[planes - 1 :], conduct), fast_g, slow_g, slow_tau)
+    rough0 = lax.optimization_barrier(rough0)
+    first0 = edge_rates(start0[None], volts0[None], 0, low0[None], volts0[None, 1:2], conduct, fast_g, slow_g, slow_tau)[0]
+    last0 = edge_rates(
+        start0[None], volts0[None], planes - 1, volts0[None, planes - 2 : planes - 1], high0[None], conduct,
+        fast_g, slow_g, slow_tau,
+    )[0]
+    derivs0 = jnp.concatenate([first0, rough0[:, 1 : planes - 1], last0], axis=1)
     ends0 = start0 + slice_len * (sums[4] * derivs0)
-    derivs0, ends0 = lax.optimization_barrier((derivs0, ends0))
+    first0, last0, ends0 = lax.optimization_barrier((first0, last0, ends0))
+    derivs0 = jnp.concatenate([first0, rough0[:, 1 : planes - 1], last0], axis=1)
     arrived1 = lax.ppermute(ends0, "tm", tm_pairs)
 
     dv = derivs0[0]

time: 69.8 us -> 73 us (1.046)
  the two profiles are of different devices: /device:TPU:1 before, /device:TPU:21 now
where the time goes in v13:
time: 73 us; the launch traced here: 72.6 us
  starting transfers between devices  42.7 us (58%)
  waiting for transfers between devices  13.5 us (18%)
  other arithmetic  11.8 us (16%)
  local copies, waits for them, and re-layouts  3.92 us (5%)
    ppermute x6, starting transfers between devices, shift_space(): return lax.ppermute(block, 'space', pairs)  24.1 us
    ppermute x1, starting transfers between devices, steps(): arrived1 = lax.ppermute(ends0, 'tm', tm_pairs)  10.3 us
    ppermute x1, starting transfers between devices, steps(): arrived2 = lax.ppermute(ends1, 'tm', tm_pairs)  8.3 us
    ppermute x6, waiting for transfers between devices, shift_space(): return lax.ppermute(block, 'space', pairs)  7.02 us
    ppermute x1, waiting for transfers between devices, steps(): arrived1 = lax.ppermute(ends0, 'tm', tm_pairs)  6.49 us
    another operation x13, other arithmetic, rates(): return jnp.stack([dvolt, dact, dinact, dslow], axis=-4)  4.9 us
    div x3, other arithmetic, rates(): dact = (jax.nn.sigmoid(8.0 * (volt - 0.2)) - act) / 0.5  2.22 us
  transfers between devices with their start and end apart: 8, of which 2 were waited for; matrix products, arithmetic and copies ran while one was open for 15% of the time, Pallas kernels for 0%

profile of v13, /device:TPU:21, one launch (start us, length us, event | category | flops | bytes accessed | tf_op | source)
XLA Modules:
  0.0 72.6 jit_solution(1761998543055517214)
XLA Ops:
  0.0 0.8 %slice_bitcast_fusion.45 = (f32[1,64,128]{2,1,0:T(8,128)S(1)}, f32[1,64,128]{2,1,0:T(8,128)S(1)}) fusion(f32[1,4,4,64,128]{4,3,2,1,0:T(8,128)} %param.4), kind=kLoop, calls=%fused_computation.399 | loop fusion | bytes 131072 | tf_op jit(solution)/shard_map/slice | solution.py:63
  0.8 3.5 %collective-permute-start = (f32[1,64,128]{2,1,0:T(8,128)S(1)}, f32[1,64,128]{2,1,0:T(8,128)S(1)}, u32[]{:S(2)}, u32[]{:S(2)}) collective-permute-start(f32[1,64,128]{2,1,0:T(8,128)S(1)} %get-tuple-element.87), channel_id=1, source_target_pairs={{0,1},{1,2},{2,3},{3,4},{4,5},{5,6},{6,7},{7,8},{8,9},{9,10},{10,1... | collective-permute-start | bytes 98312 | tf_op jit(solution)/shard_map/ppermute | solution.py:58
  4.4 4.6 %collective-permute-start.1 = (f32[1,64,128]{2,1,0:T(8,128)S(1)}, f32[1,64,128]{2,1,0:T(8,128)S(1)}, u32[]{:S(2)}, u32[]{:S(2)}) collective-permute-start(f32[1,64,128]{2,1,0:T(8,128)S(1)} %get-tuple-element.88), channel_id=1, source_target_pairs={{1,0},{2,1},{3,2},{4,3},{5,4},{6,5},{7,6},{8,7},{9,8},{10,9},{11,1... | collective-permute-start | bytes 98312 | tf_op jit(solution)/shard_map/ppermute | solution.py:58
  9.0 1.2 %fusion.162 = (f32[1,4,64,128]{3,2,1,0:T(8,128)S(1)}, f32[1,4,64,128]{3,2,1,0:T(8,128)S(1)}) fusion(f32[1,4,4,64,128]{4,3,2,1,0:T(8,128)} %param.4), kind=kLoop, calls=%fused_computation.289 | loop fusion | flops 655360 | bytes 655360 | tf_op jit(solution)/shard_map/div | solution.py:87
  10.2 0.9 %slice_bitcast_fusion.18 = (f32[1,4,64,128]{3,2,1,0:T(8,128)S(1)}, f32[4,64,128]{2,1,0:T(8,128)S(1)}) fusion(f32[1,4,4,64,128]{4,3,2,1,0:T(8,128)} %param.4), kind=kLoop, calls=%fused_computation.302 | loop fusion | bytes 393216 | tf_op jit(solution)/shard_map/slice | solution.py:130
  11.1 0.1 fusion.207
  11.2 0.1 fusion.210
  11.3 1.5 %fusion.133 = (f32[1,4,64,128]{3,2,1,0:T(8,128)S(1)}, pred[4,64,128]{2,1,0:T(8,128)(4,1)S(1)}, pred[4,64,128]{2,1,0:T(8,128)(4,1)S(1)}, pred[4,64,128]{2,1,0:T(8...) fusion(f32[4,64,128]{2,1,0:T(8,128)S(1)} %get-tuple-element.86,, ...), kind=kLoop, calls=%fused_computation.239 | loop fusion | flops 1933312 | bytes 1513472 | tf_op jit(solution)/shard_map/stack | solution.py:92
  12.8 0.2 fusion.165
  13.0 0.1 bitcast_divide_fusion.7
  13.3 0.0 collective-permute-done.1
  13.3 0.1 fusion.179
  13.4 0.0 collective-permute-done
  13.5 0.1 fusion.173
  13.6 0.1 fusion.64
  13.7 0.1 add_dynamic-update-slice_fusion.3
  13.8 0.1 add_dynamic-update-slice_fusion.2
  13.8 0.1 add_dynamic-update-slice_fusion.1
  13.9 0.1 add_dynamic-update-slice_fusion
  14.0 0.1 fusion.67
  14.1 0.1 slice_bitcast_fusion
  14.2 0.2 fusion.205
  14.4 0.8 %fusion.43 = (f32[5,1,4,64,128]{4,3,2,0,1:T(8,128)S(1)}, f32[5,1,4,64,128]{4,3,2,0,1:T(8,128)S(1)}, f32[5,1,4,64,128]{4,3,2,0,1:T(8,128)S(1)}) fusion(f32[5,4,4,64,128]{4,3,2,1,0:T(8,128)S(1)} %fusion.67, f32[4,64,128]{2,1,0:T(8,128)S(1)} %get-tuple-element.104), kind=kLoop, calls=%fused_computation.85 | loop fusion | flops 4423680 | bytes 4718592 | tf_op jit(solution)/shard_map/div | solution.py:87
  15.2 1.9 %collective-permute-start.4 = (f32[1,64,128]{2,1,0:T(8,128)S(1)}, f32[1,64,128]{2,1,0:T(8,128)S(1)}, u32[]{:S(2)}, u32[]{:S(2)}) collective-permute-start(f32[1,64,128]{2,1,0:T(8,128)S(1)} %slice_bitcast_fusion.31), channel_id=1, source_target_pairs={{0,1},{1,2},{2,3},{3,4},{4,5},{5,6},{6,7},{7,8},{8,9},{9,10},{10,1... | collective-permute-start | bytes 98312 | tf_op jit(solution)/shard_map/ppermute | solution.py:58
  17.1 6.1 %collective-permute-start.3 = (f32[1,64,128]{2,1,0:T(8,128)S(1)}, f32[1,64,128]{2,1,0:T(8,128)S(1)}, u32[]{:S(2)}, u32[]{:S(2)}) collective-permute-start(f32[1,64,128]{2,1,0:T(8,128)S(1)} %slice_bitcast_fusion.32), channel_id=1, source_target_pairs={{1,0},{2,1},{3,2},{4,3},{5,4},{6,5},{7,6},{8,7},{9,8},{10,9},{11,1... | collective-permute-start | bytes 98312 | tf_op jit(solution)/shard_map/ppermute | solution.py:58
  23.2 10.3 %collective-permute-start.2 = (f32[4,4,64,128]{3,2,1,0:T(8,128)S(1)}, f32[4,4,64,128]{3,2,1,0:T(8,128)S(1)}, u32[]{:S(2)}, u32[]{:S(2)}) collective-permute-start(f32[4,4,64,128]{3,2,1,0:T(8,128)S(1)} %fusion.64), channel_id=1, source_target_pairs={{0,16},{16,32},{32,48},{48,64},{64,80},{80,96},{96,112},{112,128},... | collective-permute-start | bytes 1572872 | tf_op jit(solution)/shard_map/ppermute | solution.py:147
  33.8 0.9 %fusion.5 = f32[5,1,4,64,128]{4,3,2,0,1:T(8,128)S(1)} fusion(f32[5,4,64,128]{3,2,1,0:T(8,128)S(1)} %slice_bitcast_fusion, f32[5,4,64,1]{3,2,1,0:T(8,128)S(1)} %get-tuple-element.72, f32[5,4,64,1]{3,2,1,0:T(8,128)S(1)} %get-tuple-element.71, f32[5,4,1,128]{3,2,1,0:T(1,128)S(1)} %get-tuple-element.70, f32[5,4,1,128]{3,2,1,0:T(1,128)S(1)} %get-tuple-element.69, ...), kind=kLoop, calls=%fused_computation.25 | loop fusion | flops 5242880 | bytes 4290560 | tf_op jit(solution)/shard_map/stack | solution.py:92
  34.6 0.2 pad_maximum_fusion
  34.8 0.3 fusion.60
  35.1 6.5 %collective-permute-done.2 = f32[4,4,64,128]{3,2,1,0:T(8,128)S(1)} collective-permute-done((f32[4,4,64,128]{3,2,1,0:T(8,128)S(1)}, f32[4,4,64,128]{3,2,1,0:T(8,128)S(1)}, u32[]{:S(2)}, u32[]{:S(2)}) %collective-permute-start.2) | collective-permute-done | bytes 524320 | tf_op jit(solution)/shard_map/ppermute | solution.py:147
  41.6 0.1 fusion.198
  41.8 0.0 copy-start.2
  41.8 0.0 copy-start.3
  41.8 0.0 copy-start.4
  41.8 0.0 copy-start.5
  41.8 0.0 copy-start.6
  41.9 0.2 slice_bitcast_fusion.9
  42.0 8.3 %collective-permute-start.5 = (f32[4,4,64,128]{3,2,1,0:T(8,128)S(1)}, f32[4,4,64,128]{3,2,1,0:T(8,128)S(1)}, u32[]{:S(2)}, u32[]{:S(2)}) collective-permute-start(f32[4,4,64,128]{3,2,1,0:T(8,128)S(1)} %get-tuple-element.15), channel_id=1, source_target_pairs={{0,16},{16,32},{32,48},{48,64},{64,80},{80,96},{96,112},{112,128},... | collective-permute-start | bytes 1572872 | tf_op jit(solution)/shard_map/ppermute | solution.py:161
  50.4 1.0 %multiply_add_fusion = f32[5,4,4,64,128]{4,3,2,0,1:T(8,128)S(1)} fusion(f32[4,4,64,128]{3,2,1,0:T(8,128)S(1)} %get-tuple-element.46, f32[5]{0:T(128)S(1)} %copy-done.2, f32[4,4,64,128]{3,2,1,0:T(8,128)S(1)} %get-tuple-element.47, f32[5]{0:T(128)S(1)} %copy-done.3, f32[4,4,64,128]{3,2,1,0:T(8,128)S(1)} %get-tuple-element.48, f32[5]{0:T(128)S(1)} %copy-done.4, ...), kind=kLoop, calls=%fused_computation.2 | loop fusion | flops 7208960 | bytes 5767268 | tf_op jit(solution)/shard_map/add | solution.py:106
  51.4 0.1 fusion.127
  51.6 0.8 %slice_bitcast_fusion.50 = (f32[5,4,64,128]{3,2,1,0:T(8,128)S(1)}, f32[5,1,4,64,128]{4,3,2,0,1:T(8,128)S(1)}, f32[5,1,4,64,128]{4,3,2,0,1:T(8,128)S(1)}, f32[5,1...) fusion(f32[5,4,4,64,128]{4,3,2,0,1:T(8,128)S(1)} %multiply_add_fusion, f32[4,64,128]{2,1,0:T(8,128)S(1)} %get-tuple-element.104), kind=kLoop, calls=%fused_computation.406 | loop fusion | flops 4423680 | bytes 6029312 | tf_op jit(solution)/shard_map/squeeze | solution.py:170
  52.4 0.1 copy.119
  52.4 0.2 fusion.200
  52.6 0.1 fusion.201
  52.7 0.2 fusion.203
  52.9 0.1 fusion.117
  53.0 0.2 multiply_add_fusion.2
  53.2 2.6 %collective-permute-start.6 = (f32[5,1,64,128]{3,2,0,1:T(8,128)S(1)}, f32[5,1,64,128]{3,2,0,1:T(8,128)S(1)}, u32[]{:S(2)}, u32[]{:S(2)}) collective-permute-start(f32[5,1,64,128]{3,2,0,1:T(8,128)S(1)} %get-tuple-element.124), channel_id=1, source_target_pairs={{0,1},{1,2},{2,3},{3,4},{4,5},{5,6},{6,7},{7,8},{8,9},{9,10},{10,1... | collective-permute-start | bytes 491528 | tf_op jit(solution)/shard_map/ppermute | solution.py:58
  55.9 5.4 %collective-permute-start.7 = (f32[5,1,64,128]{3,2,0,1:T(8,128)S(1)}, f32[5,1,64,128]{3,2,0,1:T(8,128)S(1)}, u32[]{:S(2)}, u32[]{:S(2)}) collective-permute-start(f32[5,1,64,128]{3,2,0,1:T(8,128)S(1)} %get-tuple-element.125), channel_id=1, source_target_pairs={{1,0},{2,1},{3,2},{4,3},{5,4},{6,5},{7,6},{8,7},{9,8},{10,9},{11,1... | collective-permute-start | bytes 491528 | tf_op jit(solution)/shard_map/ppermute | solution.py:58
  61.2 0.3 fusion.81
  61.5 1.0 %fusion.45 = f32[5,1,4,64,128]{4,3,0,2,1:T(8,128)S(1)} fusion(f32[5,1,4,64,128]{4,3,2,0,1:T(8,128)S(1)} %get-tuple-element.44, f32[5,4,4,64,128]{4,3,2,0,1:T(8,128)S(1)} %multiply_add_fusion, f32[4,64,128]{2,1,0:T(8,128)S(1)} %get-tuple-element.105, f32[4,64,128]{2,1,0:T(8,128)S(1)} %get-tuple-element.106, f32[5,4,64,128]{3,2,1,0:T(8,128)S(1)} %get-tuple-element.40, ...), kind=kLoop, calls=%fused_computation.89 | loop fusion | flops 5242880 | bytes 5601280 | tf_op jit(solution)/shard_map/stack | solution.py:92
  62.5 0.3 pad_maximum_fusion.1
  62.8 0.3 fusion.48
  63.1 0.0 copy-start.1
  63.1 7.0 %collective-permute-done.7 = f32[5,1,64,128]{3,2,0,1:T(8,128)S(1)} collective-permute-done((f32[5,1,64,128]{3,2,0,1:T(8,128)S(1)}, f32[5,1,64,128]{3,2,0,1:T(8,128)S(1)}, u32[]{:S(2)}, u32[]{:S(2)}) %collective-permute-start.7) | collective-permute-done | bytes 163872 | tf_op jit(solution)/shard_map/ppermute | solution.py:58
  70.1 0.3 fusion.79
  70.4 0.1 pad_maximum_fusion.15
  70.5 0.3 fusion.73
  70.7 0.0 slice-start
  70.8 0.1 pad_maximum_fusion.14
  70.8 0.1 fusion.136
  70.9 0.1 fusion.143
  70.9 0.7 %slice-done = f32[4,2,64,128]{3,2,1,0:T(8,128)S(1)} async-done(((f32[4,4,64,128]{3,2,1,0:T(8,128)}), f32[4,2,64,128]{3,2,1,0:T(8,128)S(1)}, s32[]{:S(2)}) %slice-start) | async-done | bytes 262168 | tf_op jit(solution)/shard_map/slice | solution.py:184
  71.7 0.9 %fusion.65 = f32[1,4,4,64,128]{4,3,2,1,0:T(8,128)} fusion(f32[4,1,64,128]{3,2,1,0:T(8,128)S(1)} %fusion.136, f32[4,2,64,128]{3,2,1,0:T(8,128)S(1)} %slice-done, f32[4,1,64,128]{3,2,1,0:T(8,128)S(1)} %fusion.143, f32[4,4,64,128]{3,2,1,0:T(8,128)S(1)} %collective-permute-done.5, f32[1,4,4,64,128]{4,3,2,1,0:T(8,128)S(1)} %copy-done, pred[]{:T(512)S(6)} %eq.38), kind=kLoop, calls=%fused_computation.129 | loop fusion | flops 524288 | bytes 2097153 | tf_op jit(solution)/shard_map/broadcast_in_dim | solution.py:187
  (42 shorter events, 0.4 us)
Async XLA Ops:
  0.0 12.8 %copy-start = (f32[1,4,4,64,128]{4,3,2,1,0:T(8,128)S(1)}, f32[1,4,4,64,128]{4,3,2,1,0:T(8,128)}, u32[]{:S(2)}) copy-start(f32[1,4,4,64,128]{4,3,2,1,0:T(8,128)} %param.4) | copy-start | bytes 1572868
  0.8 12.6 %collective-permute-start = (f32[1,64,128]{2,1,0:T(8,128)S(1)}, f32[1,64,128]{2,1,0:T(8,128)S(1)}, u32[]{:S(2)}, u32[]{:S(2)}) collective-permute-start(f32[1,64,128]{2,1,0:T(8,128)S(1)} %get-tuple-element.87), channel_id=1, source_target_pairs={{0,1},{1,2},{2,3},{3,4},{4,5},{5,6},{6,7},{7,8},{8,9},{9,10},{10,1... | collective-permute-start | bytes 98312 | tf_op jit(solution)/shard_map/ppermute | solution.py:58
  4.4 8.9 %collective-permute-start.1 = (f32[1,64,128]{2,1,0:T(8,128)S(1)}, f32[1,64,128]{2,1,0:T(8,128)S(1)}, u32[]{:S(2)}, u32[]{:S(2)}) collective-permute-start(f32[1,64,128]{2,1,0:T(8,128)S(1)} %get-tuple-element.88), channel_id=1, source_target_pairs={{1,0},{2,1},{3,2},{4,3},{5,4},{6,5},{7,6},{8,7},{9,8},{10,9},{11,1... | collective-permute-start | bytes 98312 | tf_op jit(solution)/shard_map/ppermute | solution.py:58
  15.2 18.4 %collective-permute-start.4 = (f32[1,64,128]{2,1,0:T(8,128)S(1)}, f32[1,64,128]{2,1,0:T(8,128)S(1)}, u32[]{:S(2)}, u32[]{:S(2)}) collective-permute-start(f32[1,64,128]{2,1,0:T(8,128)S(1)} %slice_bitcast_fusion.31), channel_id=1, source_target_pairs={{0,1},{1,2},{2,3},{3,4},{4,5},{5,6},{6,7},{7,8},{8,9},{9,10},{10,1... | collective-permute-start | bytes 98312 | tf_op jit(solution)/shard_map/ppermute | solution.py:58
  17.1 16.5 %collective-permute-start.3 = (f32[1,64,128]{2,1,0:T(8,128)S(1)}, f32[1,64,128]{2,1,0:T(8,128)S(1)}, u32[]{:S(2)}, u32[]{:S(2)}) collective-permute-start(f32[1,64,128]{2,1,0:T(8,128)S(1)} %slice_bitcast_fusion.32), channel_id=1, source_target_pairs={{1,0},{2,1},{3,2},{4,3},{5,4},{6,5},{7,6},{8,7},{9,8},{10,9},{11,1... | collective-permute-start | bytes 98312 | tf_op jit(solution)/shard_map/ppermute | solution.py:58
  23.2 18.4 %collective-permute-start.2 = (f32[4,4,64,128]{3,2,1,0:T(8,128)S(1)}, f32[4,4,64,128]{3,2,1,0:T(8,128)S(1)}, u32[]{:S(2)}, u32[]{:S(2)}) collective-permute-start(f32[4,4,64,128]{3,2,1,0:T(8,128)S(1)} %fusion.64), channel_id=1, source_target_pairs={{0,16},{16,32},{32,48},{48,64},{64,80},{80,96},{96,112},{112,128},... | collective-permute-start | bytes 1572872 | tf_op jit(solution)/shard_map/ppermute | solution.py:147
  41.8 8.6 %copy-start.2 = (f32[5]{0:T(128)S(1)}, f32[5]{0:T(128)}, u32[]{:S(2)}) copy-start(f32[5]{0:T(128)} %constant.195) | copy-start | bytes 64
  41.8 8.6 %copy-start.3 = (f32[5]{0:T(128)S(1)}, f32[5]{0:T(128)}, u32[]{:S(2)}) copy-start(f32[5]{0:T(128)} %constant.193) | copy-start | bytes 64
  41.8 8.6 %copy-start.4 = (f32[5]{0:T(128)S(1)}, f32[5]{0:T(128)}, u32[]{:S(2)}) copy-start(f32[5]{0:T(128)} %constant.191) | copy-start | bytes 64
  41.8 8.6 %copy-start.5 = (f32[5]{0:T(128)S(1)}, f32[5]{0:T(128)}, u32[]{:S(2)}) copy-start(f32[5]{0:T(128)} %constant.189) | copy-start | bytes 64
  41.8 8.6 %copy-start.6 = (f32[5]{0:T(128)S(1)}, f32[5]{0:T(128)}, u32[]{:S(2)}) copy-start(f32[5]{0:T(128)} %constant.187) | copy-start | bytes 64
  42.0 28.9 %collective-permute-start.5 = (f32[4,4,64,128]{3,2,1,0:T(8,128)S(1)}, f32[4,4,64,128]{3,2,1,0:T(8,128)S(1)}, u32[]{:S(2)}, u32[]{:S(2)}) collective-permute-start(f32[4,4,64,128]{3,2,1,0:T(8,128)S(1)} %get-tuple-element.15), channel_id=1, source_target_pairs={{0,16},{16,32},{32,48},{48,64},{64,80},{80,96},{96,112},{112,128},... | collective-permute-start | bytes 1572872 | tf_op jit(solution)/shard_map/ppermute | solution.py:161
  53.2 17.2 %collective-permute-start.6 = (f32[5,1,64,128]{3,2,0,1:T(8,128)S(1)}, f32[5,1,64,128]{3,2,0,1:T(8,128)S(1)}, u32[]{:S(2)}, u32[]{:S(2)}) collective-permute-start(f32[5,1,64,128]{3,2,0,1:T(8,128)S(1)} %get-tuple-element.124), channel_id=1, source_target_pairs={{0,1},{1,2},{2,3},{3,4},{4,5},{5,6},{6,7},{7,8},{8,9},{9,10},{10,1... | collective-permute-start | bytes 491528 | tf_op jit(solution)/shard_map/ppermute | solution.py:58
  55.9 14.3 %collective-permute-start.7 = (f32[5,1,64,128]{3,2,0,1:T(8,128)S(1)}, f32[5,1,64,128]{3,2,0,1:T(8,128)S(1)}, u32[]{:S(2)}, u32[]{:S(2)}) collective-permute-start(f32[5,1,64,128]{3,2,0,1:T(8,128)S(1)} %get-tuple-element.125), channel_id=1, source_target_pairs={{1,0},{2,1},{3,2},{4,3},{5,4},{6,5},{7,6},{8,7},{9,8},{10,9},{11,1... | collective-permute-start | bytes 491528 | tf_op jit(solution)/shard_map/ppermute | solution.py:58
  63.1 7.6 %copy-start.1 = (f32[4,4,64,128]{3,2,1,0:T(8,128)}, f32[4,4,64,128]{3,2,1,0:T(8,128)S(1)}, u32[]{:S(2)}) copy-start(f32[4,4,64,128]{3,2,1,0:T(8,128)S(1)} %fusion.48) | copy-start | bytes 1572868
  70.7 1.0 %slice-start = ((f32[4,4,64,128]{3,2,1,0:T(8,128)}), f32[4,2,64,128]{3,2,1,0:T(8,128)S(1)}, s32[]{:S(2)}) async-start(f32[4,4,64,128]{3,2,1,0:T(8,128)} %copy-done.1), calls=%async_computation | async-start | bytes 524288 | tf_op jit(solution)/shard_map/slice | solution.py:184
